TPU v7x, 256 devices: a whole 4x4x8 slice. The times are simulated.
256 devices in a mesh: seq: 32 (over x_hi, z, core), tensor: 8 (over y, x_lo).
Axes of the slice: x: 4 (x_hi: 2, x_lo: 2; x = x_hi * 2 + x_lo), y: 4, z: 8, core: 2. Of those that a mesh axis runs over, the one named last changes fastest.
Arguments:
- tokens: bfloat16 [4, 1024, 4096], P(None, 'seq', 'tensor'), may hold values from -600 to 600
- norm_gain: bfloat16 [4096], replicated, may hold values from 0.099609375 to 1.8984375
- w_query: bfloat16 [4096, 2048], P(None, 'tensor'), may hold values from -0.1875 to 0.1875
- w_key: bfloat16 [4096, 2048], P(None, 'tensor'), may hold values from -0.09375 to 0.09375
- w_value: bfloat16 [4096, 2048], P(None, 'tensor'), may hold values from -0.09375 to 0.09375
- w_out: bfloat16 [2048, 4096], P('tensor'), may hold values from -1 to 1
- cache_keys: bfloat16 [4, 8192, 2048], P(None, 'seq', 'tensor'), may hold values from -103 to 103
- cache_values: bfloat16 [4, 8192, 2048], P(None, 'seq', 'tensor'), may hold values from -6 to 6
- cache_len: int32 [4], replicated, may hold values from 1 to 8192, as said below
- group_len: int32 [4], replicated, may hold values from 1 to 1024, 3584 in all
Outputs:
- mixed: bfloat16 [4, 1024, 4096], P(None, 'seq', 'tensor')
- new_keys: bfloat16 [4, 1024, 2048], P(None, 'seq', 'tensor')
- new_values: bfloat16 [4, 1024, 2048], P(None, 'seq', 'tensor')
Inputs may be any that keep to these rules, and one draw needn't show every extreme that they name: `cache_len`: one request's cache holds all 8192 positions. `group_len`: the new-token counts sum to 3584.
All inputs are finite; a program needn't handle non-finite values.
Results may differ from a plain program's by a relative error of at most 0.0075.
The roundings to bfloat16 on the way count: a program that leaves them out, or rounds other values in their place, can miss the bound.
Values may be sent and summed in bfloat16 or wider, within the bound.
No kernel may reach another device: no remote copies, remote signals or barrier semaphores. Data moves between devices by JAX's collectives and lax.ppermute only.
A program may use at most 128 MiB of HBM per device.

v0:
```python
import jax
import jax.numpy as jnp
from jax import lax
from jax.sharding import PartitionSpec as P

HD = 128


def rotate(vector, position):
    half_dim = vector.shape[-1] // 2
    frequency = 1000000.0 ** (-(jnp.arange(half_dim, dtype=jnp.float32) * 2.0 / vector.shape[-1]))
    angles = position.astype(jnp.float32)[..., None] * frequency
    cosine = jnp.concatenate([jnp.cos(angles), jnp.cos(angles)], -1)[..., None, :]
    sine = jnp.concatenate([jnp.sin(angles), jnp.sin(angles)], -1)[..., None, :]
    turned = jnp.concatenate([-vector[..., half_dim:], vector[..., :half_dim]], -1)
    return vector * cosine + turned * sine


def body(
    tokens,
    norm_gain,
    w_query,
    w_key,
    w_value,
    w_out,
    cache_keys,
    cache_values,
    cache_len,
    group_len,
):
    seq_index = lax.axis_index("seq")
    requests, local_rows, width_part = tokens.shape
    gathered = lax.all_gather(tokens, "tensor", axis=2, tiled=True).astype(jnp.float32)
    inverse_rms = lax.rsqrt(jnp.mean(gathered * gathered, -1, keepdims=True) + 1e-05)
    normed = (gathered * inverse_rms * norm_gain.astype(jnp.float32)).astype(jnp.bfloat16)
    flat_rows = normed.reshape(requests * local_rows, -1)
    heads_width = w_query.shape[1]
    local_heads = heads_width // HD

    def project(weight):
        return jnp.dot(flat_rows, weight, preferred_element_type=jnp.float32).reshape(
            requests, local_rows, local_heads, HD
        )

    offsets = jnp.arange(local_rows, dtype=jnp.int32)
    first_row = seq_index * local_rows
    position = cache_len[:, None] + first_row + offsets[None, :]
    queries = (
        rotate(project(w_query), position)
        .astype(jnp.bfloat16)
        .reshape(requests, local_rows, heads_width)
    )
    key_new = (
        rotate(project(w_key), position)
        .astype(jnp.bfloat16)
        .reshape(requests, local_rows, heads_width)
    )
    value_new = project(w_value).astype(jnp.bfloat16).reshape(requests, local_rows, heads_width)
    live_rows = (first_row + offsets)[None, :] < group_len[:, None]
    new_keys = jnp.where(live_rows[..., None], key_new, jnp.zeros_like(key_new))
    new_values = jnp.where(live_rows[..., None], value_new, jnp.zeros_like(value_new))
    all_queries = lax.all_gather(queries, "seq", axis=1, tiled=True)
    group_total = all_queries.shape[1]
    seq_count = group_total // local_rows
    cache_slots = cache_keys.shape[1]
    slot_index = seq_index * cache_slots + jnp.arange(cache_slots, dtype=jnp.int32)
    query_index = jnp.arange(group_total, dtype=jnp.int32)
    token_index = first_row + offsets
    score_scale = HD ** (-0.5)
    numer_width = local_rows * heads_width
    attended_list = []
    for request in range(requests):
        query_rows = all_queries[request].reshape(group_total, local_heads, HD)
        cache_k = cache_keys[request].reshape(cache_slots, local_heads, HD)
        cache_v = cache_values[request].reshape(cache_slots, local_heads, HD)
        group_k = key_new[request].reshape(local_rows, local_heads, HD)
        group_v = value_new[request].reshape(local_rows, local_heads, HD)
        cache_ok = (slot_index < cache_len[request])[None, None, :]
        group_ok = (
            (token_index[None, :] <= query_index[:, None])
            & (token_index < group_len[request])[None, :]
        )[None]
        cache_scores = jnp.where(
            cache_ok,
            jnp.einsum("qhd,khd->hqk", query_rows, cache_k, preferred_element_type=jnp.float32)
            * score_scale,
            -1e30,
        )
        group_scores = jnp.where(
            group_ok,
            jnp.einsum("qhd,khd->hqk", query_rows, group_k, preferred_element_type=jnp.float32)
            * score_scale,
            -1e30,
        )
        row_peak = jnp.maximum(jnp.max(cache_scores, -1), jnp.max(group_scores, -1))
        cache_weights = jnp.where(cache_ok, jnp.exp(cache_scores - row_peak[..., None]), 0.0)
        group_weights = jnp.where(group_ok, jnp.exp(group_scores - row_peak[..., None]), 0.0)
        row_mass = jnp.sum(cache_weights, -1) + jnp.sum(group_weights, -1)
        numerators = jnp.einsum(
            "hqk,khd->qhd",
            cache_weights.astype(jnp.bfloat16),
            cache_v,
            preferred_element_type=jnp.float32,
        ) + jnp.einsum(
            "hqk,khd->qhd",
            group_weights.astype(jnp.bfloat16),
            group_v,
            preferred_element_type=jnp.float32,
        )
        stats = jnp.stack([row_peak.T, row_mass.T], -1)
        pair_rows = local_rows * local_heads
        payload = jnp.concatenate(
            [
                numerators.reshape(seq_count, pair_rows, HD),
                stats.reshape(seq_count, -1, HD),
            ],
            1,
        )
        received = lax.all_to_all(payload, "seq", 0, 0, tiled=True)
        block_stats = received[:, pair_rows:].reshape(seq_count, pair_rows, 2)
        block_peak = block_stats[..., 0]
        factor = jnp.exp(block_peak - jnp.max(block_peak, 0))
        mass_sum = jnp.sum(block_stats[..., 1] * factor, 0).reshape(local_rows, local_heads)
        numer_sum = jnp.sum(received[:, :pair_rows] * factor[..., None], 0)
        numer_sum = numer_sum.reshape(local_rows, local_heads, HD)
        attended_list.append(numer_sum / mass_sum[..., None])
    attended = (
        jnp.where(live_rows[..., None, None], jnp.stack(attended_list), 0.0)
        .astype(jnp.bfloat16)
        .reshape(requests * local_rows, heads_width)
    )
    partial_out = jnp.dot(attended, w_out, preferred_element_type=jnp.float32).reshape(
        requests, local_rows, -1
    )
    mixed = lax.psum_scatter(partial_out, "tensor", scatter_dimension=2, tiled=True).astype(
        jnp.bfloat16
    )
    return (mixed, new_keys, new_values)


def solution(mesh):
    placed = (
        P(None, "seq", "tensor"),
        P(),
        P(None, "tensor"),
        P(None, "tensor"),
        P(None, "tensor"),
        P("tensor", None),
        P(None, "seq", "tensor"),
        P(None, "seq", "tensor"),
        P(),
        P(),
    )
    return jax.shard_map(
        body,
        mesh=mesh,
        in_specs=placed,
        out_specs=(P(None, "seq", "tensor"), P(None, "seq", "tensor"), P(None, "seq", "tensor")),
        check_vma=False,
    )
```

profile of v0, /device:TPU:32, one launch (start us, length us, event | category | flops | bytes accessed | tf_op | source)
XLA Modules:
  0.0 372.8 jit_solution(4754881490199022731)
XLA Ops:
  8.0 4.1 %copy.198 = bf16[256,4096]{1,0:T(8,128)(2,1)} copy(bf16[256,4096]{0,1:T(8,128)(2,1)} %bitcast.196) | data formatting | bytes 4194304 | tf_op jit(solution)/shard_map/dot_general | solution.py:41
  12.1 4.1 %copy.197 = bf16[256,4096]{1,0:T(8,128)(2,1)} copy(bf16[256,4096]{0,1:T(8,128)(2,1)} %bitcast.197) | data formatting | bytes 4194304 | tf_op jit(solution)/shard_map/dot_general | solution.py:41
  17.4 38.2 %all-gather.3.cloned.1.call-done = bf16[4,32,4096]{2,1,0:T(8,128)(2,1)} async-done(((bf16[4,32,512]{2,1,0:T(8,128)(2,1)}), bf16[4,32,4096]{2,1,0:T(8,128)(2,1)}) %all-gather.3.cloned.1.call-update) | async-done | bytes 1048592 | tf_op jit(solution)/shard_map/all_gather | solution.py:33
  55.6 1.5 fusion
  57.1 2.9 fusion.92
  62.0 1.8 fusion.120
  63.9 1.9 fusion.119
  66.5 4.1 %copy.199 = bf16[256,4096]{1,0:T(8,128)(2,1)} copy(bf16[256,4096]{0,1:T(8,128)(2,1)} %bitcast.198) | data formatting | bytes 4194304 | tf_op jit(solution)/shard_map/dot_general | solution.py:41
  71.3 1.2 broadcast_compare_fusion.3
  72.6 1.2 broadcast_compare_fusion.1
  74.5 1.9 fusion.96
  77.1 3.1 convolution_convert_fusion
  80.2 60.0 %all-gather.5.cloned.1.call-done = bf16[4,1024,256]{2,1,0:T(8,128)(2,1)} async-done(((bf16[4,32,256]{2,1,0:T(8,128)(2,1)}), bf16[4,1024,256]{2,1,0:T(8,128)(2,1)}) %all-gather.5.cloned.1.call-update) | async-done | bytes 2097168 | tf_op jit(solution)/shard_map/all_gather | solution.py:62
  140.2 2.7 fusion.118
  143.7 1.1 fusion.127
  145.0 1.3 fusion.15
  147.0 1.2 copy.164
  148.3 1.9 reshape.500
  150.1 2.4 convolution_bitcast_fusion.1
  152.6 1.1 fusion.17
  154.6 1.1 pad_maximum_fusion.3
  155.7 5.7 %all-to-all-start.3 = ((f32[32,65,128]{2,1,0:T(8,128)}), f32[32,65,128]{2,1,0:T(8,128)}, u32[]{:S(2)}, u32[]{:S(2)}) async-start(f32[32,65,128]{2,1,0:T(8,128)} %pad_maximum_fusion.3), calls=%async_computation.3 | async-start | bytes 2359296 | tf_op jit(solution)/shard_map/all_to_all | solution.py:119
  164.7 1.0 fusion.128
  165.8 1.4 fusion.7
  167.3 1.2 copy-done.2
  169.8 1.2 copy.148
  171.1 1.9 reshape.496
  172.9 2.4 convolution_bitcast_fusion.3
  175.4 1.1 fusion.18
  177.3 1.1 pad_maximum_fusion.2
  178.5 16.3 %all-to-all-done.3 = f32[32,65,128]{2,1,0:T(8,128)} async-done(((f32[32,65,128]{2,1,0:T(8,128)}), f32[32,65,128]{2,1,0:T(8,128)}, u32[]{:S(2)}, u32[]{:S(2)}) %all-to-all-start.3) | async-done | bytes 1064992 | tf_op jit(solution)/shard_map/all_to_all | solution.py:119
  194.8 4.5 %all-to-all-start.2 = ((f32[32,65,128]{2,1,0:T(8,128)}), f32[32,65,128]{2,1,0:T(8,128)}, u32[]{:S(2)}, u32[]{:S(2)}) async-start(f32[32,65,128]{2,1,0:T(8,128)} %pad_maximum_fusion.2), calls=%async_computation.2 | async-start | bytes 2359296 | tf_op jit(solution)/shard_map/all_to_all | solution.py:119
  199.2 1.3 fusion.98
  201.0 1.4 fusion.6
  202.5 1.2 copy-done.3
  205.0 1.2 copy.132
  206.2 1.9 reshape.492
  208.1 2.4 convolution_bitcast_fusion.5
  210.6 1.1 fusion.19
  212.5 1.1 pad_maximum_fusion.1
  213.7 18.3 %all-to-all-done.2 = f32[32,65,128]{2,1,0:T(8,128)} async-done(((f32[32,65,128]{2,1,0:T(8,128)}), f32[32,65,128]{2,1,0:T(8,128)}, u32[]{:S(2)}, u32[]{:S(2)}) %all-to-all-start.2) | async-done | bytes 1064992 | tf_op jit(solution)/shard_map/all_to_all | solution.py:119
  232.0 4.7 %all-to-all-start.1 = ((f32[32,65,128]{2,1,0:T(8,128)}), f32[32,65,128]{2,1,0:T(8,128)}, u32[]{:S(2)}, u32[]{:S(2)}) async-start(f32[32,65,128]{2,1,0:T(8,128)} %pad_maximum_fusion.1), calls=%async_computation.1 | async-start | bytes 2359296 | tf_op jit(solution)/shard_map/all_to_all | solution.py:119
  239.3 1.4 fusion.5
  240.9 1.2 copy-done.4
  243.3 1.3 reshape.488
  244.6 2.4 convolution_bitcast_fusion.7
  247.0 1.1 fusion.20
  248.9 1.1 pad_maximum_fusion
  251.1 18.1 %all-to-all-done.1 = f32[32,65,128]{2,1,0:T(8,128)} async-done(((f32[32,65,128]{2,1,0:T(8,128)}), f32[32,65,128]{2,1,0:T(8,128)}, u32[]{:S(2)}, u32[]{:S(2)}) %all-to-all-start.1) | async-done | bytes 1064992 | tf_op jit(solution)/shard_map/all_to_all | solution.py:119
  269.2 3.7 all-to-all-start
  273.7 1.6 fusion.30
  275.8 0.9 slice.222
  276.8 1.1 fusion.123
  278.1 1.6 fusion.31
  279.7 0.9 multiply_reduce_fusion.1
  281.9 1.1 fusion.122
  284.6 1.6 fusion.32
  286.8 1.0 multiply_reduce_fusion.2
  288.6 17.3 %all-to-all-done = f32[32,65,128]{2,1,0:T(8,128)S(1)} async-done(((f32[32,65,128]{2,1,0:T(8,128)}), f32[32,65,128]{2,1,0:T(8,128)S(1)}, u32[]{:S(2)}, u32[]{:S(2)}) %all-to-all-start) | async-done | bytes 1064992 | tf_op jit(solution)/shard_map/all_to_all | solution.py:119
  306.0 1.1 fusion.121
  309.1 1.0 multiply_reduce_fusion.3
  311.2 2.5 fusion.3
  315.3 49.4 %reduce-scatter.2.cloned.1.call-done = f32[4,32,512]{2,1,0:T(8,128)} async-done(((f32[4,32,4096]{2,1,0:T(8,128)}), f32[4,32,512]{2,1,0:T(8,128)}) %reduce-scatter.2.cloned.1.call-update) | async-done | bytes 262160 | tf_op jit(solution)/shard_map/reduce_scatter | solution.py:135
  364.6 1.6 convert_element_type.74
  (173 shorter events, 33.4 us)
Async XLA Ops:
  7.2 304.0 %copy-start = (bf16[256,4096]{1,0:T(8,128)(2,1)S(1)}, bf16[256,4096]{1,0:T(8,128)(2,1)}, u32[]{:S(2)}) copy-start(bf16[256,4096]{1,0:T(8,128)(2,1)} %param.15) | copy-start | bytes 6291460
  7.2 48.4 %all-gather.3.cloned.1.call-start = ((), (), s32[]{:S(2)}) async-start(), calls=%async_computation.5 | async-start | bytes 1179648 | tf_op jit(solution)/shard_map/all_gather | solution.py:33
  7.9 132.3 %all-gather.5.cloned.1.call-start = ((), (), s32[]{:S(2)}) async-start(), calls=%async_computation.6 | async-start | bytes 2162688 | tf_op jit(solution)/shard_map/all_gather | solution.py:62
  8.0 4.1 %copy-start.25 = (bf16[4096]{0:T(1024)(128)(2,1)S(1)}, bf16[4096]{0:T(1024)(128)(2,1)}, u32[]{:S(2)}) copy-start(bf16[4096]{0:T(1024)(128)(2,1)} %param.11) | copy-start | bytes 24580
  12.1 4.1 %copy-start.26 = (s32[4]{0:T(128)S(1)}, s32[4]{0:T(128)}, u32[]{:S(2)}) copy-start(s32[4]{0:T(128)} %param.18) | copy-start | bytes 52
  57.1 2.9 copy-start.5
  57.1 2.9 copy-start.9
  57.1 2.9 copy-start.34
  60.1 1.0 copy-start.21
  66.5 4.2 %copy-start.28 = (s32[4]{0:T(128)S(1)}, s32[4]{0:T(128)}, u32[]{:S(2)}) copy-start(s32[4]{0:T(128)} %param.19) | copy-start | bytes 52
  66.5 7.3 %copy-start.27 = (s32[4]{0:T(128)S(1)}, s32[4]{0:T(128)}, u32[]{:S(2)}) copy-start(s32[4]{0:T(128)} %param.18) | copy-start | bytes 52
  66.5 10.5 %copy-start.35 = (f32[4,32]{1,0:T(4,128)S(1)}, f32[4,32]{1,0:T(4,128)}, u32[]{:S(2)}) copy-start(f32[4,32]{1,0:T(4,128)} %copy-done.34) | copy-start | bytes 1540
  70.7 72.2 %copy-start.36 = (s32[32]{0:T(128)}, s32[32]{0:T(128)S(1)}, u32[]{:S(2)}) copy-start(s32[32]{0:T(128)S(1)} %iota_add_fusion.1) | copy-start | bytes 388
  76.4 66.8 %copy-start.31 = (pred[256]{0:T(512)(128)(4,1)}, pred[256]{0:T(512)(128)(4,1)S(1)}, u32[]{:S(2)}) copy-start(pred[256]{0:T(512)(128)(4,1)S(1)} %get-tuple-element.65) | copy-start | bytes 772
  143.7 1.4 copy-start.1
  143.7 2.6 copy-start.12
  145.0 5.1 %copy-start.32 = (pred[256]{0:T(512)(128)(4,1)S(1)}, pred[256]{0:T(512)(128)(4,1)}, u32[]{:S(2)}) copy-start(pred[256]{0:T(512)(128)(4,1)} %copy-done.31) | copy-start | bytes 772
  150.1 2.4 copy-start.13
  152.6 1.9 copy-start.22
  154.5 6.9 %copy-start.17 = (bf16[1,256,256]{2,1,0:T(8,128)(2,1)S(1)}, bf16[1,256,256]{2,1,0:T(8,128)(2,1)}, u32[]{:S(2)}) copy-start(bf16[1,256,256]{2,1,0:T(8,128)(2,1)} %get-tuple-element.12) | copy-start | bytes 393220
  154.5 7.7 %copy-start.19 = (bf16[1,256,256]{2,1,0:T(8,128)(2,1)S(1)}, bf16[1,256,256]{2,1,0:T(8,128)(2,1)}, u32[]{:S(2)}) copy-start(bf16[1,256,256]{2,1,0:T(8,128)(2,1)} %get-tuple-element.8) | copy-start | bytes 393220
  154.6 8.4 %copy-start.16 = (bf16[1,256,256]{2,1,0:T(8,128)(2,1)S(1)}, bf16[1,256,256]{2,1,0:T(8,128)(2,1)}, u32[]{:S(2)}) copy-start(bf16[1,256,256]{2,1,0:T(8,128)(2,1)} %get-tuple-element.13) | copy-start | bytes 393220
  155.7 8.0 %copy-start.18 = (bf16[1,256,256]{2,1,0:T(8,128)(2,1)S(1)}, bf16[1,256,256]{2,1,0:T(8,128)(2,1)}, u32[]{:S(2)}) copy-start(bf16[1,256,256]{2,1,0:T(8,128)(2,1)} %get-tuple-element.9) | copy-start | bytes 393220
  155.7 8.8 %copy-start.8 = (bf16[1,1024,256]{2,1,0:T(8,128)(2,1)S(1)}, bf16[1,1024,256]{2,1,0:T(8,128)(2,1)}, u32[]{:S(2)}) copy-start(bf16[1,1024,256]{2,1,0:T(8,128)(2,1)} %get-tuple-element.5) | copy-start | bytes 1572868
  155.7 10.1 %copy-start.30 = (pred[256]{0:T(512)(128)(4,1)S(1)}, pred[256]{0:T(512)(128)(4,1)}, u32[]{:S(2)}) copy-start(pred[256]{0:T(512)(128)(4,1)} %get-tuple-element.66) | copy-start | bytes 772
  155.7 39.1 %all-to-all-start.3 = ((f32[32,65,128]{2,1,0:T(8,128)}), f32[32,65,128]{2,1,0:T(8,128)}, u32[]{:S(2)}, u32[]{:S(2)}) async-start(f32[32,65,128]{2,1,0:T(8,128)} %pad_maximum_fusion.3), calls=%async_computation.3 | async-start | bytes 2359296 | tf_op jit(solution)/shard_map/all_to_all | solution.py:119
  164.7 2.5 copy-start.10
  167.2 1.4 copy-start.2
  172.9 2.4 copy-start.11
  175.4 1.9 copy-start.23
  177.3 23.2 %copy-start.7 = (bf16[1,1024,256]{2,1,0:T(8,128)(2,1)S(1)}, bf16[1,1024,256]{2,1,0:T(8,128)(2,1)}, u32[]{:S(2)}) copy-start(bf16[1,1024,256]{2,1,0:T(8,128)(2,1)} %get-tuple-element.6) | copy-start | bytes 1572868
  194.8 37.2 %all-to-all-start.2 = ((f32[32,65,128]{2,1,0:T(8,128)}), f32[32,65,128]{2,1,0:T(8,128)}, u32[]{:S(2)}, u32[]{:S(2)}) async-start(f32[32,65,128]{2,1,0:T(8,128)} %pad_maximum_fusion.2), calls=%async_computation.2 | async-start | bytes 2359296 | tf_op jit(solution)/shard_map/all_to_all | solution.py:119
  202.4 1.4 copy-start.3
  210.6 1.9 copy-start.24
  212.5 24.2 %copy-start.29 = (s32[4]{0:T(128)S(1)}, s32[4]{0:T(128)}, u32[]{:S(2)}) copy-start(s32[4]{0:T(128)} %param.19) | copy-start | bytes 52
  212.5 24.2 %copy-start.37 = (s32[32]{0:T(128)S(1)}, s32[32]{0:T(128)}, u32[]{:S(2)}) copy-start(s32[32]{0:T(128)} %copy-done.36) | copy-start | bytes 388
  212.5 24.8 %copy-start.14 = (bf16[1,256,256]{2,1,0:T(8,128)(2,1)S(1)}, bf16[1,256,256]{2,1,0:T(8,128)(2,1)}, u32[]{:S(2)}) copy-start(bf16[1,256,256]{2,1,0:T(8,128)(2,1)} %get-tuple-element.11) | copy-start | bytes 393220
  212.5 25.6 %copy-start.15 = (bf16[1,256,256]{2,1,0:T(8,128)(2,1)S(1)}, bf16[1,256,256]{2,1,0:T(8,128)(2,1)}, u32[]{:S(2)}) copy-start(bf16[1,256,256]{2,1,0:T(8,128)(2,1)} %get-tuple-element.7) | copy-start | bytes 393220
  212.5 26.3 %copy-start.6 = (bf16[1,1024,256]{2,1,0:T(8,128)(2,1)S(1)}, bf16[1,1024,256]{2,1,0:T(8,128)(2,1)}, u32[]{:S(2)}) copy-start(bf16[1,1024,256]{2,1,0:T(8,128)(2,1)} %get-tuple-element.3) | copy-start | bytes 1572868
  232.0 37.2 %all-to-all-start.1 = ((f32[32,65,128]{2,1,0:T(8,128)}), f32[32,65,128]{2,1,0:T(8,128)}, u32[]{:S(2)}, u32[]{:S(2)}) async-start(f32[32,65,128]{2,1,0:T(8,128)} %pad_maximum_fusion.1), calls=%async_computation.1 | async-start | bytes 2359296 | tf_op jit(solution)/shard_map/all_to_all | solution.py:119
  240.7 1.4 copy-start.4
  269.2 36.7 %all-to-all-start = ((f32[32,65,128]{2,1,0:T(8,128)}), f32[32,65,128]{2,1,0:T(8,128)S(1)}, u32[]{:S(2)}, u32[]{:S(2)}) async-start(f32[32,65,128]{2,1,0:T(8,128)} %pad_maximum_fusion), calls=%async_computation | async-start | bytes 2359296 | tf_op jit(solution)/shard_map/all_to_all | solution.py:119
  272.9 91.7 %reduce-scatter.2.cloned.1.call-start = ((), (), s32[]{:S(2)}) async-start(), calls=%async_computation.7 | async-start | bytes 2359296 | tf_op jit(solution)/shard_map/reduce_scatter | solution.py:135
  313.7 0.8 copy-start.20
  313.7 0.8 copy-start.33
Sparse Core Ops, SparseCore 0:
  9.8 45.7 all-gather.2
  62.1 78.0 all-gather.4
  313.8 50.7 reduce-scatter.1
where the time goes:
time: 376 us; the launch traced here: 373 us
  waiting for transfers between devices  218 us (58%)
  local copies, waits for them, and re-layouts  53.5 us (14%)
  other arithmetic  36.7 us (10%)
  matrix products  30.8 us (8%)
  starting transfers between devices  18.7 us (5%)
  between operations  14.7 us (4%)
    all_to_all x4, waiting for transfers between devices, body(): received = lax.all_to_all(payload, 'seq', 0, 0, tiled=True)  70 us
    all_gather x1, waiting for transfers between devices, body(): all_queries = lax.all_gather(queries, 'seq', axis=1, tiled=True)  60 us
    reduce_scatter x1, waiting for transfers between devices, body(): lax.psum_scatter(partial_out, 'tensor', scatter_dimension=2, tiled=True)  49.4 us
    all_gather x1, waiting for transfers between devices, body(): lax.all_gather(tokens, 'tensor', axis=2, tiled=True).astype(jnp.float32)  38.2 us
    all_to_all x4, starting transfers between devices, body(): received = lax.all_to_all(payload, 'seq', 0, 0, tiled=True)  18.6 us
    dot_general x3, local copies, waits for them, and re-layouts, project(): jnp.dot(flat_rows, weight, preferred_element_type=jnp.float32)  12.4 us
    unnamed x84, local copies, waits for them, and re-layouts  10.3 us
    dot_general x4, matrix products, body(): jnp.einsum('hqk,khd->qhd', cache_weights.astype(jnp.bfloat16), cache_v, p...  9.73 us
  transfers between devices with their start and end apart: 7, of which 7 were waited for; matrix products, arithmetic and copies ran while one was open for 23% of the time, Pallas kernels for 0%

commit v1 on v0

--- a/solution.py
+++ b/solution.py
@@ -69,6 +69,7 @@
     score_scale = HD ** (-0.5)
     numer_width = local_rows * heads_width
     attended_list = []
+    payload_list = []
     for request in range(requests):
         query_rows = all_queries[request].reshape(group_total, local_heads, HD)
         cache_k = cache_keys[request].reshape(cache_slots, local_heads, HD)
@@ -116,14 +117,20 @@
             ],
             1,
         )
-        received = lax.all_to_all(payload, "seq", 0, 0, tiled=True)
-        block_stats = received[:, pair_rows:].reshape(seq_count, pair_rows, 2)
-        block_peak = block_stats[..., 0]
-        factor = jnp.exp(block_peak - jnp.max(block_peak, 0))
-        mass_sum = jnp.sum(block_stats[..., 1] * factor, 0).reshape(local_rows, local_heads)
-        numer_sum = jnp.sum(received[:, :pair_rows] * factor[..., None], 0)
-        numer_sum = numer_sum.reshape(local_rows, local_heads, HD)
-        attended_list.append(numer_sum / mass_sum[..., None])
+        payload_list.append(payload)
+    block_rows = payload_list[0].shape[1]
+    for first in range(0, requests, 2):
+        sent = jnp.concatenate(payload_list[first : first + 2], 1)
+        arrived = lax.all_to_all(sent, "seq", 0, 0, tiled=True)
+        for member in range(sent.shape[1] // block_rows):
+            received = arrived[:, member * block_rows : (member + 1) * block_rows]
+            block_stats = received[:, pair_rows:].reshape(seq_count, pair_rows, 2)
+            block_peak = block_stats[..., 0]
+            factor = jnp.exp(block_peak - jnp.max(block_peak, 0))
+            mass_sum = jnp.sum(block_stats[..., 1] * factor, 0).reshape(local_rows, local_heads)
+            numer_sum = jnp.sum(received[:, :pair_rows] * factor[..., None], 0)
+            numer_sum = numer_sum.reshape(local_rows, local_heads, HD)
+            attended_list.append(numer_sum / mass_sum[..., None])
     attended = (
         jnp.where(live_rows[..., None, None], jnp.stack(attended_list), 0.0)
         .astype(jnp.bfloat16)

time: 376 us -> 360 us (0.957)
  other arithmetic: 36.7 us -> 27.9 us
  starting transfers between devices: 18.7 us -> 10.4 us
    all_to_all x4 -> x2, starting transfers between devices: 18.6 us -> 10.3 us  [body(): arrived = lax.all_to_all(sent, 'seq', 0, 0, tiled=True)]
    all_to_all x4 -> x2, waiting for transfers between devices: 70 us -> 76.3 us  [body(): arrived = lax.all_to_all(sent, 'seq', 0, 0, tiled=True)]
    all_gather x1, waiting for transfers between devices: 60 us -> 56 us  [body(): all_queries = lax.all_gather(queries, 'seq', axis=1, tiled=True)]
    unnamed x84 -> x80, local copies, waits for them, and re-layouts: 10.3 us -> 12.3 us
  transfers between devices with their start and end apart: 7 -> 5, of which waited for: 7 -> 5; matrix products, arithmetic and copies ran while one was open for 23% -> 18% of each run, Pallas kernels for 0% -> 0%
where the time goes in v1:
time: 360 us; the launch traced here: 358 us
  waiting for transfers between devices  221 us (61%)
  local copies, waits for them, and re-layouts  54 us (15%)
  matrix products  29.6 us (8%)
  other arithmetic  27.9 us (8%)
  between operations  14.7 us (4%)
  starting transfers between devices  10.4 us (3%)
    all_to_all x2, waiting for transfers between devices, body(): arrived = lax.all_to_all(sent, 'seq', 0, 0, tiled=True)  76.3 us
    all_gather x1, waiting for transfers between devices, body(): all_queries = lax.all_gather(queries, 'seq', axis=1, tiled=True)  56 us
    reduce_scatter x1, waiting for transfers between devices, body(): lax.psum_scatter(partial_out, 'tensor', scatter_dimension=2, tiled=True)  50 us
    all_gather x1, waiting for transfers between devices, body(): lax.all_gather(tokens, 'tensor', axis=2, tiled=True).astype(jnp.float32)  38.2 us
    dot_general x3, local copies, waits for them, and re-layouts, project(): jnp.dot(flat_rows, weight, preferred_element_type=jnp.float32)  12.4 us
    unnamed x80, local copies, waits for them, and re-layouts  12.3 us
    all_to_all x2, starting transfers between devices, body(): arrived = lax.all_to_all(sent, 'seq', 0, 0, tiled=True)  10.3 us
    dot_general x4, matrix products, body(): jnp.einsum('hqk,khd->qhd', cache_weights.astype(jnp.bfloat16), cache_v, p...  9.76 us
  transfers between devices with their start and end apart: 5, of which 5 were waited for; matrix products, arithmetic and copies ran while one was open for 18% of the time, Pallas kernels for 0%

profile of v1, /device:TPU:32, one launch (start us, length us, event | category | flops | bytes accessed | tf_op | source)
XLA Modules:
  0.0 358.0 jit_solution(6051463962905533376)
XLA Ops:
  8.0 4.1 %copy.198 = bf16[256,4096]{1,0:T(8,128)(2,1)} copy(bf16[256,4096]{0,1:T(8,128)(2,1)} %bitcast.196) | data formatting | bytes 4194304 | tf_op jit(solution)/shard_map/dot_general | solution.py:41
  12.1 4.1 %copy.197 = bf16[256,4096]{1,0:T(8,128)(2,1)} copy(bf16[256,4096]{0,1:T(8,128)(2,1)} %bitcast.197) | data formatting | bytes 4194304 | tf_op jit(solution)/shard_map/dot_general | solution.py:41
  17.4 38.2 %all-gather.3.cloned.1.call-done = bf16[4,32,4096]{2,1,0:T(8,128)(2,1)} async-done(((bf16[4,32,512]{2,1,0:T(8,128)(2,1)}), bf16[4,32,4096]{2,1,0:T(8,128)(2,1)}) %all-gather.3.cloned.1.call-update) | async-done | bytes 1048592 | tf_op jit(solution)/shard_map/all_gather | solution.py:33
  55.6 1.5 fusion
  57.1 2.9 fusion.92
  60.1 0.9 fusion.94
  62.0 1.8 fusion.122
  63.8 1.0 copy.210
  64.8 1.9 fusion.121
  66.7 1.7 copy.211
  68.4 4.1 %copy.199 = bf16[256,4096]{1,0:T(8,128)(2,1)} copy(bf16[256,4096]{0,1:T(8,128)(2,1)} %bitcast.198) | data formatting | bytes 4194304 | tf_op jit(solution)/shard_map/dot_general | solution.py:41
  73.2 1.7 copy.209
  75.6 1.2 broadcast_compare_fusion.3
  76.8 1.3 broadcast_compare_fusion.1
  78.7 1.8 fusion.96
  81.2 3.1 convolution_convert_fusion
  84.3 56.0 %all-gather.5.cloned.1.call-done = bf16[4,1024,256]{2,1,0:T(8,128)(2,1)} async-done(((bf16[4,32,256]{2,1,0:T(8,128)(2,1)}), bf16[4,1024,256]{2,1,0:T(8,128)(2,1)}) %all-gather.5.cloned.1.call-update) | async-done | bytes 2097168 | tf_op jit(solution)/shard_map/all_gather | solution.py:62
  140.2 2.7 fusion.120
  143.7 1.1 fusion.129
  145.0 1.3 fusion.15
  147.1 1.2 copy.159
  148.3 1.9 reshape.498
  150.2 2.4 convolution_bitcast_fusion.1
  152.6 1.1 fusion.17
  153.8 1.8 copy.158
  155.8 1.0 fusion.130
  156.8 1.4 fusion.7
  158.3 1.3 copy-done.2
  161.0 1.4 copy.148
  162.4 1.9 reshape.496
  164.3 2.4 convolution_bitcast_fusion.3
  166.8 1.2 fusion.18
  167.9 0.8 copy.147
  168.8 1.6 pad_maximum_fusion.1
  170.4 5.7 %all-to-all-start.1 = ((f32[32,130,128]{2,1,0:T(8,128)}), f32[32,130,128]{2,1,0:T(8,128)}, u32[]{:S(2)}, u32[]{:S(2)}) async-start(f32[32,130,128]{2,1,0:T(8,128)} %pad_maximum_fusion.1), calls=%async_computation.1 | async-start | bytes 4456448 | tf_op jit(solution)/shard_map/all_to_all | solution.py:124
  176.1 0.8 copy.206
  176.9 0.8 copy.207
  177.6 0.8 copy.204
  178.4 0.7 copy.205
  179.1 1.3 fusion.98
  180.9 1.4 fusion.6
  182.5 1.2 copy-done.3
  185.0 1.2 copy.127
  186.2 1.9 reshape.490
  188.1 2.4 convolution_bitcast_fusion.5
  190.5 1.1 fusion.19
  191.7 1.8 copy.126
  193.9 1.4 fusion.5
  195.5 1.2 copy-done.4
  197.9 1.3 reshape.488
  199.2 2.5 convolution_bitcast_fusion.7
  202.1 0.8 copy.115
  202.9 1.6 pad_maximum_fusion
  204.5 27.5 %all-to-all-done.1 = f32[32,130,128]{2,1,0:T(8,128)} async-done(((f32[32,130,128]{2,1,0:T(8,128)}), f32[32,130,128]{2,1,0:T(8,128)}, u32[]{:S(2)}, u32[]{:S(2)}) %all-to-all-start.1) | async-done | bytes 2129952 | tf_op jit(solution)/shard_map/all_to_all | solution.py:124
  232.0 4.6 %all-to-all-start = ((f32[32,130,128]{2,1,0:T(8,128)}), f32[32,130,128]{2,1,0:T(8,128)}, u32[]{:S(2)}, u32[]{:S(2)}) async-start(f32[32,130,128]{2,1,0:T(8,128)} %pad_maximum_fusion), calls=%async_computation | async-start | bytes 4456448 | tf_op jit(solution)/shard_map/all_to_all | solution.py:124
  236.7 1.0 fusion.119
  239.5 2.2 fusion.31
  242.6 48.8 %all-to-all-done = f32[32,130,128]{2,1,0:T(8,128)} async-done(((f32[32,130,128]{2,1,0:T(8,128)}), f32[32,130,128]{2,1,0:T(8,128)}, u32[]{:S(2)}, u32[]{:S(2)}) %all-to-all-start) | async-done | bytes 2129952 | tf_op jit(solution)/shard_map/all_to_all | solution.py:124
  291.4 1.0 fusion.118
  294.2 1.9 fusion.33
  297.2 1.9 fusion.3
  299.0 0.7 bitcast_select_fusion
  299.8 50.0 %reduce-scatter.2.cloned.1.call-done = f32[4,32,512]{2,1,0:T(8,128)} async-done(((f32[4,32,4096]{2,1,0:T(8,128)}), f32[4,32,512]{2,1,0:T(8,128)}) %reduce-scatter.2.cloned.1.call-update) | async-done | bytes 262160 | tf_op jit(solution)/shard_map/reduce_scatter | solution.py:142
  349.8 1.6 convert_element_type.74
  (159 shorter events, 18.1 us)
Async XLA Ops:
  7.2 290.0 %copy-start = (bf16[256,4096]{1,0:T(8,128)(2,1)S(1)}, bf16[256,4096]{1,0:T(8,128)(2,1)}, u32[]{:S(2)}) copy-start(bf16[256,4096]{1,0:T(8,128)(2,1)} %param.15) | copy-start | bytes 6291460
  7.2 48.4 %all-gather.3.cloned.1.call-start = ((), (), s32[]{:S(2)}) async-start(), calls=%async_computation.3 | async-start | bytes 1179648 | tf_op jit(solution)/shard_map/all_gather | solution.py:33
  7.9 132.3 %all-gather.5.cloned.1.call-start = ((), (), s32[]{:S(2)}) async-start(), calls=%async_computation.4 | async-start | bytes 2162688 | tf_op jit(solution)/shard_map/all_gather | solution.py:62
  8.0 4.1 %copy-start.25 = (bf16[4096]{0:T(1024)(128)(2,1)S(1)}, bf16[4096]{0:T(1024)(128)(2,1)}, u32[]{:S(2)}) copy-start(bf16[4096]{0:T(1024)(128)(2,1)} %param.11) | copy-start | bytes 24580
  12.1 4.1 %copy-start.26 = (s32[4]{0:T(128)S(1)}, s32[4]{0:T(128)}, u32[]{:S(2)}) copy-start(s32[4]{0:T(128)} %param.18) | copy-start | bytes 52
  57.1 2.9 copy-start.7
  57.1 2.9 copy-start.11
  57.1 2.9 copy-start.33
  60.1 1.0 copy-start.21
  68.4 6.5 %copy-start.28 = (s32[4]{0:T(128)S(1)}, s32[4]{0:T(128)}, u32[]{:S(2)}) copy-start(s32[4]{0:T(128)} %param.19) | copy-start | bytes 52
  68.4 9.7 %copy-start.27 = (s32[4]{0:T(128)S(1)}, s32[4]{0:T(128)}, u32[]{:S(2)}) copy-start(s32[4]{0:T(128)} %param.18) | copy-start | bytes 52
  74.9 68.1 %copy-start.34 = (s32[32]{0:T(128)}, s32[32]{0:T(128)S(1)}, u32[]{:S(2)}) copy-start(s32[32]{0:T(128)S(1)} %iota_add_fusion.1) | copy-start | bytes 388
  80.5 62.7 %copy-start.31 = (pred[256]{0:T(512)(128)(4,1)}, pred[256]{0:T(512)(128)(4,1)S(1)}, u32[]{:S(2)}) copy-start(pred[256]{0:T(512)(128)(4,1)S(1)} %get-tuple-element.73) | copy-start | bytes 772
  143.7 1.4 copy-start.1
  143.7 2.6 copy-start.14
  145.0 5.1 %copy-start.32 = (pred[256]{0:T(512)(128)(4,1)S(1)}, pred[256]{0:T(512)(128)(4,1)}, u32[]{:S(2)}) copy-start(pred[256]{0:T(512)(128)(4,1)} %copy-done.31) | copy-start | bytes 772
  150.2 2.4 copy-start.15
  152.6 3.0 copy-start.10
  153.8 3.0 copy-start.30
  156.8 3.4 copy-start.12
  158.3 1.4 copy-start.2
  164.3 2.4 copy-start.13
  166.7 2.0 copy-start.6
  166.7 2.0 copy-start.23
  166.7 2.0 copy-start.24
  170.3 5.8 %copy-start.17 = (bf16[1,256,256]{2,1,0:T(8,128)(2,1)S(1)}, bf16[1,256,256]{2,1,0:T(8,128)(2,1)}, u32[]{:S(2)}) copy-start(bf16[1,256,256]{2,1,0:T(8,128)(2,1)} %get-tuple-element.21) | copy-start | bytes 393220
  170.3 6.5 %copy-start.19 = (bf16[1,256,256]{2,1,0:T(8,128)(2,1)S(1)}, bf16[1,256,256]{2,1,0:T(8,128)(2,1)}, u32[]{:S(2)}) copy-start(bf16[1,256,256]{2,1,0:T(8,128)(2,1)} %get-tuple-element.17) | copy-start | bytes 393220
  170.3 7.3 %copy-start.16 = (bf16[1,256,256]{2,1,0:T(8,128)(2,1)S(1)}, bf16[1,256,256]{2,1,0:T(8,128)(2,1)}, u32[]{:S(2)}) copy-start(bf16[1,256,256]{2,1,0:T(8,128)(2,1)} %get-tuple-element.19) | copy-start | bytes 393220
  170.3 8.0 %copy-start.18 = (bf16[1,256,256]{2,1,0:T(8,128)(2,1)S(1)}, bf16[1,256,256]{2,1,0:T(8,128)(2,1)}, u32[]{:S(2)}) copy-start(bf16[1,256,256]{2,1,0:T(8,128)(2,1)} %get-tuple-element.15) | copy-start | bytes 393220
  170.3 10.1 %copy-start.9 = (bf16[1,1024,256]{2,1,0:T(8,128)(2,1)S(1)}, bf16[1,1024,256]{2,1,0:T(8,128)(2,1)}, u32[]{:S(2)}) copy-start(bf16[1,1024,256]{2,1,0:T(8,128)(2,1)} %get-tuple-element.14) | copy-start | bytes 1572868
  170.4 61.7 %all-to-all-start.1 = ((f32[32,130,128]{2,1,0:T(8,128)}), f32[32,130,128]{2,1,0:T(8,128)}, u32[]{:S(2)}, u32[]{:S(2)}) async-start(f32[32,130,128]{2,1,0:T(8,128)} %pad_maximum_fusion.1), calls=%async_computation.1 | async-start | bytes 4456448 | tf_op jit(solution)/shard_map/all_to_all | solution.py:124
  182.4 1.3 copy-start.3
  190.5 3.0 copy-start.8
  195.4 1.3 copy-start.4
  199.2 2.5 copy-start.20
  201.7 1.2 copy-start.5
  201.7 1.2 copy-start.22
  204.5 32.1 %copy-start.29 = (s32[4]{0:T(128)S(1)}, s32[4]{0:T(128)}, u32[]{:S(2)}) copy-start(s32[4]{0:T(128)} %param.19) | copy-start | bytes 52
  204.5 32.1 %copy-start.35 = (s32[32]{0:T(128)S(1)}, s32[32]{0:T(128)}, u32[]{:S(2)}) copy-start(s32[32]{0:T(128)} %copy-done.34) | copy-start | bytes 388
  232.0 59.4 %all-to-all-start = ((f32[32,130,128]{2,1,0:T(8,128)}), f32[32,130,128]{2,1,0:T(8,128)}, u32[]{:S(2)}, u32[]{:S(2)}) async-start(f32[32,130,128]{2,1,0:T(8,128)} %pad_maximum_fusion), calls=%async_computation | async-start | bytes 4456448 | tf_op jit(solution)/shard_map/all_to_all | solution.py:124
  236.6 113.2 %reduce-scatter.2.cloned.1.call-start = ((), (), s32[]{:S(2)}) async-start(), calls=%async_computation.5 | async-start | bytes 2359296 | tf_op jit(solution)/shard_map/reduce_scatter | solution.py:142
Sparse Core Ops, SparseCore 0:
  9.8 45.7 all-gather.2
  62.1 78.1 all-gather.4
  299.2 50.6 reduce-scatter.1

commit v2 on v1

--- a/solution.py
+++ b/solution.py
@@ -59,8 +59,11 @@
     live_rows = (first_row + offsets)[None, :] < group_len[:, None]
     new_keys = jnp.where(live_rows[..., None], key_new, jnp.zeros_like(key_new))
     new_values = jnp.where(live_rows[..., None], value_new, jnp.zeros_like(value_new))
-    all_queries = lax.all_gather(queries, "seq", axis=1, tiled=True)
-    group_total = all_queries.shape[1]
+    pair_queries = [
+        lax.all_gather(queries[first : first + 2], "seq", axis=1, tiled=True)
+        for first in range(0, requests, 2)
+    ]
+    group_total = pair_queries[0].shape[1]
     seq_count = group_total // local_rows
     cache_slots = cache_keys.shape[1]
     slot_index = seq_index * cache_slots + jnp.arange(cache_slots, dtype=jnp.int32)
@@ -71,7 +74,7 @@
     attended_list = []
     payload_list = []
     for request in range(requests):
-        query_rows = all_queries[request].reshape(group_total, local_heads, HD)
+        query_rows = pair_queries[request // 2][request % 2].reshape(group_total, local_heads, HD)
         cache_k = cache_keys[request].reshape(cache_slots, local_heads, HD)
         cache_v = cache_values[request].reshape(cache_slots, local_heads, HD)
         group_k = key_new[request].reshape(local_rows, local_heads, HD)
@@ -131,17 +134,26 @@
             numer_sum = jnp.sum(received[:, :pair_rows] * factor[..., None], 0)
             numer_sum = numer_sum.reshape(local_rows, local_heads, HD)
             attended_list.append(numer_sum / mass_sum[..., None])
-    attended = (
-        jnp.where(live_rows[..., None, None], jnp.stack(attended_list), 0.0)
-        .astype(jnp.bfloat16)
-        .reshape(requests * local_rows, heads_width)
-    )
-    partial_out = jnp.dot(attended, w_out, preferred_element_type=jnp.float32).reshape(
-        requests, local_rows, -1
-    )
-    mixed = lax.psum_scatter(partial_out, "tensor", scatter_dimension=2, tiled=True).astype(
-        jnp.bfloat16
-    )
+    mixed_list = []
+    for first in range(0, requests, 2):
+        attended = (
+            jnp.where(
+                live_rows[first : first + 2, :, None, None],
+                jnp.stack(attended_list[first : first + 2]),
+                0.0,
+            )
+            .astype(jnp.bfloat16)
+            .reshape(-1, heads_width)
+        )
+        partial_out = jnp.dot(attended, w_out, preferred_element_type=jnp.float32).reshape(
+            -1, local_rows, w_out.shape[1]
+        )
+        mixed_list.append(
+            lax.psum_scatter(partial_out, "tensor", scatter_dimension=2, tiled=True).astype(
+                jnp.bfloat16
+            )
+        )
+    mixed = jnp.concatenate(mixed_list, 0)
     return (mixed, new_keys, new_values)
 
 

time: 360 us -> 374 us (1.039)
  local copies, waits for them, and re-layouts: 54 us -> 60.7 us
  starting transfers between devices: 10.4 us -> 14.3 us
    all_gather x1 -> x2, waiting for transfers between devices: 56 us -> 92.2 us  [body(): lax.all_gather(queries[first:first + 2], 'seq', axis=1, tiled=True)]
    all_to_all x2, waiting for transfers between devices: 76.3 us -> 48.2 us  [body(): arrived = lax.all_to_all(sent, 'seq', 0, 0, tiled=True)]
    reduce_scatter x1 -> x2, waiting for transfers between devices: 50 us -> 42.9 us  [body(): lax.psum_scatter(partial_out, 'tensor', scatter_dimension=2, tiled=True)]
    unnamed x80 -> x75, local copies, waits for them, and re-layouts: 12.3 us -> 16.4 us
  transfers between devices with their start and end apart: 5 -> 7, of which waited for: 5 -> 5; matrix products, arithmetic and copies ran while one was open for 18% -> 29% of each run, Pallas kernels for 0% -> 0%
where the time goes in v2:
time: 374 us; the launch traced here: 372 us
  waiting for transfers between devices  222 us (59%)
  local copies, waits for them, and re-layouts  60.7 us (16%)
  matrix products  30.9 us (8%)
  other arithmetic  29 us (8%)
  between operations  14.7 us (4%)
  starting transfers between devices  14.3 us (4%)
    all_gather x2, waiting for transfers between devices, body(): lax.all_gather(queries[first:first + 2], 'seq', axis=1, tiled=True)  92.2 us
    all_to_all x2, waiting for transfers between devices, body(): arrived = lax.all_to_all(sent, 'seq', 0, 0, tiled=True)  48.2 us
    reduce_scatter x2, waiting for transfers between devices, body(): lax.psum_scatter(partial_out, 'tensor', scatter_dimension=2, tiled=True)  42.9 us
    all_gather x1, waiting for transfers between devices, body(): lax.all_gather(tokens, 'tensor', axis=2, tiled=True).astype(jnp.float32)  38.2 us
    unnamed x75, local copies, waits for them, and re-layouts  16.4 us
    all_to_all x2, starting transfers between devices, body(): arrived = lax.all_to_all(sent, 'seq', 0, 0, tiled=True)  13.7 us
    dot_general x3, local copies, waits for them, and re-layouts, project(): jnp.dot(flat_rows, weight, preferred_element_type=jnp.float32)  12.4 us
    dot_general x4, matrix products, body(): jnp.einsum('hqk,khd->qhd', cache_weights.astype(jnp.bfloat16), cache_v, p...  9.76 us
  transfers between devices with their start and end apart: 7, of which 5 were waited for; matrix products, arithmetic and copies ran while one was open for 29% of the time, Pallas kernels for 0%

profile of v2, /device:TPU:32, one launch (start us, length us, event | category | flops | bytes accessed | tf_op | source)
XLA Modules:
  0.0 372.0 jit_solution(17640662961514611982)
XLA Ops:
  8.0 4.1 %copy.200 = bf16[256,4096]{1,0:T(8,128)(2,1)} copy(bf16[256,4096]{0,1:T(8,128)(2,1)} %bitcast.203) | data formatting | bytes 4194304 | tf_op jit(solution)/shard_map/dot_general | solution.py:41
  12.1 4.1 %copy.199 = bf16[256,4096]{1,0:T(8,128)(2,1)} copy(bf16[256,4096]{0,1:T(8,128)(2,1)} %bitcast.204) | data formatting | bytes 4194304 | tf_op jit(solution)/shard_map/dot_general | solution.py:41
  17.4 38.2 %all-gather.4.cloned.1.call-done = bf16[4,32,4096]{2,1,0:T(8,128)(2,1)} async-done(((bf16[4,32,512]{2,1,0:T(8,128)(2,1)}), bf16[4,32,4096]{2,1,0:T(8,128)(2,1)}) %all-gather.4.cloned.1.call-update) | async-done | bytes 1048592 | tf_op jit(solution)/shard_map/all_gather | solution.py:33
  55.6 1.5 fusion
  57.1 2.9 fusion.91
  62.8 1.8 fusion.130
  64.6 1.0 copy.212
  65.6 1.9 fusion.129
  67.5 1.7 copy.213
  69.2 4.1 %copy.201 = bf16[256,4096]{1,0:T(8,128)(2,1)} copy(bf16[256,4096]{0,1:T(8,128)(2,1)} %bitcast.205) | data formatting | bytes 4194304 | tf_op jit(solution)/shard_map/dot_general | solution.py:41
  73.3 1.6 copy.210
  75.0 1.7 copy.211
  76.6 1.7 copy.208
  78.3 1.7 copy.209
  80.7 1.7 copy.207
  83.0 1.3 broadcast_compare_fusion.3
  84.3 1.2 broadcast_compare_fusion.1
  86.1 1.8 fusion.101
  87.8 1.8 fusion.103
  90.3 1.4 copy.223
  91.7 3.1 convolution_convert_fusion
  94.8 43.8 %all-gather.8.cloned.1.call-done = bf16[2,1024,256]{2,1,0:T(8,128)(2,1)} async-done(((bf16[2,32,256]{2,1,0:T(8,128)(2,1)}), bf16[2,1024,256]{2,1,0:T(8,128)(2,1)}) %all-gather.8.cloned.1.call-update) | async-done | bytes 1048592 | tf_op jit(solution)/shard_map/all_gather | solution.py:63
  138.6 2.1 fusion.128
  141.4 1.1 fusion.138
  142.7 1.3 fusion.17
  144.8 1.2 copy.161
  146.0 1.9 reshape.484
  147.9 2.4 convolution_bitcast_fusion.1
  150.4 1.1 fusion.19
  151.5 1.8 copy.160
  153.6 1.0 fusion.139
  154.6 1.4 fusion.9
  156.2 1.2 copy-done.2
  158.6 1.2 copy.150
  159.9 1.9 reshape.482
  161.8 2.4 convolution_bitcast_fusion.3
  164.2 1.2 fusion.20
  166.3 1.6 pad_maximum_fusion.1
  167.8 6.7 %all-to-all-start.1 = ((f32[32,130,128]{2,1,0:T(8,128)}), f32[32,130,128]{2,1,0:T(8,128)}, u32[]{:S(2)}, u32[]{:S(2)}) async-start(f32[32,130,128]{2,1,0:T(8,128)} %pad_maximum_fusion.1), calls=%async_computation.2 | async-start | bytes 4456448 | tf_op jit(solution)/shard_map/all_to_all | solution.py:127
  174.5 48.5 %all-gather.6.cloned.1.call-done = bf16[2,1024,256]{2,1,0:T(8,128)(2,1)} async-done(((bf16[2,32,256]{2,1,0:T(8,128)(2,1)}), bf16[2,1024,256]{2,1,0:T(8,128)(2,1)}) %all-gather.6.cloned.1.call-update) | async-done | bytes 1048592 | tf_op jit(solution)/shard_map/all_gather | solution.py:63
  223.0 2.1 fusion.127
  225.5 1.4 fusion.8
  227.0 1.2 copy-done.3
  229.5 1.2 copy.128
  230.8 1.9 reshape.476
  232.7 2.4 convolution_bitcast_fusion.5
  235.1 1.1 fusion.21
  236.3 1.8 copy.127
  238.5 1.4 fusion.7
  240.1 1.2 copy-done.4
  242.5 1.3 reshape.474
  243.8 2.5 convolution_bitcast_fusion.7
  247.5 1.6 pad_maximum_fusion
  249.1 7.0 %all-to-all-start = ((f32[32,130,128]{2,1,0:T(8,128)}), f32[32,130,128]{2,1,0:T(8,128)}, u32[]{:S(2)}, u32[]{:S(2)}) async-start(f32[32,130,128]{2,1,0:T(8,128)} %pad_maximum_fusion), calls=%async_computation | async-start | bytes 4456448 | tf_op jit(solution)/shard_map/all_to_all | solution.py:127
  256.6 1.0 fusion.126
  259.4 1.9 fusion.33
  262.3 1.5 fusion.3
  263.9 48.2 %all-to-all-done = f32[32,130,128]{2,1,0:T(8,128)} async-done(((f32[32,130,128]{2,1,0:T(8,128)}), f32[32,130,128]{2,1,0:T(8,128)}, u32[]{:S(2)}, u32[]{:S(2)}) %all-to-all-start) | async-done | bytes 2129952 | tf_op jit(solution)/shard_map/all_to_all | solution.py:127
  312.1 1.0 fusion.125
  314.8 1.9 fusion.35
  317.8 1.6 fusion.5
  320.1 0.9 convert_element_type.84
  321.0 42.9 %reduce-scatter.3.cloned.1.call-done = f32[2,32,512]{2,1,0:T(8,128)} async-done(((f32[2,32,4096]{2,1,0:T(8,128)}), f32[2,32,512]{2,1,0:T(8,128)}) %reduce-scatter.3.cloned.1.call-update) | async-done | bytes 131088 | tf_op jit(solution)/shard_map/reduce_scatter | solution.py:152
  363.9 0.9 convert_element_type.78
  (166 shorter events, 23.2 us)
Async XLA Ops:
  7.2 255.1 %copy-start = (bf16[256,4096]{1,0:T(8,128)(2,1)S(1)}, bf16[256,4096]{1,0:T(8,128)(2,1)}, u32[]{:S(2)}) copy-start(bf16[256,4096]{1,0:T(8,128)(2,1)} %param.15) | copy-start | bytes 6291460
  7.2 48.4 %all-gather.4.cloned.1.call-start = ((), (), s32[]{:S(2)}) async-start(), calls=%async_computation.4 | async-start | bytes 1179648 | tf_op jit(solution)/shard_map/all_gather | solution.py:33
  7.9 130.7 %all-gather.8.cloned.1.call-start = ((), (), s32[]{:S(2)}) async-start(), calls=%async_computation.7 | async-start | bytes 1081344 | tf_op jit(solution)/shard_map/all_gather | solution.py:63
  8.0 4.1 %copy-start.20 = (bf16[4096]{0:T(1024)(128)(2,1)S(1)}, bf16[4096]{0:T(1024)(128)(2,1)}, u32[]{:S(2)}) copy-start(bf16[4096]{0:T(1024)(128)(2,1)} %param.11) | copy-start | bytes 24580
  12.1 4.1 %copy-start.21 = (s32[4]{0:T(128)S(1)}, s32[4]{0:T(128)}, u32[]{:S(2)}) copy-start(s32[4]{0:T(128)} %param.18) | copy-start | bytes 52
  57.1 2.9 copy-start.7
  57.1 2.9 copy-start.10
  57.1 2.9 copy-start.30
  60.1 1.0 copy-start.16
  62.5 160.4 %all-gather.6.cloned.1.call-start = ((), (), s32[]{:S(2)}) async-start(), calls=%async_computation.5 | async-start | bytes 1081344 | tf_op jit(solution)/shard_map/all_gather | solution.py:63
  69.2 13.2 %copy-start.23 = (s32[4]{0:T(128)S(1)}, s32[4]{0:T(128)}, u32[]{:S(2)}) copy-start(s32[4]{0:T(128)} %param.19) | copy-start | bytes 52
  69.2 16.3 %copy-start.22 = (s32[4]{0:T(128)S(1)}, s32[4]{0:T(128)}, u32[]{:S(2)}) copy-start(s32[4]{0:T(128)} %param.18) | copy-start | bytes 52
  82.4 12.4 %copy-start.31 = (s32[32]{0:T(128)}, s32[32]{0:T(128)S(1)}, u32[]{:S(2)}) copy-start(s32[32]{0:T(128)S(1)} %iota_add_fusion.1) | copy-start | bytes 388
  87.8 53.0 %copy-start.28 = (pred[256]{0:T(512)(128)(4,1)}, pred[256]{0:T(512)(128)(4,1)S(1)}, u32[]{:S(2)}) copy-start(pred[256]{0:T(512)(128)(4,1)S(1)} %get-tuple-element.77) | copy-start | bytes 772
  141.4 1.4 copy-start.1
  141.4 2.7 copy-start.13
  142.7 5.2 %copy-start.29 = (pred[256]{0:T(512)(128)(4,1)S(1)}, pred[256]{0:T(512)(128)(4,1)}, u32[]{:S(2)}) copy-start(pred[256]{0:T(512)(128)(4,1)} %copy-done.28) | copy-start | bytes 772
  147.9 2.4 copy-start.14
  150.4 3.0 copy-start.8
  151.5 3.1 copy-start.27
  153.5 2.5 copy-start.11
  156.1 1.4 copy-start.2
  161.8 2.4 copy-start.12
  164.2 2.0 copy-start.6
  164.2 2.0 copy-start.18
  164.2 2.0 copy-start.19
  167.8 81.3 %all-to-all-start.1 = ((f32[32,130,128]{2,1,0:T(8,128)}), f32[32,130,128]{2,1,0:T(8,128)}, u32[]{:S(2)}, u32[]{:S(2)}) async-start(f32[32,130,128]{2,1,0:T(8,128)} %pad_maximum_fusion.1), calls=%async_computation.2 | async-start | bytes 4456448 | tf_op jit(solution)/shard_map/all_to_all | solution.py:127
  174.5 51.0 %copy-start.26 = (pred[256]{0:T(512)(128)(4,1)S(1)}, pred[256]{0:T(512)(128)(4,1)}, u32[]{:S(2)}) copy-start(pred[256]{0:T(512)(128)(4,1)} %get-tuple-element.79) | copy-start | bytes 772
  226.9 1.3 copy-start.3
  235.1 3.0 copy-start.9
  236.2 2.3 copy-start.25
  240.0 1.3 copy-start.4
  243.8 2.5 copy-start.15
  246.3 1.2 copy-start.5
  246.3 1.2 copy-start.17
  249.1 7.4 %copy-start.24 = (s32[4]{0:T(128)S(1)}, s32[4]{0:T(128)}, u32[]{:S(2)}) copy-start(s32[4]{0:T(128)} %param.19) | copy-start | bytes 52
  249.1 7.4 %copy-start.32 = (s32[32]{0:T(128)S(1)}, s32[32]{0:T(128)}, u32[]{:S(2)}) copy-start(s32[32]{0:T(128)} %copy-done.31) | copy-start | bytes 388
  249.1 63.0 %all-to-all-start = ((f32[32,130,128]{2,1,0:T(8,128)}), f32[32,130,128]{2,1,0:T(8,128)}, u32[]{:S(2)}, u32[]{:S(2)}) async-start(f32[32,130,128]{2,1,0:T(8,128)} %pad_maximum_fusion), calls=%async_computation | async-start | bytes 4456448 | tf_op jit(solution)/shard_map/all_to_all | solution.py:127
  256.2 63.9 %reduce-scatter.5.cloned.1.call-start = ((), (), s32[]{:S(2)}) async-start(), calls=%async_computation.8 | async-start | bytes 1179648 | tf_op jit(solution)/shard_map/reduce_scatter | solution.py:152
  263.8 100.1 %reduce-scatter.3.cloned.1.call-start = ((), (), s32[]{:S(2)}) async-start(), calls=%async_computation.6 | async-start | bytes 1179648 | tf_op jit(solution)/shard_map/reduce_scatter | solution.py:152
Sparse Core Ops, SparseCore 0:
  9.8 45.7 all-gather.3
  62.7 75.8 all-gather.7
  141.4 81.5 all-gather.5
  263.9 54.4 reduce-scatter.4
  320.8 43.0 reduce-scatter.2

commit v3 on v1

--- a/solution.py
+++ b/solution.py
@@ -59,80 +59,100 @@
     live_rows = (first_row + offsets)[None, :] < group_len[:, None]
     new_keys = jnp.where(live_rows[..., None], key_new, jnp.zeros_like(key_new))
     new_values = jnp.where(live_rows[..., None], value_new, jnp.zeros_like(value_new))
-    all_queries = lax.all_gather(queries, "seq", axis=1, tiled=True)
-    group_total = all_queries.shape[1]
-    seq_count = group_total // local_rows
+    seq_count = lax.axis_size("seq")
+    group_total = seq_count * local_rows
     cache_slots = cache_keys.shape[1]
-    slot_index = seq_index * cache_slots + jnp.arange(cache_slots, dtype=jnp.int32)
+    head = seq_index % local_heads
+    partner = seq_index + 1 - 2 * head
+    swap = [(index, index + 1 - 2 * (index % 2)) for index in range(seq_count)]
+
+    def own_head(array):
+        return lax.dynamic_slice_in_dim(array, head * HD, HD, axis=2)
+
+    def other_head(array):
+        return lax.dynamic_slice_in_dim(array, (1 - head) * HD, HD, axis=2)
+
+    cache_pair = lax.ppermute(
+        jnp.concatenate([other_head(cache_keys), other_head(cache_values)], 1), "seq", swap
+    )
+    fresh_pair = lax.ppermute(
+        jnp.concatenate([other_head(key_new), other_head(value_new)], 1), "seq", swap
+    )
+    pair_keys = jnp.concatenate([own_head(cache_keys), cache_pair[:, :cache_slots]], 1)
+    pair_values = jnp.concatenate([own_head(cache_values), cache_pair[:, cache_slots:]], 1)
+    group_keys = jnp.concatenate([own_head(key_new), fresh_pair[:, :local_rows]], 1)
+    group_values = jnp.concatenate([own_head(value_new), fresh_pair[:, local_rows:]], 1)
+    slot_arange = jnp.arange(cache_slots, dtype=jnp.int32)
+    slot_index = jnp.concatenate(
+        [seq_index * cache_slots + slot_arange, partner * cache_slots + slot_arange]
+    )
+    token_index = jnp.concatenate(
+        [seq_index * local_rows + offsets, partner * local_rows + offsets]
+    )
+    query_heads = jnp.stack(
+        [queries[:, :, h * HD : (h + 1) * HD] for h in range(local_heads)]
+    ).reshape(local_heads, requests * local_rows, HD)
+    query_sent = jnp.tile(query_heads, (seq_count // local_heads, 1, 1))
+    query_got = lax.all_to_all(query_sent, "seq", 0, 0, tiled=True)
     query_index = jnp.arange(group_total, dtype=jnp.int32)
-    token_index = first_row + offsets
     score_scale = HD ** (-0.5)
-    numer_width = local_rows * heads_width
-    attended_list = []
     payload_list = []
     for request in range(requests):
-        query_rows = all_queries[request].reshape(group_total, local_heads, HD)
-        cache_k = cache_keys[request].reshape(cache_slots, local_heads, HD)
-        cache_v = cache_values[request].reshape(cache_slots, local_heads, HD)
-        group_k = key_new[request].reshape(local_rows, local_heads, HD)
-        group_v = value_new[request].reshape(local_rows, local_heads, HD)
-        cache_ok = (slot_index < cache_len[request])[None, None, :]
-        group_ok = (
-            (token_index[None, :] <= query_index[:, None])
-            & (token_index < group_len[request])[None, :]
-        )[None]
+        query_rows = query_got[:, request * local_rows : (request + 1) * local_rows].reshape(
+            group_total, HD
+        )
+        cache_ok = (slot_index < cache_len[request])[None, :]
+        group_ok = (token_index[None, :] <= query_index[:, None]) & (
+            token_index < group_len[request]
+        )[None, :]
         cache_scores = jnp.where(
             cache_ok,
-            jnp.einsum("qhd,khd->hqk", query_rows, cache_k, preferred_element_type=jnp.float32)
+            jnp.dot(query_rows, pair_keys[request].T, preferred_element_type=jnp.float32)
             * score_scale,
             -1e30,
         )
         group_scores = jnp.where(
             group_ok,
-            jnp.einsum("qhd,khd->hqk", query_rows, group_k, preferred_element_type=jnp.float32)
+            jnp.dot(query_rows, group_keys[request].T, preferred_element_type=jnp.float32)
             * score_scale,
             -1e30,
         )
         row_peak = jnp.maximum(jnp.max(cache_scores, -1), jnp.max(group_scores, -1))
-        cache_weights = jnp.where(cache_ok, jnp.exp(cache_scores - row_peak[..., None]), 0.0)
-        group_weights = jnp.where(group_ok, jnp.exp(group_scores - row_peak[..., None]), 0.0)
+        cache_weights = jnp.where(cache_ok, jnp.exp(cache_scores - row_peak[:, None]), 0.0)
+        group_weights = jnp.where(group_ok, jnp.exp(group_scores - row_peak[:, None]), 0.0)
         row_mass = jnp.sum(cache_weights, -1) + jnp.sum(group_weights, -1)
-        numerators = jnp.einsum(
-            "hqk,khd->qhd",
+        numerators = jnp.dot(
             cache_weights.astype(jnp.bfloat16),
-            cache_v,
+            pair_values[request],
             preferred_element_type=jnp.float32,
-        ) + jnp.einsum(
-            "hqk,khd->qhd",
+        ) + jnp.dot(
             group_weights.astype(jnp.bfloat16),
-            group_v,
+            group_values[request],
             preferred_element_type=jnp.float32,
         )
-        stats = jnp.stack([row_peak.T, row_mass.T], -1)
-        pair_rows = local_rows * local_heads
-        payload = jnp.concatenate(
-            [
-                numerators.reshape(seq_count, pair_rows, HD),
-                stats.reshape(seq_count, -1, HD),
-            ],
-            1,
+        stats = jnp.stack([row_peak, row_mass], -1).reshape(seq_count, 1, local_rows * 2)
+        stats = jnp.pad(stats, ((0, 0), (0, 0), (0, HD - local_rows * 2)))
+        payload_list.append(
+            jnp.concatenate([numerators.reshape(seq_count, local_rows, HD), stats], 1)
         )
-        payload_list.append(payload)
-    block_rows = payload_list[0].shape[1]
+    block_rows = local_rows + 1
+    attended_list = []
     for first in range(0, requests, 2):
         sent = jnp.concatenate(payload_list[first : first + 2], 1)
         arrived = lax.all_to_all(sent, "seq", 0, 0, tiled=True)
         for member in range(sent.shape[1] // block_rows):
-            received = arrived[:, member * block_rows : (member + 1) * block_rows]
-            block_stats = received[:, pair_rows:].reshape(seq_count, pair_rows, 2)
-            block_peak = block_stats[..., 0]
-            factor = jnp.exp(block_peak - jnp.max(block_peak, 0))
-            mass_sum = jnp.sum(block_stats[..., 1] * factor, 0).reshape(local_rows, local_heads)
-            numer_sum = jnp.sum(received[:, :pair_rows] * factor[..., None], 0)
-            numer_sum = numer_sum.reshape(local_rows, local_heads, HD)
-            attended_list.append(numer_sum / mass_sum[..., None])
+            head_parts = []
+            for h in range(local_heads):
+                received = arrived[h::local_heads, member * block_rows : (member + 1) * block_rows]
+                block_stats = received[:, local_rows, : local_rows * 2].reshape(-1, local_rows, 2)
+                block_peak = block_stats[..., 0]
+                factor = jnp.exp(block_peak - jnp.max(block_peak, 0))
+                mass_sum = jnp.sum(block_stats[..., 1] * factor, 0)
+                numer_sum = jnp.sum(received[:, :local_rows] * factor[..., None], 0)
+                head_parts.append(numer_sum / mass_sum[:, None])
+            attended_list.append(jnp.concatenate(head_parts, -1))
     attended = (
-        jnp.where(live_rows[..., None, None], jnp.stack(attended_list), 0.0)
+        jnp.where(live_rows[..., None], jnp.stack(attended_list), 0.0)
         .astype(jnp.bfloat16)
         .reshape(requests * local_rows, heads_width)
     )

time: 360 us -> 271 us (0.75)
  waiting for transfers between devices: 221 us -> 124 us
  other arithmetic: 27.9 us -> 45.5 us
  local copies, waits for them, and re-layouts: 54 us -> 40.5 us
  starting transfers between devices: 10.4 us -> 18.7 us
  matrix products: 29.6 us -> 23.8 us
    all_gather x1 -> x0, waiting for transfers between devices: 56 us -> none  [body(): all_queries = lax.all_gather(queries, 'seq', axis=1, tiled=True)]
    all_to_all x2, waiting for transfers between devices: 76.3 us -> 29.3 us  [body(): arrived = lax.all_to_all(sent, 'seq', 0, 0, tiled=True)]
    all_to_all x0 -> x1, waiting for transfers between devices: none -> 13.6 us  [body(): query_got = lax.all_to_all(query_sent, 'seq', 0, 0, tiled=True)]
    all_to_all x0 -> x1, starting transfers between devices: none -> 9.82 us  [body(): query_got = lax.all_to_all(query_sent, 'seq', 0, 0, tiled=True)]
    unnamed x80 -> x94, local copies, waits for them, and re-layouts: 12.3 us -> 2.57 us
    reduce_sum x6 -> x16, other arithmetic: 4.84 us -> 11.9 us  [the longest x8 6.68 us: body(): numer_sum = jnp.sum(received[:, :local_rows] * factor[..., None], 0)]
    dot_general x16, matrix products: 20.9 us -> 15.1 us  [the longest x4 6.73 us: body(): jnp.dot(cache_weights.astype(jnp.bfloat16), pair_values[request], preferr...]
    add x4 -> x0, local copies, waits for them, and re-layouts: 5.23 us -> none  [body(): jnp.einsum('hqk,khd->qhd', cache_weights.astype(jnp.bfloat16), cache_v, p...]
  transfers between devices with their start and end apart: 5 -> 7, of which waited for: 5 -> 5; matrix products, arithmetic and copies ran while one was open for 18% -> 27% of each run, Pallas kernels for 0% -> 0%
where the time goes in v3:
time: 271 us; the launch traced here: 268 us
  waiting for transfers between devices  124 us (46%)
  other arithmetic  45.5 us (17%)
  local copies, waits for them, and re-layouts  40.5 us (15%)
  matrix products  23.8 us (9%)
  starting transfers between devices  18.7 us (7%)
  between operations  15.1 us (6%)
    reduce_scatter x1, waiting for transfers between devices, body(): lax.psum_scatter(partial_out, 'tensor', scatter_dimension=2, tiled=True)  46.4 us
    all_gather x1, waiting for transfers between devices, body(): lax.all_gather(tokens, 'tensor', axis=2, tiled=True).astype(jnp.float32)  34.4 us
    all_to_all x2, waiting for transfers between devices, body(): arrived = lax.all_to_all(sent, 'seq', 0, 0, tiled=True)  29.3 us
    all_to_all x1, waiting for transfers between devices, body(): query_got = lax.all_to_all(query_sent, 'seq', 0, 0, tiled=True)  13.6 us
    dot_general x3, local copies, waits for them, and re-layouts, project(): jnp.dot(flat_rows, weight, preferred_element_type=jnp.float32)  12.4 us
    all_to_all x1, starting transfers between devices, body(): query_got = lax.all_to_all(query_sent, 'seq', 0, 0, tiled=True)  9.82 us
    all_to_all x2, starting transfers between devices, body(): arrived = lax.all_to_all(sent, 'seq', 0, 0, tiled=True)  8.4 us
    dot_general x4, matrix products, body(): jnp.dot(cache_weights.astype(jnp.bfloat16), pair_values[request], preferr...  6.73 us
  transfers between devices with their start and end apart: 7, of which 5 were waited for; matrix products, arithmetic and copies ran while one was open for 27% of the time, Pallas kernels for 0%

profile of v3, /device:TPU:32, one launch (start us, length us, event | category | flops | bytes accessed | tf_op | source)
XLA Modules:
  0.0 267.9 jit_solution(5694304191916388764)
XLA Ops:
  7.9 1.1 constant_dynamic-slice_fusion.7
  9.0 1.8 constant_dynamic-slice_fusion.1
  10.8 0.8 pad_maximum_fusion.2
  11.7 4.1 %copy.153 = bf16[256,4096]{1,0:T(8,128)(2,1)} copy(bf16[256,4096]{0,1:T(8,128)(2,1)} %bitcast.189) | data formatting | bytes 4194304 | tf_op jit(solution)/shard_map/dot_general | solution.py:41
  15.8 4.1 %copy.154 = bf16[256,4096]{1,0:T(8,128)(2,1)} copy(bf16[256,4096]{0,1:T(8,128)(2,1)} %bitcast.190) | data formatting | bytes 4194304 | tf_op jit(solution)/shard_map/dot_general | solution.py:41
  21.2 34.4 %all-gather.2.cloned.1.call-done = bf16[4,32,4096]{2,1,0:T(8,128)(2,1)} async-done(((bf16[4,32,512]{2,1,0:T(8,128)(2,1)}), bf16[4,32,4096]{2,1,0:T(8,128)(2,1)}) %all-gather.2.cloned.1.call-update) | async-done | bytes 1048592 | tf_op jit(solution)/shard_map/all_gather | solution.py:33
  55.6 1.5 fusion
  57.2 2.9 %fusion.128 = f32[4,32,2,128]{3,1,2,0:T(8,128)S(1)} fusion(bf16[2,128,4096,1]{2,1,0,3:T(8,128)(2,1)} %bitcast.194, bf16[4,32,4096]{2,1,0:T(8,128)(2,1)} %all-gather.2.cloned.1.call-done, f32[4096]{0:T(1024)S(1)} %convert_element_type.64, f32[4,32]{1,0:T(4,128)S(1)} %add_rsqrt_fusion), kind=kOutput, calls=%fused_computation.186 | convolution fusion | flops 270532608 | bytes 3293696 | tf_op jit(solution)/shard_map/dot_general | solution.py:41
  60.2 0.9 fusion.126
  61.4 1.2 tile.11
  62.7 9.8 %all-to-all-start = ((bf16[32,128,128]{2,1,0:T(8,128)(2,1)}), bf16[32,128,128]{2,1,0:T(8,128)(2,1)}, u32[]{:S(2)}, u32[]{:S(2)}) async-start(bf16[32,128,128]{2,1,0:T(8,128)(2,1)} %bitcast.9), calls=%async_computation | async-start | bytes 2097152 | tf_op jit(solution)/shard_map/all_to_all | solution.py:96
  72.5 4.1 %copy.155 = bf16[256,4096]{1,0:T(8,128)(2,1)} copy(bf16[256,4096]{0,1:T(8,128)(2,1)} %bitcast.191) | data formatting | bytes 4194304 | tf_op jit(solution)/shard_map/dot_general | solution.py:41
  77.3 1.2 broadcast_compare_fusion.6
  79.2 3.0 %broadcast_compare_fusion.1 = (pred[512]{0:T(512)(128)(4,1)S(1)}, pred[512]{0:T(512)(128)(4,1)}, pred[512]{0:T(512)(128)(4,1)S(1)}, pred[512]{0:T(512)(128)(4,1)}) fusion(s32[]{:T(128)} %bitcast.56, s32[256]{0:T(256)S(1)} %iota_add_fusion, s32[256]{0:T(256)S(1)} %iota_add_fusion.1, s32[]{:T(128)} %bitcast.27, s32[]{:T(128)} %bitcast.67, s32[]{:T(128)} %bitcast), kind=kLoop, calls=%fused_computation.249 | loop fusion | flops 2560 | bytes 4112 | tf_op jit(solution)/shard_map/lt | solution.py:104
  82.2 2.4 broadcast_compare_fusion.7
  84.7 2.4 fusion.21
  87.6 1.8 fusion.191
  89.4 13.6 %all-to-all-done = bf16[32,128,128]{2,1,0:T(8,128)(2,1)} async-done(((bf16[32,128,128]{2,1,0:T(8,128)(2,1)}), bf16[32,128,128]{2,1,0:T(8,128)(2,1)}, u32[]{:S(2)}, u32[]{:S(2)}) %all-to-all-start) | async-done | bytes 1048608 | tf_op jit(solution)/shard_map/all_to_all | solution.py:96
  103.0 1.3 fusion.190
  104.8 1.8 fusion.7
  106.6 1.7 fusion.8
  110.5 1.1 fusion.9
  111.6 1.7 convolution_add_fusion.2
  113.3 1.6 convolution_add_fusion.3
  115.0 0.9 fusion.55
  117.0 2.2 pad_maximum_fusion
  119.2 3.7 %all-to-all-start.1 = ((f32[32,66,128]{2,1,0:T(8,128)}), f32[32,66,128]{2,1,0:T(8,128)S(1)}, u32[]{:S(2)}, u32[]{:S(2)}) async-start(f32[32,66,128]{2,1,0:T(8,128)} %pad_maximum_fusion), calls=%async_computation.1 | async-start | bytes 2359296 | tf_op jit(solution)/shard_map/all_to_all | solution.py:142
  122.9 1.2 broadcast_compare_fusion.4
  124.2 3.9 %fusion.13 = (f32[1024]{0:T(1024)S(1)}, f32[1024]{0:T(1024)}) fusion(f32[1024,512]{0,1:T(8,128)} %get-tuple-element.97, f32[1024]{0:T(1024)S(1)} %max.60, pred[512]{0:T(512)(128)(4,1)} %copy-done.33, f32[1024]{0:T(1024)S(1)} %max.62, f32[1024,512]{0,1:T(8,128)} %get-tuple-element.85, pred[512]{0:T(512)(128)(4,1)} %copy-done.31), kind=kLoop, calls=%fused_computation.23 | loop fusion | flops 5240832 | bytes 4211712 | tf_op jit(solution)/shard_map/reduce_sum | solution.py:123
  128.1 1.0 copy.132
  129.1 1.9 reshape.410
  131.0 1.3 pad.15
  133.0 1.0 copy.133
  134.1 1.9 reshape.413
  136.7 1.3 fusion.65
  138.0 1.1 fusion.63
  139.1 2.6 convolution_add_fusion.1
  141.8 0.8 convolution_add_fusion
  142.6 1.1 pad_maximum_fusion.1
  143.7 12.2 %all-to-all-done.1 = f32[32,66,128]{2,1,0:T(8,128)S(1)} async-done(((f32[32,66,128]{2,1,0:T(8,128)}), f32[32,66,128]{2,1,0:T(8,128)S(1)}, u32[]{:S(2)}, u32[]{:S(2)}) %all-to-all-start.1) | async-done | bytes 1081376 | tf_op jit(solution)/shard_map/all_to_all | solution.py:142
  155.9 4.7 %all-to-all-start.2 = ((f32[32,66,128]{2,1,0:T(8,128)}), f32[32,66,128]{2,1,0:T(8,128)}, u32[]{:S(2)}, u32[]{:S(2)}) async-start(f32[32,66,128]{2,1,0:T(8,128)} %pad_maximum_fusion.1), calls=%async_computation.2 | async-start | bytes 2359296 | tf_op jit(solution)/shard_map/all_to_all | solution.py:142
  160.7 1.0 fusion.188
  162.5 0.8 fusion.194
  163.3 0.8 slice.353
  164.2 0.8 slice.349
  165.0 0.8 slice.345
  166.3 0.8 fusion.197
  167.7 0.8 fusion.196
  168.7 0.8 fusion.195
  170.1 1.7 fusion.50
  171.8 1.7 fusion.47
  173.5 1.7 fusion.48
  175.2 1.1 fusion.49
  176.3 17.1 %all-to-all-done.2 = f32[32,66,128]{2,1,0:T(8,128)} async-done(((f32[32,66,128]{2,1,0:T(8,128)}), f32[32,66,128]{2,1,0:T(8,128)}, u32[]{:S(2)}, u32[]{:S(2)}) %all-to-all-start.2) | async-done | bytes 1081376 | tf_op jit(solution)/shard_map/all_to_all | solution.py:142
  193.4 1.4 fusion.189
  196.4 0.8 fusion.198
  200.8 0.9 multiply_reduce_fusion.7
  202.6 0.9 multiply_reduce_fusion.4
  204.3 0.9 multiply_reduce_fusion.5
  206.0 0.9 multiply_reduce_fusion.6
  207.0 0.9 multiply_reduce_fusion.3
  208.9 2.5 fusion.3
  213.0 46.4 %reduce-scatter.2.cloned.1.call-done = f32[4,32,512]{2,1,0:T(8,128)} async-done(((f32[4,32,4096]{2,1,0:T(8,128)}), f32[4,32,512]{2,1,0:T(8,128)}) %reduce-scatter.2.cloned.1.call-update) | async-done | bytes 262160 | tf_op jit(solution)/shard_map/reduce_scatter | solution.py:162
  259.4 1.6 convert_element_type.79
  (207 shorter events, 22.0 us)
Async XLA Ops:
  7.2 201.7 %copy-start = (bf16[256,4096]{1,0:T(8,128)(2,1)S(1)}, bf16[256,4096]{1,0:T(8,128)(2,1)}, u32[]{:S(2)}) copy-start(bf16[256,4096]{1,0:T(8,128)(2,1)} %param.15) | copy-start | bytes 6291460
  7.2 4.5 %copy-start.22 = (bf16[4096]{0:T(1024)(128)(2,1)S(1)}, bf16[4096]{0:T(1024)(128)(2,1)}, u32[]{:S(2)}) copy-start(bf16[4096]{0:T(1024)(128)(2,1)} %param.11) | copy-start | bytes 24580
  7.2 48.4 %all-gather.2.cloned.1.call-start = ((), (), s32[]{:S(2)}) async-start(), calls=%async_computation.4 | async-start | bytes 1179648 | tf_op jit(solution)/shard_map/all_gather | solution.py:33
  11.7 76.0 %collective-permute-start = (bf16[4,512,128]{2,1,0:T(8,128)(2,1)}, bf16[4,512,128]{2,1,0:T(8,128)(2,1)}, u32[]{:S(2)}, u32[]{:S(2)}) collective-permute-start(bf16[4,512,128]{2,1,0:T(8,128)(2,1)} %pad_maximum_fusion.2), channel_id=1, source_target_pairs={{0,8},{8,0},{16,24},{24,16},{32,40},{40,32},{48,56},{56,48},{64,72... | collective-permute-start | bytes 1572872 | tf_op jit(solution)/shard_map/ppermute | solution.py:75
  11.7 48.5 %copy-start.20 = (f32[4096]{0:T(1024)}, f32[4096]{0:T(1024)S(1)}, u32[]{:S(2)}) copy-start(f32[4096]{0:T(1024)S(1)} %convert_element_type.64) | copy-start | bytes 49156
  15.8 4.2 %copy-start.23 = (s32[4]{0:T(128)S(1)}, s32[4]{0:T(128)}, u32[]{:S(2)}) copy-start(s32[4]{0:T(128)} %param.18) | copy-start | bytes 52
  20.0 57.4 %copy-start.46 = (s32[32]{0:T(128)}, s32[32]{0:T(128)S(1)}, u32[]{:S(2)}) copy-start(s32[32]{0:T(128)S(1)} %iota_add_fusion.3) | copy-start | bytes 388
  57.1 3.0 %copy-start.44 = (f32[4,32]{1,0:T(4,128)}, f32[4,32]{1,0:T(4,128)S(1)}, u32[]{:S(2)}) copy-start(f32[4,32]{1,0:T(4,128)S(1)} %add_rsqrt_fusion) | copy-start | bytes 1540
  57.1 3.0 %copy-start.2 = (bf16[256,4096]{1,0:T(8,128)(2,1)S(1)}, bf16[256,4096]{1,0:T(8,128)(2,1)}, u32[]{:S(2)}) copy-start(bf16[256,4096]{1,0:T(8,128)(2,1)} %copy.154) | copy-start | bytes 6291460
  57.1 3.1 %copy-start.4 = (bf16[4,32,4096]{2,1,0:T(8,128)(2,1)S(1)}, bf16[4,32,4096]{2,1,0:T(8,128)(2,1)}, u32[]{:S(2)}) copy-start(bf16[4,32,4096]{2,1,0:T(8,128)(2,1)} %all-gather.2.cloned.1.call-done) | copy-start | bytes 3145732
  60.2 1.0 copy-start.13
  61.4 23.3 %copy-start.8 = (bf16[4,2,4,8,128]{4,3,2,1,0:T(8,128)(2,1)}, bf16[4,2,4,8,128]{4,3,2,1,0:T(8,128)(2,1)S(1)}, u32[]{:S(2)}) copy-start(bf16[4,2,4,8,128]{4,3,2,1,0:T(8,128)(2,1)S(1)} %get-tuple-element.27) | copy-start | bytes 196612
  62.7 40.3 %all-to-all-start = ((bf16[32,128,128]{2,1,0:T(8,128)(2,1)}), bf16[32,128,128]{2,1,0:T(8,128)(2,1)}, u32[]{:S(2)}, u32[]{:S(2)}) async-start(bf16[32,128,128]{2,1,0:T(8,128)(2,1)} %bitcast.9), calls=%async_computation | async-start | bytes 2097152 | tf_op jit(solution)/shard_map/all_to_all | solution.py:96
  72.5 4.2 %copy-start.24 = (s32[4]{0:T(128)S(1)}, s32[4]{0:T(128)}, u32[]{:S(2)}) copy-start(s32[4]{0:T(128)} %param.19) | copy-start | bytes 52
  72.5 12.1 %copy-start.21 = (f32[4096]{0:T(1024)S(1)}, f32[4096]{0:T(1024)}, u32[]{:S(2)}) copy-start(f32[4096]{0:T(1024)} %copy-done.20) | copy-start | bytes 49156
  72.5 12.1 %copy-start.45 = (f32[4,32]{1,0:T(4,128)S(1)}, f32[4,32]{1,0:T(4,128)}, u32[]{:S(2)}) copy-start(f32[4,32]{1,0:T(4,128)} %copy-done.44) | copy-start | bytes 1540
  78.6 36.4 %copy-start.19 = (s32[64]{0:T(128)}, s32[64]{0:T(128)S(1)}, u32[]{:S(2)}) copy-start(s32[64]{0:T(128)S(1)} %get-tuple-element.8) | copy-start | bytes 772
  82.2 22.6 %copy-start.33 = (pred[512]{0:T(512)(128)(4,1)}, pred[512]{0:T(512)(128)(4,1)S(1)}, u32[]{:S(2)}) copy-start(pred[512]{0:T(512)(128)(4,1)S(1)} %get-tuple-element.67) | copy-start | bytes 1540
  82.2 24.4 %copy-start.31 = (pred[512]{0:T(512)(128)(4,1)}, pred[512]{0:T(512)(128)(4,1)S(1)}, u32[]{:S(2)}) copy-start(pred[512]{0:T(512)(128)(4,1)S(1)} %get-tuple-element.69) | copy-start | bytes 1540
  87.1 2.3 copy-start.14
  87.1 17.2 %copy-start.39 = (pred[64]{0:T(512)(128)(4,1)S(1)}, pred[64]{0:T(512)(128)(4,1)}, u32[]{:S(2)}) copy-start(pred[64]{0:T(512)(128)(4,1)} %get-tuple-element.78) | copy-start | bytes 196
  87.2 17.3 %copy-start.37 = (pred[64]{0:T(512)(128)(4,1)S(1)}, pred[64]{0:T(512)(128)(4,1)}, u32[]{:S(2)}) copy-start(pred[64]{0:T(512)(128)(4,1)} %get-tuple-element.7) | copy-start | bytes 196
  87.2 22.9 %copy-start.6 = (bf16[4,32,128]{2,1,0:T(8,128)(2,1)}, bf16[4,32,128]{2,1,0:T(8,128)(2,1)S(1)}, u32[]{:S(2)}) copy-start(bf16[4,32,128]{2,1,0:T(8,128)(2,1)S(1)} %get-tuple-element.33) | copy-start | bytes 98308
  87.3 2.2 collective-permute-start.1
  89.4 20.7 %copy-start.7 = (bf16[4,32,128]{2,1,0:T(8,128)(2,1)}, bf16[4,32,128]{2,1,0:T(8,128)(2,1)S(1)}, u32[]{:S(2)}) copy-start(bf16[4,32,128]{2,1,0:T(8,128)(2,1)S(1)} %get-tuple-element.35) | copy-start | bytes 98308
  104.8 10.2 %copy-start.5 = (f32[1024,64]{0,1:T(8,128)}, f32[1024,64]{0,1:T(8,128)S(1)}, u32[]{:S(2)}) copy-start(f32[1024,64]{0,1:T(8,128)S(1)} %get-tuple-element.99) | copy-start | bytes 786436
  106.6 1.8 copy-start.41
  106.6 2.0 copy-start.36
  108.3 0.7 copy-start.42
  108.3 0.9 copy-start.35
  110.5 1.1 copy-start.11
  110.5 1.1 copy-start.16
  113.3 1.7 copy-start.38
  113.3 1.7 copy-start.40
  115.9 1.1 copy-start.10
  117.0 5.9 %copy-start.25 = (s32[4]{0:T(128)S(1)}, s32[4]{0:T(128)}, u32[]{:S(2)}) copy-start(s32[4]{0:T(128)} %param.19) | copy-start | bytes 52
  119.2 36.7 %all-to-all-start.1 = ((f32[32,66,128]{2,1,0:T(8,128)}), f32[32,66,128]{2,1,0:T(8,128)S(1)}, u32[]{:S(2)}, u32[]{:S(2)}) async-start(f32[32,66,128]{2,1,0:T(8,128)} %pad_maximum_fusion), calls=%async_computation.1 | async-start | bytes 2359296 | tf_op jit(solution)/shard_map/all_to_all | solution.py:142
  134.1 5.0 %copy-start.34 = (pred[512]{0:T(512)(128)(4,1)S(1)}, pred[512]{0:T(512)(128)(4,1)}, u32[]{:S(2)}) copy-start(pred[512]{0:T(512)(128)(4,1)} %copy-done.33) | copy-start | bytes 1540
  139.1 2.6 copy-start.1
  139.1 2.6 copy-start.12
  139.1 2.6 copy-start.17
  139.1 2.6 copy-start.32
  141.7 0.9 copy-start.18
  155.9 37.4 %all-to-all-start.2 = ((f32[32,66,128]{2,1,0:T(8,128)}), f32[32,66,128]{2,1,0:T(8,128)}, u32[]{:S(2)}, u32[]{:S(2)}) async-start(f32[32,66,128]{2,1,0:T(8,128)} %pad_maximum_fusion.1), calls=%async_computation.2 | async-start | bytes 2359296 | tf_op jit(solution)/shard_map/all_to_all | solution.py:142
  160.6 98.8 %reduce-scatter.2.cloned.1.call-start = ((), (), s32[]{:S(2)}) async-start(), calls=%async_computation.5 | async-start | bytes 2359296 | tf_op jit(solution)/shard_map/reduce_scatter | solution.py:162
  161.7 0.7 copy-start.3
  163.3 13.0 %copy-start.26 = (f32[32]{0:T(128)}, f32[32]{0:T(128)S(1)}, u32[]{:S(2)}) copy-start(f32[32]{0:T(128)S(1)} %get-tuple-element.42) | copy-start | bytes 388
  167.1 0.5 copy-start.28
  168.5 7.8 %copy-start.29 = (f32[32]{0:T(128)}, f32[32]{0:T(128)S(1)}, u32[]{:S(2)}) copy-start(f32[32]{0:T(128)S(1)} %get-tuple-element.48) | copy-start | bytes 388
  169.6 0.5 copy-start.27
  197.2 0.7 copy-start.30
  211.4 0.8 copy-start.9
  211.4 0.9 copy-start.15
  211.4 0.9 copy-start.43
Sparse Core Ops, SparseCore 0:
  9.8 45.7 all-gather.1
  211.5 47.8 reduce-scatter.1

commit v4 on v3

--- a/solution.py
+++ b/solution.py
@@ -137,6 +137,8 @@
         )
     block_rows = local_rows + 1
     attended_list = []
+    mixed_list = []
+    tensor_count = lax.axis_size("tensor")
     for first in range(0, requests, 2):
         sent = jnp.concatenate(payload_list[first : first + 2], 1)
         arrived = lax.all_to_all(sent, "seq", 0, 0, tiled=True)
@@ -151,17 +153,26 @@
                 numer_sum = jnp.sum(received[:, :local_rows] * factor[..., None], 0)
                 head_parts.append(numer_sum / mass_sum[:, None])
             attended_list.append(jnp.concatenate(head_parts, -1))
-    attended = (
-        jnp.where(live_rows[..., None], jnp.stack(attended_list), 0.0)
-        .astype(jnp.bfloat16)
-        .reshape(requests * local_rows, heads_width)
-    )
-    partial_out = jnp.dot(attended, w_out, preferred_element_type=jnp.float32).reshape(
-        requests, local_rows, -1
-    )
-    mixed = lax.psum_scatter(partial_out, "tensor", scatter_dimension=2, tiled=True).astype(
-        jnp.bfloat16
-    )
+        attended = (
+            jnp.where(
+                live_rows[first : first + 2, :, None],
+                jnp.stack(attended_list[first : first + 2]),
+                0.0,
+            )
+            .astype(jnp.bfloat16)
+            .reshape(-1, heads_width)
+        )
+        partial_out = jnp.einsum(
+            "rk,kcn->crn",
+            attended,
+            w_out.reshape(heads_width, tensor_count, -1),
+            preferred_element_type=jnp.float32,
+        )
+        partial_sums = lax.all_to_all(partial_out, "tensor", 0, 0, tiled=True)
+        mixed_list.append(
+            jnp.sum(partial_sums, 0).astype(jnp.bfloat16).reshape(-1, local_rows, partial_out.shape[2])
+        )
+    mixed = jnp.concatenate(mixed_list, 0)
     return (mixed, new_keys, new_values)
 
 

time: 271 us -> 246 us (0.908)
  waiting for transfers between devices: 124 us -> 114 us
  other arithmetic: 45.5 us -> 35.6 us
  local copies, waits for them, and re-layouts: 40.5 us -> 31.4 us
  starting transfers between devices: 18.7 us -> 25.7 us
    reduce_scatter x1 -> x0, waiting for transfers between devices: 46.4 us -> none  [body(): lax.psum_scatter(partial_out, 'tensor', scatter_dimension=2, tiled=True)]
    all_to_all x0 -> x2, waiting for transfers between devices: none -> 24.9 us  [body(): partial_sums = lax.all_to_all(partial_out, 'tensor', 0, 0, tiled=True)]
    all_to_all x2, waiting for transfers between devices: 29.3 us -> 38.4 us  [body(): arrived = lax.all_to_all(sent, 'seq', 0, 0, tiled=True)]
    all_to_all x0 -> x2, starting transfers between devices: none -> 7.11 us  [body(): partial_sums = lax.all_to_all(partial_out, 'tensor', 0, 0, tiled=True)]
    reduce_sum x8, other arithmetic: 6.68 us -> 2.87 us  [body(): numer_sum = jnp.sum(received[:, :local_rows] * factor[..., None], 0)]
    dot_general x3, local copies, waits for them, and re-layouts: 12.4 us -> 8.79 us  [project(): jnp.dot(flat_rows, weight, preferred_element_type=jnp.float32)]
    reduce_sum x8, other arithmetic: 5.19 us -> 2.23 us  [body(): mass_sum = jnp.sum(block_stats[..., 1] * factor, 0)]
  transfers between devices with their start and end apart: 7 -> 8, of which waited for: 5 -> 6; matrix products, arithmetic and copies ran while one was open for 27% -> 26% of each run, Pallas kernels for 0% -> 0%
where the time goes in v4:
time: 246 us; the launch traced here: 245 us
  waiting for transfers between devices  114 us (46%)
  other arithmetic  35.6 us (14%)
  local copies, waits for them, and re-layouts  31.4 us (13%)
  starting transfers between devices  25.7 us (10%)
  matrix products  22.3 us (9%)
  between operations  15.4 us (6%)
    all_to_all x2, waiting for transfers between devices, body(): arrived = lax.all_to_all(sent, 'seq', 0, 0, tiled=True)  38.4 us
    all_gather x1, waiting for transfers between devices, body(): lax.all_gather(tokens, 'tensor', axis=2, tiled=True).astype(jnp.float32)  35.2 us
    all_to_all x2, waiting for transfers between devices, body(): partial_sums = lax.all_to_all(partial_out, 'tensor', 0, 0, tiled=True)  24.9 us
    all_to_all x1, waiting for transfers between devices, body(): query_got = lax.all_to_all(query_sent, 'seq', 0, 0, tiled=True)  15.2 us
    all_to_all x1, starting transfers between devices, body(): query_got = lax.all_to_all(query_sent, 'seq', 0, 0, tiled=True)  9.76 us
    dot_general x3, local copies, waits for them, and re-layouts, project(): jnp.dot(flat_rows, weight, preferred_element_type=jnp.float32)  8.79 us
    all_to_all x2, starting transfers between devices, body(): arrived = lax.all_to_all(sent, 'seq', 0, 0, tiled=True)  8.4 us
    all_to_all x2, starting transfers between devices, body(): partial_sums = lax.all_to_all(partial_out, 'tensor', 0, 0, tiled=True)  7.11 us
  transfers between devices with their start and end apart: 8, of which 6 were waited for; matrix products, arithmetic and copies ran while one was open for 26% of the time, Pallas kernels for 0%

profile of v4, /device:TPU:32, one launch (start us, length us, event | category | flops | bytes accessed | tf_op | source)
XLA Modules:
  0.0 244.7 jit_solution(6118520458351824971)
XLA Ops:
  7.2 0.7 all-gather.2.cloned.1.call-update
  7.9 1.1 constant_dynamic-slice_fusion.7
  9.0 1.8 constant_dynamic-slice_fusion.1
  10.8 0.9 pad_maximum_fusion.2
  11.7 2.9 %copy.161 = bf16[256,4096]{1,0:T(8,128)(2,1)} copy(bf16[256,4096]{0,1:T(8,128)(2,1)S(1)} %bitcast.212) | data formatting | bytes 4194304 | tf_op jit(solution)/shard_map/dot_general | solution.py:41
  14.6 2.9 %copy.162 = bf16[256,4096]{1,0:T(8,128)(2,1)S(1)} copy(bf16[256,4096]{0,1:T(8,128)(2,1)} %bitcast.213) | data formatting | bytes 4194304 | tf_op jit(solution)/shard_map/dot_general | solution.py:41
  19.7 0.7 pad_maximum_fusion.7
  20.4 35.2 %all-gather.2.cloned.1.call-done = bf16[4,32,4096]{2,1,0:T(8,128)(2,1)} async-done(((bf16[4,32,512]{2,1,0:T(8,128)(2,1)}), bf16[4,32,4096]{2,1,0:T(8,128)(2,1)}) %all-gather.2.cloned.1.call-update) | async-done | bytes 1048592 | tf_op jit(solution)/shard_map/all_gather | solution.py:33
  55.6 1.5 fusion
  57.1 2.8 %fusion.136 = f32[4,32,2,128]{3,1,2,0:T(8,128)S(1)} fusion(bf16[2,128,4096,1]{2,1,0,3:T(8,128)(2,1)} %bitcast.217, bf16[4,32,4096]{2,1,0:T(8,128)(2,1)} %all-gather.2.cloned.1.call-done, f32[4096]{0:T(1024)S(1)} %convert_element_type.96, f32[4,32]{1,0:T(4,128)S(1)} %add_rsqrt_fusion), kind=kOutput, calls=%fused_computation.193 | convolution fusion | flops 270532608 | bytes 3293696 | tf_op jit(solution)/shard_map/dot_general | solution.py:41
  60.1 0.8 fusion.134
  61.3 1.2 tile.11
  62.6 9.8 %all-to-all-start = ((bf16[32,128,128]{2,1,0:T(8,128)(2,1)}), bf16[32,128,128]{2,1,0:T(8,128)(2,1)S(1)}, u32[]{:S(2)}, u32[]{:S(2)}) async-start(bf16[32,128,128]{2,1,0:T(8,128)(2,1)} %bitcast.9), calls=%async_computation | async-start | bytes 2097152 | tf_op jit(solution)/shard_map/all_to_all | solution.py:96
  72.4 2.9 %copy.163 = bf16[256,4096]{1,0:T(8,128)(2,1)} copy(bf16[256,4096]{0,1:T(8,128)(2,1)S(1)} %bitcast.214) | data formatting | bytes 4194304 | tf_op jit(solution)/shard_map/dot_general | solution.py:41
  75.9 0.7 broadcast_compare_fusion.6
  77.3 2.6 %broadcast_compare_fusion.1 = (pred[512]{0:T(512)(128)(4,1)S(1)}, pred[512]{0:T(512)(128)(4,1)S(1)}, pred[512]{0:T(512)(128)(4,1)S(1)}, pred[512]{0:T(512)(128)(4,1)S(1)}) fusion(s32[]{:T(128)} %bitcast.60, s32[256]{0:T(256)S(1)} %copy-done.58, s32[256]{0:T(256)S(1)} %copy-done.57, s32[]{:T(128)} %bitcast.27, s32[]{:T(128)} %bitcast.71, s32[]{:T(128)} %bitcast), kind=kLoop, calls=%fused_computation.256 | loop fusion | flops 2560 | bytes 4112 | tf_op jit(solution)/shard_map/lt | solution.py:104
  80.6 1.9 broadcast_compare_fusion.7
  82.5 2.8 %fusion.31 = bf16[4,2,4,8,128]{4,3,2,1,0:T(8,128)(2,1)S(1)} fusion(bf16[2,128,4096,1]{2,1,0,3:T(8,128)(2,1)} %bitcast.215, bf16[4,32,4096]{2,1,0:T(8,128)(2,1)} %all-gather.2.cloned.1.call-done, f32[4096]{0:T(1024)S(1)} %convert_element_type.96, f32[4,32]{1,0:T(4,128)S(1)} %copy-done.56), kind=kOutput, calls=%fused_computation.48 | convolution fusion | flops 270565376 | bytes 3228160 | tf_op jit(solution)/shard_map/dot_general | solution.py:41
  85.8 1.8 fusion.197
  87.6 15.2 %all-to-all-done = bf16[32,128,128]{2,1,0:T(8,128)(2,1)S(1)} async-done(((bf16[32,128,128]{2,1,0:T(8,128)(2,1)}), bf16[32,128,128]{2,1,0:T(8,128)(2,1)S(1)}, u32[]{:S(2)}, u32[]{:S(2)}) %all-to-all-start) | async-done | bytes 1048608 | tf_op jit(solution)/shard_map/all_to_all | solution.py:96
  103.4 1.8 fusion.9
  107.8 1.1 fusion.13
  108.9 0.9 convolution_add_fusion.2
  109.7 1.6 convolution_add_fusion.3
  111.4 0.9 fusion.65
  113.5 2.2 pad_maximum_fusion
  115.7 3.7 %all-to-all-start.1 = ((f32[32,66,128]{2,1,0:T(8,128)}), f32[32,66,128]{2,1,0:T(8,128)S(1)}, u32[]{:S(2)}, u32[]{:S(2)}) async-start(f32[32,66,128]{2,1,0:T(8,128)} %pad_maximum_fusion), calls=%async_computation.1 | async-start | bytes 2359296 | tf_op jit(solution)/shard_map/all_to_all | solution.py:144
  120.0 3.3 %fusion.17 = (f32[1024]{0:T(1024)S(1)}, f32[1024]{0:T(1024)}) fusion(f32[1024,512]{0,1:T(8,128)} %get-tuple-element.99, f32[1024]{0:T(1024)S(1)} %max.60, pred[512]{0:T(512)(128)(4,1)S(1)} %copy-done.48, f32[1024]{0:T(1024)S(1)} %max.62, f32[1024,512]{0,1:T(8,128)S(1)} %get-tuple-element.87, pred[512]{0:T(512)(128)(4,1)S(1)} %copy-done.45), kind=kLoop, calls=%fused_computation.27 | loop fusion | flops 5240832 | bytes 4211712 | tf_op jit(solution)/shard_map/reduce_sum | solution.py:123
  123.3 1.0 copy.139
  124.3 1.9 reshape.479
  126.3 1.3 pad.15
  127.6 0.7 add.213
  128.3 1.0 copy.140
  129.3 1.9 reshape.482
  131.2 0.7 pad.16
  131.9 1.3 fusion.75
  133.2 1.1 fusion.73
  134.3 2.5 %convolution_add_fusion.1 = f32[1024,128]{1,0:T(8,128)S(1)} fusion(f32[1024,128]{1,0:T(8,128)S(1)} %fusion.75, f32[1024,512]{0,1:T(8,128)} %get-tuple-element.99, f32[1024]{0:T(1024)S(1)} %max.60, pred[512]{0:T(512)(128)(4,1)S(1)} %copy-done.49, bf16[4,256,128]{2,1,0:T(8,128)(2,1)} %get-tuple-element.21, bf16[4,256,128]{2,1,0:T(8,128)(2,1)} %get-tuple-element.23), kind=kOutput, calls=%fused_computation.34 | convolution fusion | flops 137232384 | bytes 3674624 | tf_op jit(solution)/shard_map/dot_general | solution.py:124
  136.9 0.8 convolution_add_fusion
  137.7 1.1 pad_maximum_fusion.1
  138.8 13.6 %all-to-all-done.1 = f32[32,66,128]{2,1,0:T(8,128)S(1)} async-done(((f32[32,66,128]{2,1,0:T(8,128)}), f32[32,66,128]{2,1,0:T(8,128)S(1)}, u32[]{:S(2)}, u32[]{:S(2)}) %all-to-all-start.1) | async-done | bytes 1081376 | tf_op jit(solution)/shard_map/all_to_all | solution.py:144
  152.4 4.7 %all-to-all-start.3 = ((f32[32,66,128]{2,1,0:T(8,128)}), f32[32,66,128]{2,1,0:T(8,128)}, u32[]{:S(2)}, u32[]{:S(2)}) async-start(f32[32,66,128]{2,1,0:T(8,128)} %pad_maximum_fusion.1), calls=%async_computation.3 | async-start | bytes 2359296 | tf_op jit(solution)/shard_map/all_to_all | solution.py:144
  157.3 0.8 fusion.200
  158.6 0.8 fusion.203
  160.0 0.8 fusion.202
  161.1 0.8 fusion.201
  162.5 0.7 fusion.60
  163.2 0.7 fusion.57
  164.0 0.7 fusion.58
  164.9 24.8 %all-to-all-done.3 = f32[32,66,128]{2,1,0:T(8,128)} async-done(((f32[32,66,128]{2,1,0:T(8,128)}), f32[32,66,128]{2,1,0:T(8,128)}, u32[]{:S(2)}, u32[]{:S(2)}) %all-to-all-start.3) | async-done | bytes 1081376 | tf_op jit(solution)/shard_map/all_to_all | solution.py:144
  189.6 1.4 fusion.195
  191.9 0.8 copy.143
  192.7 0.8 fusion.204
  193.5 0.7 subtract_exponential_fusion.3
  194.2 0.8 copy.144
  197.1 0.9 multiply_reduce_fusion.3
  199.0 0.7 fusion.132
  199.9 1.5 fusion.24
  201.3 3.6 %all-to-all-start.4 = ((f32[8,64,512]{2,1,0:T(8,128)}), f32[8,64,512]{2,1,0:T(8,128)S(1)}, u32[]{:S(2)}, u32[]{:S(2)}) async-start(f32[8,64,512]{2,1,0:T(8,128)} %fusion.24), calls=%async_computation.4 | async-start | bytes 2097152 | tf_op jit(solution)/shard_map/all_to_all | solution.py:171
  206.2 1.5 fusion.21
  207.8 11.7 %all-to-all-done.4 = f32[8,64,512]{2,1,0:T(8,128)S(1)} async-done(((f32[8,64,512]{2,1,0:T(8,128)}), f32[8,64,512]{2,1,0:T(8,128)S(1)}, u32[]{:S(2)}, u32[]{:S(2)}) %all-to-all-start.4) | async-done | bytes 1048608 | tf_op jit(solution)/shard_map/all_to_all | solution.py:171
  219.5 3.6 %all-to-all-start.2 = ((f32[8,64,512]{2,1,0:T(8,128)}), f32[8,64,512]{2,1,0:T(8,128)S(1)}, u32[]{:S(2)}, u32[]{:S(2)}) async-start(f32[8,64,512]{2,1,0:T(8,128)} %fusion.21), calls=%async_computation.2 | async-start | bytes 2097152 | tf_op jit(solution)/shard_map/all_to_all | solution.py:171
  223.1 0.7 broadcast_select_fusion
  223.9 13.2 %all-to-all-done.2 = f32[8,64,512]{2,1,0:T(8,128)S(1)} async-done(((f32[8,64,512]{2,1,0:T(8,128)}), f32[8,64,512]{2,1,0:T(8,128)S(1)}, u32[]{:S(2)}, u32[]{:S(2)}) %all-to-all-start.2) | async-done | bytes 1048608 | tf_op jit(solution)/shard_map/all_to_all | solution.py:171
  (240 shorter events, 17.7 us)
Async XLA Ops:
  7.2 4.5 %copy-start.31 = (bf16[4096]{0:T(1024)(128)(2,1)S(1)}, bf16[4096]{0:T(1024)(128)(2,1)}, u32[]{:S(2)}) copy-start(bf16[4096]{0:T(1024)(128)(2,1)} %param.11) | copy-start | bytes 24580
  7.2 4.5 %copy-start.1 = (bf16[4096,256]{1,0:T(8,128)(2,1)S(1)}, bf16[4096,256]{1,0:T(8,128)(2,1)}, u32[]{:S(2)}) copy-start(bf16[4096,256]{1,0:T(8,128)(2,1)} %param.12) | copy-start | bytes 6291460
  7.2 48.4 %all-gather.2.cloned.1.call-start = ((), (), s32[]{:S(2)}) async-start(), calls=%async_computation.5 | async-start | bytes 1179648 | tf_op jit(solution)/shard_map/all_gather | solution.py:33
  11.7 74.1 %collective-permute-start = (bf16[4,512,128]{2,1,0:T(8,128)(2,1)}, bf16[4,512,128]{2,1,0:T(8,128)(2,1)}, u32[]{:S(2)}, u32[]{:S(2)}) collective-permute-start(bf16[4,512,128]{2,1,0:T(8,128)(2,1)} %pad_maximum_fusion.2), channel_id=1, source_target_pairs={{0,8},{8,0},{16,24},{24,16},{32,40},{40,32},{48,56},{56,48},{64,72... | collective-permute-start | bytes 1572872 | tf_op jit(solution)/shard_map/ppermute | solution.py:75
  14.6 4.6 %copy-start.32 = (s32[4]{0:T(128)S(1)}, s32[4]{0:T(128)}, u32[]{:S(2)}) copy-start(s32[4]{0:T(128)} %param.18) | copy-start | bytes 52
  57.1 3.0 %copy-start.55 = (f32[4,32]{1,0:T(4,128)}, f32[4,32]{1,0:T(4,128)S(1)}, u32[]{:S(2)}) copy-start(f32[4,32]{1,0:T(4,128)S(1)} %add_rsqrt_fusion) | copy-start | bytes 1540
  57.1 3.0 %copy-start.3 = (bf16[4,32,4096]{2,1,0:T(8,128)(2,1)S(1)}, bf16[4,32,4096]{2,1,0:T(8,128)(2,1)}, u32[]{:S(2)}) copy-start(bf16[4,32,4096]{2,1,0:T(8,128)(2,1)} %all-gather.2.cloned.1.call-done) | copy-start | bytes 3145732
  60.1 1.0 copy-start.13
  61.1 11.2 %copy-start.2 = (bf16[4096,256]{1,0:T(8,128)(2,1)S(1)}, bf16[4096,256]{1,0:T(8,128)(2,1)}, u32[]{:S(2)}) copy-start(bf16[4096,256]{1,0:T(8,128)(2,1)} %param.14) | copy-start | bytes 6291460
  61.3 21.2 %copy-start.9 = (bf16[4,2,4,8,128]{4,3,2,1,0:T(8,128)(2,1)}, bf16[4,2,4,8,128]{4,3,2,1,0:T(8,128)(2,1)S(1)}, u32[]{:S(2)}) copy-start(bf16[4,2,4,8,128]{4,3,2,1,0:T(8,128)(2,1)S(1)} %get-tuple-element.27) | copy-start | bytes 196612
  62.6 40.2 %all-to-all-start = ((bf16[32,128,128]{2,1,0:T(8,128)(2,1)}), bf16[32,128,128]{2,1,0:T(8,128)(2,1)S(1)}, u32[]{:S(2)}, u32[]{:S(2)}) async-start(bf16[32,128,128]{2,1,0:T(8,128)(2,1)} %bitcast.9), calls=%async_computation | async-start | bytes 2097152 | tf_op jit(solution)/shard_map/all_to_all | solution.py:96
  72.3 3.0 %copy-start.34 = (s32[4]{0:T(128)S(1)}, s32[4]{0:T(128)}, u32[]{:S(2)}) copy-start(s32[4]{0:T(128)} %param.19) | copy-start | bytes 52
  72.4 3.6 %copy-start.59 = (s32[32]{0:T(128)S(1)}, s32[32]{0:T(128)}, u32[]{:S(2)}) copy-start(s32[32]{0:T(128)} %iota_add_fusion.3) | copy-start | bytes 388
  72.4 4.3 %copy-start.33 = (s32[4]{0:T(128)S(1)}, s32[4]{0:T(128)}, u32[]{:S(2)}) copy-start(s32[4]{0:T(128)} %param.18) | copy-start | bytes 52
  72.4 5.0 %copy-start.57 = (s32[256]{0:T(256)S(1)}, s32[256]{0:T(256)}, u32[]{:S(2)}) copy-start(s32[256]{0:T(256)} %iota_add_fusion.1) | copy-start | bytes 3076
  72.4 5.0 %copy-start.58 = (s32[256]{0:T(256)S(1)}, s32[256]{0:T(256)}, u32[]{:S(2)}) copy-start(s32[256]{0:T(256)} %iota_add_fusion) | copy-start | bytes 3076
  72.4 10.1 %copy-start.56 = (f32[4,32]{1,0:T(4,128)S(1)}, f32[4,32]{1,0:T(4,128)}, u32[]{:S(2)}) copy-start(f32[4,32]{1,0:T(4,128)} %copy-done.55) | copy-start | bytes 1540
  76.7 34.7 %copy-start.30 = (s32[64]{0:T(128)}, s32[64]{0:T(128)S(1)}, u32[]{:S(2)}) copy-start(s32[64]{0:T(128)S(1)} %get-tuple-element.8) | copy-start | bytes 772
  76.7 34.7 %copy-start.52 = (pred[64]{0:T(512)(128)(4,1)}, pred[64]{0:T(512)(128)(4,1)S(1)}, u32[]{:S(2)}) copy-start(pred[64]{0:T(512)(128)(4,1)S(1)} %get-tuple-element.7) | copy-start | bytes 196
  79.9 23.4 %copy-start.47 = (pred[512]{0:T(512)(128)(4,1)}, pred[512]{0:T(512)(128)(4,1)S(1)}, u32[]{:S(2)}) copy-start(pred[512]{0:T(512)(128)(4,1)S(1)} %get-tuple-element.67) | copy-start | bytes 1540
  80.0 25.2 %copy-start.44 = (pred[512]{0:T(512)(128)(4,1)}, pred[512]{0:T(512)(128)(4,1)S(1)}, u32[]{:S(2)}) copy-start(pred[512]{0:T(512)(128)(4,1)S(1)} %get-tuple-element.69) | copy-start | bytes 1540
  82.4 29.0 %copy-start.53 = (pred[64]{0:T(512)(128)(4,1)}, pred[64]{0:T(512)(128)(4,1)S(1)}, u32[]{:S(2)}) copy-start(pred[64]{0:T(512)(128)(4,1)S(1)} %get-tuple-element.80) | copy-start | bytes 196
  85.3 2.3 copy-start.14
  85.3 22.0 %copy-start.7 = (bf16[4,32,128]{2,1,0:T(8,128)(2,1)}, bf16[4,32,128]{2,1,0:T(8,128)(2,1)S(1)}, u32[]{:S(2)}) copy-start(bf16[4,32,128]{2,1,0:T(8,128)(2,1)S(1)} %get-tuple-element.33) | copy-start | bytes 98308
  85.4 2.2 collective-permute-start.1
  87.6 19.8 %copy-start.8 = (bf16[4,32,128]{2,1,0:T(8,128)(2,1)}, bf16[4,32,128]{2,1,0:T(8,128)(2,1)S(1)}, u32[]{:S(2)}) copy-start(bf16[4,32,128]{2,1,0:T(8,128)(2,1)S(1)} %get-tuple-element.35) | copy-start | bytes 98308
  103.1 8.3 %copy-start.4 = (f32[1024,64]{0,1:T(8,128)}, f32[1024,64]{0,1:T(8,128)S(1)}, u32[]{:S(2)}) copy-start(f32[1024,64]{0,1:T(8,128)S(1)} %get-tuple-element.89) | copy-start | bytes 786436
  103.3 8.1 %copy-start.6 = (f32[1024,64]{0,1:T(8,128)}, f32[1024,64]{0,1:T(8,128)S(1)}, u32[]{:S(2)}) copy-start(f32[1024,64]{0,1:T(8,128)S(1)} %get-tuple-element.101) | copy-start | bytes 786436
  107.7 1.1 copy-start.11
  107.7 1.1 copy-start.16
  113.4 6.0 %copy-start.50 = (pred[4,32]{1,0:T(4,128)(4,1)S(1)}, pred[4,32]{1,0:T(4,128)(4,1)}, u32[]{:S(2)}) copy-start(pred[4,32]{1,0:T(4,128)(4,1)} %broadcast_compare_fusion.4) | copy-start | bytes 388
  113.5 6.6 %copy-start.45 = (pred[512]{0:T(512)(128)(4,1)S(1)}, pred[512]{0:T(512)(128)(4,1)}, u32[]{:S(2)}) copy-start(pred[512]{0:T(512)(128)(4,1)} %copy-done.44) | copy-start | bytes 1540
  113.5 6.6 %copy-start.48 = (pred[512]{0:T(512)(128)(4,1)S(1)}, pred[512]{0:T(512)(128)(4,1)}, u32[]{:S(2)}) copy-start(pred[512]{0:T(512)(128)(4,1)} %copy-done.47) | copy-start | bytes 1540
  115.7 36.7 %all-to-all-start.1 = ((f32[32,66,128]{2,1,0:T(8,128)}), f32[32,66,128]{2,1,0:T(8,128)S(1)}, u32[]{:S(2)}, u32[]{:S(2)}) async-start(f32[32,66,128]{2,1,0:T(8,128)} %pad_maximum_fusion), calls=%async_computation.1 | async-start | bytes 2359296 | tf_op jit(solution)/shard_map/all_to_all | solution.py:144
  123.3 9.9 %copy-start.5 = (f32[1024,64]{0,1:T(8,128)S(1)}, f32[1024,64]{0,1:T(8,128)}, u32[]{:S(2)}) copy-start(f32[1024,64]{0,1:T(8,128)} %copy-done.4) | copy-start | bytes 786436
  129.3 5.0 %copy-start.49 = (pred[512]{0:T(512)(128)(4,1)S(1)}, pred[512]{0:T(512)(128)(4,1)}, u32[]{:S(2)}) copy-start(pred[512]{0:T(512)(128)(4,1)} %copy-done.47) | copy-start | bytes 1540
  134.3 2.5 %copy-start.12 = (bf16[4,256,128]{2,1,0:T(8,128)(2,1)S(1)}, bf16[4,256,128]{2,1,0:T(8,128)(2,1)}, u32[]{:S(2)}) copy-start(bf16[4,256,128]{2,1,0:T(8,128)(2,1)} %get-tuple-element.21) | copy-start | bytes 786436
  134.3 2.5 %copy-start.17 = (bf16[4,256,128]{2,1,0:T(8,128)(2,1)S(1)}, bf16[4,256,128]{2,1,0:T(8,128)(2,1)}, u32[]{:S(2)}) copy-start(bf16[4,256,128]{2,1,0:T(8,128)(2,1)} %get-tuple-element.23) | copy-start | bytes 786436
  134.3 2.5 %copy-start.46 = (pred[512]{0:T(512)(128)(4,1)S(1)}, pred[512]{0:T(512)(128)(4,1)}, u32[]{:S(2)}) copy-start(pred[512]{0:T(512)(128)(4,1)} %copy-done.44) | copy-start | bytes 1540
  152.4 37.2 %all-to-all-start.3 = ((f32[32,66,128]{2,1,0:T(8,128)}), f32[32,66,128]{2,1,0:T(8,128)}, u32[]{:S(2)}, u32[]{:S(2)}) async-start(f32[32,66,128]{2,1,0:T(8,128)} %pad_maximum_fusion.1), calls=%async_computation.3 | async-start | bytes 2359296 | tf_op jit(solution)/shard_map/all_to_all | solution.py:144
  158.2 6.6 %copy-start.35 = (f32[32]{0:T(128)}, f32[32]{0:T(128)S(1)}, u32[]{:S(2)}) copy-start(f32[32]{0:T(128)S(1)} %get-tuple-element.42) | copy-start | bytes 388
  160.9 3.8 %copy-start.39 = (f32[32]{0:T(128)}, f32[32]{0:T(128)S(1)}, u32[]{:S(2)}) copy-start(f32[32]{0:T(128)S(1)} %get-tuple-element.48) | copy-start | bytes 388
  164.8 34.9 %copy-start = (bf16[256,4096]{1,0:T(8,128)(2,1)S(1)}, bf16[256,4096]{1,0:T(8,128)(2,1)}, u32[]{:S(2)}) copy-start(bf16[256,4096]{1,0:T(8,128)(2,1)} %param.15) | copy-start | bytes 6291460
  199.7 5.2 %copy-start.22 = (f32[16,32,1]{0,2,1:T(1,128)S(1)}, f32[16,32,1]{0,2,1:T(1,128)}, u32[]{:S(2)}) copy-start(f32[16,32,1]{0,2,1:T(1,128)} %get-tuple-element.41) | copy-start | bytes 6148
  199.7 5.2 %copy-start.23 = (f32[16,32,1]{0,2,1:T(1,128)S(1)}, f32[16,32,1]{0,2,1:T(1,128)}, u32[]{:S(2)}) copy-start(f32[16,32,1]{0,2,1:T(1,128)} %get-tuple-element.43) | copy-start | bytes 6148
  199.7 5.2 %copy-start.36 = (f32[32]{0:T(128)S(1)}, f32[32]{0:T(128)}, u32[]{:S(2)}) copy-start(f32[32]{0:T(128)} %copy-done.35) | copy-start | bytes 388
  199.7 5.4 %copy-start.21 = (f32[32,128]{1,0:T(8,128)S(1)}, f32[32,128]{1,0:T(8,128)}, u32[]{:S(2)}) copy-start(f32[32,128]{1,0:T(8,128)} %fusion.60) | copy-start | bytes 49156
  199.8 5.5 %copy-start.24 = (f32[16,32,1]{0,2,1:T(1,128)S(1)}, f32[16,32,1]{0,2,1:T(1,128)}, u32[]{:S(2)}) copy-start(f32[16,32,1]{0,2,1:T(1,128)} %get-tuple-element.50) | copy-start | bytes 6148
  199.8 5.5 %copy-start.25 = (f32[16,32,1]{0,2,1:T(1,128)S(1)}, f32[16,32,1]{0,2,1:T(1,128)}, u32[]{:S(2)}) copy-start(f32[16,32,1]{0,2,1:T(1,128)} %get-tuple-element.52) | copy-start | bytes 6148
  199.8 5.5 %copy-start.38 = (f32[32]{0:T(128)S(1)}, f32[32]{0:T(128)}, u32[]{:S(2)}) copy-start(f32[32]{0:T(128)} %copy-done.37) | copy-start | bytes 388
  199.8 5.6 %copy-start.20 = (f32[32,128]{1,0:T(8,128)S(1)}, f32[32,128]{1,0:T(8,128)}, u32[]{:S(2)}) copy-start(f32[32,128]{1,0:T(8,128)} %fusion.57) | copy-start | bytes 49156
  199.8 5.7 %copy-start.26 = (f32[16,32,1]{0,2,1:T(1,128)S(1)}, f32[16,32,1]{0,2,1:T(1,128)}, u32[]{:S(2)}) copy-start(f32[16,32,1]{0,2,1:T(1,128)} %get-tuple-element.47) | copy-start | bytes 6148
  199.8 5.7 %copy-start.27 = (f32[16,32,1]{0,2,1:T(1,128)S(1)}, f32[16,32,1]{0,2,1:T(1,128)}, u32[]{:S(2)}) copy-start(f32[16,32,1]{0,2,1:T(1,128)} %get-tuple-element.49) | copy-start | bytes 6148
  199.8 5.7 %copy-start.40 = (f32[32]{0:T(128)S(1)}, f32[32]{0:T(128)}, u32[]{:S(2)}) copy-start(f32[32]{0:T(128)} %copy-done.39) | copy-start | bytes 388
  199.8 5.9 %copy-start.19 = (f32[32,128]{1,0:T(8,128)S(1)}, f32[32,128]{1,0:T(8,128)}, u32[]{:S(2)}) copy-start(f32[32,128]{1,0:T(8,128)} %fusion.58) | copy-start | bytes 49156
  199.8 6.0 %copy-start.28 = (f32[16,32,1]{0,2,1:T(1,128)S(1)}, f32[16,32,1]{0,2,1:T(1,128)}, u32[]{:S(2)}) copy-start(f32[16,32,1]{0,2,1:T(1,128)} %get-tuple-element.44) | copy-start | bytes 6148
  199.8 6.0 %copy-start.29 = (f32[16,32,1]{0,2,1:T(1,128)S(1)}, f32[16,32,1]{0,2,1:T(1,128)}, u32[]{:S(2)}) copy-start(f32[16,32,1]{0,2,1:T(1,128)} %get-tuple-element.46) | copy-start | bytes 6148
  199.9 6.0 %copy-start.42 = (f32[32]{0:T(128)S(1)}, f32[32]{0:T(128)}, u32[]{:S(2)}) copy-start(f32[32]{0:T(128)} %copy-done.41) | copy-start | bytes 388
  199.9 6.3 %copy-start.54 = (pred[2,32]{1,0:T(4,128)(4,1)S(1)}, pred[2,32]{1,0:T(4,128)(4,1)}, u32[]{:S(2)}) copy-start(pred[2,32]{1,0:T(4,128)(4,1)} %get-tuple-element.73) | copy-start | bytes 196
  201.3 18.1 %all-to-all-start.4 = ((f32[8,64,512]{2,1,0:T(8,128)}), f32[8,64,512]{2,1,0:T(8,128)S(1)}, u32[]{:S(2)}, u32[]{:S(2)}) async-start(f32[8,64,512]{2,1,0:T(8,128)} %fusion.24), calls=%async_computation.4 | async-start | bytes 2097152 | tf_op jit(solution)/shard_map/all_to_all | solution.py:171
  206.2 16.8 %copy-start.10 = (bf16[4,2,4,8,128]{4,3,2,1,0:T(8,128)(2,1)S(1)}, bf16[4,2,4,8,128]{4,3,2,1,0:T(8,128)(2,1)}, u32[]{:S(2)}) copy-start(bf16[4,2,4,8,128]{4,3,2,1,0:T(8,128)(2,1)} %copy-done.9) | copy-start | bytes 196612
  206.2 16.8 %copy-start.15 = (bf16[4,2,4,8,128]{4,3,2,1,0:T(8,128)(2,1)S(1)}, bf16[4,2,4,8,128]{4,3,2,1,0:T(8,128)(2,1)}, u32[]{:S(2)}) copy-start(bf16[4,2,4,8,128]{4,3,2,1,0:T(8,128)(2,1)} %copy-done.14) | copy-start | bytes 196612
  206.2 16.8 %copy-start.51 = (pred[4,32]{1,0:T(4,128)(4,1)S(1)}, pred[4,32]{1,0:T(4,128)(4,1)}, u32[]{:S(2)}) copy-start(pred[4,32]{1,0:T(4,128)(4,1)} %broadcast_compare_fusion.4) | copy-start | bytes 388
  219.5 17.6 %all-to-all-start.2 = ((f32[8,64,512]{2,1,0:T(8,128)}), f32[8,64,512]{2,1,0:T(8,128)S(1)}, u32[]{:S(2)}, u32[]{:S(2)}) async-start(f32[8,64,512]{2,1,0:T(8,128)} %fusion.21), calls=%async_computation.2 | async-start | bytes 2097152 | tf_op jit(solution)/shard_map/all_to_all | solution.py:171
  (4 other events, 2.6 us)
Sparse Core Ops, SparseCore 0:
  9.8 45.7 all-gather.1

commit v5 on v4

--- a/solution.py
+++ b/solution.py
@@ -30,7 +30,13 @@
 ):
     seq_index = lax.axis_index("seq")
     requests, local_rows, width_part = tokens.shape
-    gathered = lax.all_gather(tokens, "tensor", axis=2, tiled=True).astype(jnp.float32)
+    token_copies = jnp.broadcast_to(tokens[None], (lax.axis_size("tensor"),) + tokens.shape)
+    gathered = (
+        lax.all_to_all(token_copies, "tensor", 0, 0, tiled=True)
+        .transpose(1, 2, 0, 3)
+        .reshape(requests, local_rows, -1)
+        .astype(jnp.float32)
+    )
     inverse_rms = lax.rsqrt(jnp.mean(gathered * gathered, -1, keepdims=True) + 1e-05)
     normed = (gathered * inverse_rms * norm_gain.astype(jnp.float32)).astype(jnp.bfloat16)
     flat_rows = normed.reshape(requests * local_rows, -1)

time: 246 us -> 213 us (0.87)
  waiting for transfers between devices: 114 us -> 86 us
  between operations: 15.4 us -> 1.99 us
  starting transfers between devices: 25.7 us -> 32.2 us
  local copies, waits for them, and re-layouts: 31.4 us -> 34.5 us
    all_gather x1 -> x0, waiting for transfers between devices: 35.2 us -> none  [body(): lax.all_gather(tokens, 'tensor', axis=2, tiled=True).astype(jnp.float32)]
    all_to_all x0 -> x1, waiting for transfers between devices: none -> 7.61 us  [body(): lax.all_to_all(token_copies, 'tensor', 0, 0, tiled=True)]
    all_to_all x0 -> x1, starting transfers between devices: none -> 5.4 us  [body(): lax.all_to_all(token_copies, 'tensor', 0, 0, tiled=True)]
  transfers between devices with their start and end apart: 8 -> 8, of which waited for: 6 -> 6; matrix products, arithmetic and copies ran while one was open for 26% -> 29% of each run, Pallas kernels for 0% -> 0%
where the time goes in v5:
time: 213 us; the launch traced here: 212 us
  waiting for transfers between devices  86 us (40%)
  other arithmetic  34.7 us (16%)
  local copies, waits for them, and re-layouts  34.5 us (16%)
  starting transfers between devices  32.2 us (15%)
  matrix products  22.3 us (10%)
    all_to_all x2, waiting for transfers between devices, body(): arrived = lax.all_to_all(sent, 'seq', 0, 0, tiled=True)  38.4 us
    all_to_all x2, waiting for transfers between devices, body(): partial_sums = lax.all_to_all(partial_out, 'tensor', 0, 0, tiled=True)  24.9 us
    all_to_all x1, waiting for transfers between devices, body(): query_got = lax.all_to_all(query_sent, 'seq', 0, 0, tiled=True)  15.1 us
    all_to_all x1, starting transfers between devices, body(): query_got = lax.all_to_all(query_sent, 'seq', 0, 0, tiled=True)  10.9 us
    dot_general x3, local copies, waits for them, and re-layouts, project(): jnp.dot(flat_rows, weight, preferred_element_type=jnp.float32)  8.79 us
    all_to_all x2, starting transfers between devices, body(): arrived = lax.all_to_all(sent, 'seq', 0, 0, tiled=True)  8.4 us
    all_to_all x1, waiting for transfers between devices, body(): lax.all_to_all(token_copies, 'tensor', 0, 0, tiled=True)  7.61 us
    all_to_all x2, starting transfers between devices, body(): partial_sums = lax.all_to_all(partial_out, 'tensor', 0, 0, tiled=True)  7.11 us
  transfers between devices with their start and end apart: 8, of which 6 were waited for; matrix products, arithmetic and copies ran while one was open for 29% of the time, Pallas kernels for 0%

profile of v5, /device:TPU:32, one launch (start us, length us, event | category | flops | bytes accessed | tf_op | source)
XLA Modules:
  0.0 211.7 jit_solution(14003837090215644706)
XLA Ops:
  0.7 1.1 constant_dynamic-slice_fusion.7
  1.8 1.8 constant_dynamic-slice_fusion.1
  3.6 0.9 pad_maximum_fusion.2
  4.4 1.1 broadcast_in_dim.164
  5.5 5.4 %all-to-all-start = ((bf16[8,4,32,512]{3,2,1,0:T(8,128)(2,1)}), bf16[8,4,32,512]{3,2,1,0:T(8,128)(2,1)S(1)}, u32[]{:S(2)}, u32[]{:S(2)}) async-start(bf16[8,4,32,512]{3,2,1,0:T(8,128)(2,1)} %broadcast_in_dim.164), calls=%async_computation | async-start | bytes 2097152 | tf_op jit(solution)/shard_map/all_to_all | solution.py:35
  12.6 2.9 %copy.213 = bf16[256,4096]{1,0:T(8,128)(2,1)} copy(bf16[256,4096]{0,1:T(8,128)(2,1)S(1)} %bitcast.216) | data formatting | bytes 4194304 | tf_op jit(solution)/shard_map/dot_general | solution.py:47
  15.6 2.9 %copy.214 = bf16[256,4096]{1,0:T(8,128)(2,1)S(1)} copy(bf16[256,4096]{0,1:T(8,128)(2,1)} %bitcast.217) | data formatting | bytes 4194304 | tf_op jit(solution)/shard_map/dot_general | solution.py:47
  19.0 0.7 pad_maximum_fusion.7
  19.7 7.6 %all-to-all-done = bf16[8,4,32,512]{3,2,1,0:T(8,128)(2,1)S(1)} async-done(((bf16[8,4,32,512]{3,2,1,0:T(8,128)(2,1)}), bf16[8,4,32,512]{3,2,1,0:T(8,128)(2,1)S(1)}, u32[]{:S(2)}, u32[]{:S(2)}) %all-to-all-start) | async-done | bytes 1048608 | tf_op jit(solution)/shard_map/all_to_all | solution.py:35
  28.6 1.3 reshape.537
  29.9 2.8 %fusion.36 = f32[4,32,2,128]{3,1,2,0:T(8,128)S(1)} fusion(bf16[2,128,4096,1]{2,1,0,3:T(8,128)(2,1)} %bitcast.221, bf16[4,32,4096,1]{2,1,0,3:T(8,128)(2,1)} %reshape.537), kind=kOutput, calls=%fused_computation.53 | convolution fusion | flops 268435456 | bytes 3276800 | tf_op jit(solution)/shard_map/dot_general | solution.py:47
  32.9 0.8 fusion.34
  34.1 1.2 tile.11
  35.3 10.9 %all-to-all-start.1 = ((bf16[32,128,128]{2,1,0:T(8,128)(2,1)}), bf16[32,128,128]{2,1,0:T(8,128)(2,1)S(1)}, u32[]{:S(2)}, u32[]{:S(2)}) async-start(bf16[32,128,128]{2,1,0:T(8,128)(2,1)} %bitcast.9), calls=%async_computation.1 | async-start | bytes 2097152 | tf_op jit(solution)/shard_map/all_to_all | solution.py:102
  46.3 2.9 %copy.215 = bf16[256,4096]{1,0:T(8,128)(2,1)} copy(bf16[256,4096]{0,1:T(8,128)(2,1)S(1)} %bitcast.218) | data formatting | bytes 4194304 | tf_op jit(solution)/shard_map/dot_general | solution.py:47
  49.9 0.7 broadcast_compare_fusion.6
  51.3 2.6 %broadcast_compare_fusion.1 = (pred[512]{0:T(512)(128)(4,1)S(1)}, pred[512]{0:T(512)(128)(4,1)S(1)}, pred[512]{0:T(512)(128)(4,1)S(1)}, pred[512]{0:T(512)(128)(4,1)S(1)}) fusion(s32[]{:T(128)} %bitcast.59, s32[256]{0:T(256)S(1)} %copy-done.56, s32[256]{0:T(256)S(1)} %copy-done.55, s32[]{:T(128)} %bitcast.26, s32[]{:T(128)} %bitcast.70, s32[]{:T(128)} %bitcast), kind=kLoop, calls=%fused_computation.259 | loop fusion | flops 2560 | bytes 4112 | tf_op jit(solution)/shard_map/lt | solution.py:110
  54.5 2.0 broadcast_compare_fusion.7
  56.5 2.8 %fusion.31 = bf16[4,2,4,8,128]{4,3,2,1,0:T(8,128)(2,1)S(1)} fusion(bf16[2,128,4096,1]{2,1,0,3:T(8,128)(2,1)} %bitcast.219, bf16[4,32,4096,1]{2,1,0,3:T(8,128)(2,1)} %reshape.537), kind=kOutput, calls=%fused_computation.48 | convolution fusion | flops 268468224 | bytes 3211264 | tf_op jit(solution)/shard_map/dot_general | solution.py:47
  59.8 1.8 fusion.197
  61.6 15.1 %all-to-all-done.1 = bf16[32,128,128]{2,1,0:T(8,128)(2,1)S(1)} async-done(((bf16[32,128,128]{2,1,0:T(8,128)(2,1)}), bf16[32,128,128]{2,1,0:T(8,128)(2,1)S(1)}, u32[]{:S(2)}, u32[]{:S(2)}) %all-to-all-start.1) | async-done | bytes 1048608 | tf_op jit(solution)/shard_map/all_to_all | solution.py:102
  77.2 1.8 fusion.9
  81.6 1.1 fusion.13
  82.7 0.9 convolution_add_fusion.2
  83.6 1.6 convolution_add_fusion.3
  85.3 0.9 fusion.70
  87.4 2.2 %pad_maximum_fusion = f32[32,66,128]{2,1,0:T(8,128)} fusion(f32[32,1,128]{2,1,0:T(1,128)S(1)} %bitcast.266, f32[32,32,128]{2,1,0:T(8,128)S(1)} %bitcast.230, f32[32,1,128]{2,1,0:T(1,128)S(1)} %bitcast.265, f32[32,32,128]{2,1,0:T(8,128)} %bitcast.231), kind=kLoop, calls=%fused_computation.37 | loop fusion | flops 811008 | bytes 2162688 | tf_op jit(solution)/shard_map/concatenate | solution.py:149
  89.6 3.7 %all-to-all-start.2 = ((f32[32,66,128]{2,1,0:T(8,128)}), f32[32,66,128]{2,1,0:T(8,128)S(1)}, u32[]{:S(2)}, u32[]{:S(2)}) async-start(f32[32,66,128]{2,1,0:T(8,128)} %pad_maximum_fusion), calls=%async_computation.2 | async-start | bytes 2359296 | tf_op jit(solution)/shard_map/all_to_all | solution.py:150
  93.9 3.3 %fusion.17 = (f32[1024]{0:T(1024)S(1)}, f32[1024]{0:T(1024)}) fusion(f32[1024,512]{0,1:T(8,128)} %get-tuple-element.99, f32[1024]{0:T(1024)S(1)} %max.60, pred[512]{0:T(512)(128)(4,1)S(1)} %copy-done.48, f32[1024]{0:T(1024)S(1)} %max.62, f32[1024,512]{0,1:T(8,128)S(1)} %get-tuple-element.87, pred[512]{0:T(512)(128)(4,1)S(1)} %get-tuple-element.69), kind=kLoop, calls=%fused_computation.27 | loop fusion | flops 5240832 | bytes 4211712 | tf_op jit(solution)/shard_map/reduce_sum | solution.py:129
  97.2 1.0 copy.191
  98.2 1.9 reshape.532
  100.1 1.3 pad.15
  101.4 0.7 add.213
  102.1 1.0 copy.192
  103.2 1.9 reshape.535
  105.1 0.7 pad.16
  105.8 1.3 fusion.80
  107.1 1.1 fusion.78
  108.2 2.5 %convolution_add_fusion.1 = f32[1024,128]{1,0:T(8,128)S(1)} fusion(f32[1024,128]{1,0:T(8,128)S(1)} %fusion.80, f32[1024,512]{0,1:T(8,128)} %get-tuple-element.99, f32[1024]{0:T(1024)S(1)} %max.60, pred[512]{0:T(512)(128)(4,1)S(1)} %copy-done.49, bf16[4,256,128]{2,1,0:T(8,128)(2,1)} %get-tuple-element.21, bf16[4,256,128]{2,1,0:T(8,128)(2,1)} %get-tuple-element.23), kind=kOutput, calls=%fused_computation.34 | convolution fusion | flops 137232384 | bytes 3674624 | tf_op jit(solution)/shard_map/dot_general | solution.py:130
  110.7 0.8 convolution_add_fusion
  111.6 1.1 pad_maximum_fusion.1
  112.7 13.6 %all-to-all-done.2 = f32[32,66,128]{2,1,0:T(8,128)S(1)} async-done(((f32[32,66,128]{2,1,0:T(8,128)}), f32[32,66,128]{2,1,0:T(8,128)S(1)}, u32[]{:S(2)}, u32[]{:S(2)}) %all-to-all-start.2) | async-done | bytes 1081376 | tf_op jit(solution)/shard_map/all_to_all | solution.py:150
  126.3 4.7 %all-to-all-start.4 = ((f32[32,66,128]{2,1,0:T(8,128)}), f32[32,66,128]{2,1,0:T(8,128)}, u32[]{:S(2)}, u32[]{:S(2)}) async-start(f32[32,66,128]{2,1,0:T(8,128)} %pad_maximum_fusion.1), calls=%async_computation.4 | async-start | bytes 2359296 | tf_op jit(solution)/shard_map/all_to_all | solution.py:150
  131.2 0.8 fusion.200
  132.5 0.8 fusion.203
  133.9 0.8 fusion.202
  134.9 0.8 fusion.201
  136.4 0.7 fusion.65
  137.1 0.7 fusion.62
  137.9 0.7 fusion.63
  138.7 24.8 %all-to-all-done.4 = f32[32,66,128]{2,1,0:T(8,128)} async-done(((f32[32,66,128]{2,1,0:T(8,128)}), f32[32,66,128]{2,1,0:T(8,128)}, u32[]{:S(2)}, u32[]{:S(2)}) %all-to-all-start.4) | async-done | bytes 1081376 | tf_op jit(solution)/shard_map/all_to_all | solution.py:150
  163.5 1.4 fusion.195
  165.8 0.8 copy.195
  166.6 0.8 fusion.204
  167.4 0.7 subtract_exponential_fusion.3
  168.1 0.8 copy.196
  171.0 0.9 multiply_reduce_fusion.3
  173.7 1.5 fusion.24
  175.2 3.6 %all-to-all-start.5 = ((f32[8,64,512]{2,1,0:T(8,128)}), f32[8,64,512]{2,1,0:T(8,128)S(1)}, u32[]{:S(2)}, u32[]{:S(2)}) async-start(f32[8,64,512]{2,1,0:T(8,128)} %fusion.24), calls=%async_computation.5 | async-start | bytes 2097152 | tf_op jit(solution)/shard_map/all_to_all | solution.py:177
  180.1 1.5 fusion.21
  181.6 11.7 %all-to-all-done.5 = f32[8,64,512]{2,1,0:T(8,128)S(1)} async-done(((f32[8,64,512]{2,1,0:T(8,128)}), f32[8,64,512]{2,1,0:T(8,128)S(1)}, u32[]{:S(2)}, u32[]{:S(2)}) %all-to-all-start.5) | async-done | bytes 1048608 | tf_op jit(solution)/shard_map/all_to_all | solution.py:177
  193.3 3.6 %all-to-all-start.3 = ((f32[8,64,512]{2,1,0:T(8,128)}), f32[8,64,512]{2,1,0:T(8,128)S(1)}, u32[]{:S(2)}, u32[]{:S(2)}) async-start(f32[8,64,512]{2,1,0:T(8,128)} %fusion.21), calls=%async_computation.3 | async-start | bytes 2097152 | tf_op jit(solution)/shard_map/all_to_all | solution.py:177
  196.9 0.7 broadcast_select_fusion
  197.7 13.2 %all-to-all-done.3 = f32[8,64,512]{2,1,0:T(8,128)S(1)} async-done(((f32[8,64,512]{2,1,0:T(8,128)}), f32[8,64,512]{2,1,0:T(8,128)S(1)}, u32[]{:S(2)}, u32[]{:S(2)}) %all-to-all-start.3) | async-done | bytes 1048608 | tf_op jit(solution)/shard_map/all_to_all | solution.py:177
  (239 shorter events, 19.7 us)
Async XLA Ops:
  0.6 3.8 %copy-start.18 = (bf16[4,32,512]{2,1,0:T(8,128)(2,1)S(1)}, bf16[4,32,512]{2,1,0:T(8,128)(2,1)}, u32[]{:S(2)}) copy-start(bf16[4,32,512]{2,1,0:T(8,128)(2,1)} %param.10) | copy-start | bytes 393220
  3.6 9.1 %copy-start.32 = (bf16[4096]{0:T(1024)(128)(2,1)S(1)}, bf16[4096]{0:T(1024)(128)(2,1)}, u32[]{:S(2)}) copy-start(bf16[4096]{0:T(1024)(128)(2,1)} %param.11) | copy-start | bytes 24580
  3.6 9.1 %copy-start.1 = (bf16[4096,256]{1,0:T(8,128)(2,1)S(1)}, bf16[4096,256]{1,0:T(8,128)(2,1)}, u32[]{:S(2)}) copy-start(bf16[4096,256]{1,0:T(8,128)(2,1)} %param.12) | copy-start | bytes 6291460
  4.4 55.4 %collective-permute-start = (bf16[4,512,128]{2,1,0:T(8,128)(2,1)}, bf16[4,512,128]{2,1,0:T(8,128)(2,1)}, u32[]{:S(2)}, u32[]{:S(2)}) collective-permute-start(bf16[4,512,128]{2,1,0:T(8,128)(2,1)} %pad_maximum_fusion.2), channel_id=1, source_target_pairs={{0,8},{8,0},{16,24},{24,16},{32,40},{40,32},{48,56},{56,48},{64,72... | collective-permute-start | bytes 1572872 | tf_op jit(solution)/shard_map/ppermute | solution.py:81
  5.5 21.8 %all-to-all-start = ((bf16[8,4,32,512]{3,2,1,0:T(8,128)(2,1)}), bf16[8,4,32,512]{3,2,1,0:T(8,128)(2,1)S(1)}, u32[]{:S(2)}, u32[]{:S(2)}) async-start(bf16[8,4,32,512]{3,2,1,0:T(8,128)(2,1)} %broadcast_in_dim.164), calls=%async_computation | async-start | bytes 2097152 | tf_op jit(solution)/shard_map/all_to_all | solution.py:35
  15.6 2.9 %copy-start.33 = (s32[4]{0:T(128)S(1)}, s32[4]{0:T(128)}, u32[]{:S(2)}) copy-start(s32[4]{0:T(128)} %param.18) | copy-start | bytes 52
  29.9 2.9 %copy-start.3 = (bf16[4,32,4096,1]{2,1,0,3:T(8,128)(2,1)S(1)}, bf16[4,32,4096,1]{2,1,0,3:T(8,128)(2,1)}, u32[]{:S(2)}) copy-start(bf16[4,32,4096,1]{2,1,0,3:T(8,128)(2,1)} %reshape.537) | copy-start | bytes 3145732
  32.9 1.0 copy-start.13
  33.8 12.4 %copy-start.2 = (bf16[4096,256]{1,0:T(8,128)(2,1)S(1)}, bf16[4096,256]{1,0:T(8,128)(2,1)}, u32[]{:S(2)}) copy-start(bf16[4096,256]{1,0:T(8,128)(2,1)} %param.14) | copy-start | bytes 6291460
  34.0 22.5 %copy-start.9 = (bf16[4,2,4,8,128]{4,3,2,1,0:T(8,128)(2,1)}, bf16[4,2,4,8,128]{4,3,2,1,0:T(8,128)(2,1)S(1)}, u32[]{:S(2)}) copy-start(bf16[4,2,4,8,128]{4,3,2,1,0:T(8,128)(2,1)S(1)} %get-tuple-element.27) | copy-start | bytes 196612
  35.3 41.4 %all-to-all-start.1 = ((bf16[32,128,128]{2,1,0:T(8,128)(2,1)}), bf16[32,128,128]{2,1,0:T(8,128)(2,1)S(1)}, u32[]{:S(2)}, u32[]{:S(2)}) async-start(bf16[32,128,128]{2,1,0:T(8,128)(2,1)} %bitcast.9), calls=%async_computation.1 | async-start | bytes 2097152 | tf_op jit(solution)/shard_map/all_to_all | solution.py:102
  46.2 3.0 %copy-start.35 = (s32[4]{0:T(128)S(1)}, s32[4]{0:T(128)}, u32[]{:S(2)}) copy-start(s32[4]{0:T(128)} %param.19) | copy-start | bytes 52
  46.2 3.7 %copy-start.57 = (s32[32]{0:T(128)S(1)}, s32[32]{0:T(128)}, u32[]{:S(2)}) copy-start(s32[32]{0:T(128)} %iota_add_fusion.3) | copy-start | bytes 388
  46.2 4.4 %copy-start.34 = (s32[4]{0:T(128)S(1)}, s32[4]{0:T(128)}, u32[]{:S(2)}) copy-start(s32[4]{0:T(128)} %param.18) | copy-start | bytes 52
  46.3 5.0 %copy-start.55 = (s32[256]{0:T(256)S(1)}, s32[256]{0:T(256)}, u32[]{:S(2)}) copy-start(s32[256]{0:T(256)} %iota_add_fusion.1) | copy-start | bytes 3076
  46.3 5.0 %copy-start.56 = (s32[256]{0:T(256)S(1)}, s32[256]{0:T(256)}, u32[]{:S(2)}) copy-start(s32[256]{0:T(256)} %iota_add_fusion) | copy-start | bytes 3076
  50.6 34.7 %copy-start.31 = (s32[64]{0:T(128)}, s32[64]{0:T(128)S(1)}, u32[]{:S(2)}) copy-start(s32[64]{0:T(128)S(1)} %get-tuple-element.8) | copy-start | bytes 772
  50.6 34.7 %copy-start.52 = (pred[64]{0:T(512)(128)(4,1)}, pred[64]{0:T(512)(128)(4,1)S(1)}, u32[]{:S(2)}) copy-start(pred[64]{0:T(512)(128)(4,1)S(1)} %get-tuple-element.7) | copy-start | bytes 196
  53.9 23.3 %copy-start.47 = (pred[512]{0:T(512)(128)(4,1)}, pred[512]{0:T(512)(128)(4,1)S(1)}, u32[]{:S(2)}) copy-start(pred[512]{0:T(512)(128)(4,1)S(1)} %get-tuple-element.67) | copy-start | bytes 1540
  53.9 40.0 %copy-start.45 = (pred[512]{0:T(512)(128)(4,1)}, pred[512]{0:T(512)(128)(4,1)S(1)}, u32[]{:S(2)}) copy-start(pred[512]{0:T(512)(128)(4,1)S(1)} %get-tuple-element.69) | copy-start | bytes 1540
  56.5 28.8 %copy-start.53 = (pred[64]{0:T(512)(128)(4,1)}, pred[64]{0:T(512)(128)(4,1)S(1)}, u32[]{:S(2)}) copy-start(pred[64]{0:T(512)(128)(4,1)S(1)} %get-tuple-element.80) | copy-start | bytes 196
  59.3 2.3 %copy-start.14 = (bf16[4,2,4,8,128]{4,3,2,1,0:T(8,128)(2,1)}, bf16[4,2,4,8,128]{4,3,2,1,0:T(8,128)(2,1)S(1)}, u32[]{:S(2)}) copy-start(bf16[4,2,4,8,128]{4,3,2,1,0:T(8,128)(2,1)S(1)} %fusion.31) | copy-start | bytes 196612
  59.4 21.9 %copy-start.7 = (bf16[4,32,128]{2,1,0:T(8,128)(2,1)}, bf16[4,32,128]{2,1,0:T(8,128)(2,1)S(1)}, u32[]{:S(2)}) copy-start(bf16[4,32,128]{2,1,0:T(8,128)(2,1)S(1)} %get-tuple-element.33) | copy-start | bytes 98308
  59.4 2.2 %collective-permute-start.1 = (bf16[4,64,128]{2,1,0:T(8,128)(2,1)S(1)}, bf16[4,64,128]{2,1,0:T(8,128)(2,1)S(1)}, u32[]{:S(2)}, u32[]{:S(2)}) collective-permute-start(bf16[4,64,128]{2,1,0:T(8,128)(2,1)S(1)} %pad_maximum_fusion.8), channel_id=1, source_target_pairs={{0,8},{8,0},{16,24},{24,16},{32,40},{40,32},{48,56},{56,48},{64,72... | collective-permute-start | bytes 196616 | tf_op jit(solution)/shard_map/ppermute | solution.py:84
  61.6 19.7 %copy-start.8 = (bf16[4,32,128]{2,1,0:T(8,128)(2,1)}, bf16[4,32,128]{2,1,0:T(8,128)(2,1)S(1)}, u32[]{:S(2)}) copy-start(bf16[4,32,128]{2,1,0:T(8,128)(2,1)S(1)} %get-tuple-element.35) | copy-start | bytes 98308
  77.0 8.3 %copy-start.4 = (f32[1024,64]{0,1:T(8,128)}, f32[1024,64]{0,1:T(8,128)S(1)}, u32[]{:S(2)}) copy-start(f32[1024,64]{0,1:T(8,128)S(1)} %get-tuple-element.89) | copy-start | bytes 786436
  77.2 8.1 %copy-start.6 = (f32[1024,64]{0,1:T(8,128)}, f32[1024,64]{0,1:T(8,128)S(1)}, u32[]{:S(2)}) copy-start(f32[1024,64]{0,1:T(8,128)S(1)} %get-tuple-element.101) | copy-start | bytes 786436
  81.6 1.1 copy-start.11
  81.6 1.1 copy-start.16
  87.3 6.0 %copy-start.50 = (pred[4,32]{1,0:T(4,128)(4,1)S(1)}, pred[4,32]{1,0:T(4,128)(4,1)}, u32[]{:S(2)}) copy-start(pred[4,32]{1,0:T(4,128)(4,1)} %broadcast_compare_fusion.4) | copy-start | bytes 388
  87.3 6.6 %copy-start.48 = (pred[512]{0:T(512)(128)(4,1)S(1)}, pred[512]{0:T(512)(128)(4,1)}, u32[]{:S(2)}) copy-start(pred[512]{0:T(512)(128)(4,1)} %copy-done.47) | copy-start | bytes 1540
  89.6 36.7 %all-to-all-start.2 = ((f32[32,66,128]{2,1,0:T(8,128)}), f32[32,66,128]{2,1,0:T(8,128)S(1)}, u32[]{:S(2)}, u32[]{:S(2)}) async-start(f32[32,66,128]{2,1,0:T(8,128)} %pad_maximum_fusion), calls=%async_computation.2 | async-start | bytes 2359296 | tf_op jit(solution)/shard_map/all_to_all | solution.py:150
  97.2 9.9 %copy-start.5 = (f32[1024,64]{0,1:T(8,128)S(1)}, f32[1024,64]{0,1:T(8,128)}, u32[]{:S(2)}) copy-start(f32[1024,64]{0,1:T(8,128)} %copy-done.4) | copy-start | bytes 786436
  103.2 5.0 %copy-start.49 = (pred[512]{0:T(512)(128)(4,1)S(1)}, pred[512]{0:T(512)(128)(4,1)}, u32[]{:S(2)}) copy-start(pred[512]{0:T(512)(128)(4,1)} %copy-done.47) | copy-start | bytes 1540
  108.2 2.5 %copy-start.12 = (bf16[4,256,128]{2,1,0:T(8,128)(2,1)S(1)}, bf16[4,256,128]{2,1,0:T(8,128)(2,1)}, u32[]{:S(2)}) copy-start(bf16[4,256,128]{2,1,0:T(8,128)(2,1)} %get-tuple-element.21) | copy-start | bytes 786436
  108.2 2.5 %copy-start.17 = (bf16[4,256,128]{2,1,0:T(8,128)(2,1)S(1)}, bf16[4,256,128]{2,1,0:T(8,128)(2,1)}, u32[]{:S(2)}) copy-start(bf16[4,256,128]{2,1,0:T(8,128)(2,1)} %get-tuple-element.23) | copy-start | bytes 786436
  108.2 2.5 %copy-start.46 = (pred[512]{0:T(512)(128)(4,1)S(1)}, pred[512]{0:T(512)(128)(4,1)}, u32[]{:S(2)}) copy-start(pred[512]{0:T(512)(128)(4,1)} %copy-done.45) | copy-start | bytes 1540
  110.7 0.9 copy-start.19
  126.3 37.2 %all-to-all-start.4 = ((f32[32,66,128]{2,1,0:T(8,128)}), f32[32,66,128]{2,1,0:T(8,128)}, u32[]{:S(2)}, u32[]{:S(2)}) async-start(f32[32,66,128]{2,1,0:T(8,128)} %pad_maximum_fusion.1), calls=%async_computation.4 | async-start | bytes 2359296 | tf_op jit(solution)/shard_map/all_to_all | solution.py:150
  132.0 6.6 %copy-start.36 = (f32[32]{0:T(128)}, f32[32]{0:T(128)S(1)}, u32[]{:S(2)}) copy-start(f32[32]{0:T(128)S(1)} %get-tuple-element.42) | copy-start | bytes 388
  134.7 3.9 %copy-start.40 = (f32[32]{0:T(128)}, f32[32]{0:T(128)S(1)}, u32[]{:S(2)}) copy-start(f32[32]{0:T(128)S(1)} %get-tuple-element.48) | copy-start | bytes 388
  138.7 34.8 %copy-start = (bf16[256,4096]{1,0:T(8,128)(2,1)S(1)}, bf16[256,4096]{1,0:T(8,128)(2,1)}, u32[]{:S(2)}) copy-start(bf16[256,4096]{1,0:T(8,128)(2,1)} %param.15) | copy-start | bytes 6291460
  167.4 0.7 copy-start.44
  173.5 5.2 %copy-start.23 = (f32[16,32,1]{0,2,1:T(1,128)S(1)}, f32[16,32,1]{0,2,1:T(1,128)}, u32[]{:S(2)}) copy-start(f32[16,32,1]{0,2,1:T(1,128)} %get-tuple-element.41) | copy-start | bytes 6148
  173.5 5.2 %copy-start.24 = (f32[16,32,1]{0,2,1:T(1,128)S(1)}, f32[16,32,1]{0,2,1:T(1,128)}, u32[]{:S(2)}) copy-start(f32[16,32,1]{0,2,1:T(1,128)} %get-tuple-element.43) | copy-start | bytes 6148
  173.6 5.2 %copy-start.37 = (f32[32]{0:T(128)S(1)}, f32[32]{0:T(128)}, u32[]{:S(2)}) copy-start(f32[32]{0:T(128)} %copy-done.36) | copy-start | bytes 388
  173.6 5.4 %copy-start.22 = (f32[32,128]{1,0:T(8,128)S(1)}, f32[32,128]{1,0:T(8,128)}, u32[]{:S(2)}) copy-start(f32[32,128]{1,0:T(8,128)} %fusion.65) | copy-start | bytes 49156
  173.6 5.5 %copy-start.25 = (f32[16,32,1]{0,2,1:T(1,128)S(1)}, f32[16,32,1]{0,2,1:T(1,128)}, u32[]{:S(2)}) copy-start(f32[16,32,1]{0,2,1:T(1,128)} %get-tuple-element.50) | copy-start | bytes 6148
  173.6 5.5 %copy-start.26 = (f32[16,32,1]{0,2,1:T(1,128)S(1)}, f32[16,32,1]{0,2,1:T(1,128)}, u32[]{:S(2)}) copy-start(f32[16,32,1]{0,2,1:T(1,128)} %get-tuple-element.52) | copy-start | bytes 6148
  173.6 5.5 %copy-start.39 = (f32[32]{0:T(128)S(1)}, f32[32]{0:T(128)}, u32[]{:S(2)}) copy-start(f32[32]{0:T(128)} %copy-done.38) | copy-start | bytes 388
  173.6 5.6 %copy-start.21 = (f32[32,128]{1,0:T(8,128)S(1)}, f32[32,128]{1,0:T(8,128)}, u32[]{:S(2)}) copy-start(f32[32,128]{1,0:T(8,128)} %fusion.62) | copy-start | bytes 49156
  173.6 5.7 %copy-start.27 = (f32[16,32,1]{0,2,1:T(1,128)S(1)}, f32[16,32,1]{0,2,1:T(1,128)}, u32[]{:S(2)}) copy-start(f32[16,32,1]{0,2,1:T(1,128)} %get-tuple-element.47) | copy-start | bytes 6148
  173.6 5.7 %copy-start.28 = (f32[16,32,1]{0,2,1:T(1,128)S(1)}, f32[16,32,1]{0,2,1:T(1,128)}, u32[]{:S(2)}) copy-start(f32[16,32,1]{0,2,1:T(1,128)} %get-tuple-element.49) | copy-start | bytes 6148
  173.6 5.7 %copy-start.41 = (f32[32]{0:T(128)S(1)}, f32[32]{0:T(128)}, u32[]{:S(2)}) copy-start(f32[32]{0:T(128)} %copy-done.40) | copy-start | bytes 388
  173.6 5.9 %copy-start.20 = (f32[32,128]{1,0:T(8,128)S(1)}, f32[32,128]{1,0:T(8,128)}, u32[]{:S(2)}) copy-start(f32[32,128]{1,0:T(8,128)} %fusion.63) | copy-start | bytes 49156
  173.7 6.0 %copy-start.29 = (f32[16,32,1]{0,2,1:T(1,128)S(1)}, f32[16,32,1]{0,2,1:T(1,128)}, u32[]{:S(2)}) copy-start(f32[16,32,1]{0,2,1:T(1,128)} %get-tuple-element.44) | copy-start | bytes 6148
  173.7 6.0 %copy-start.30 = (f32[16,32,1]{0,2,1:T(1,128)S(1)}, f32[16,32,1]{0,2,1:T(1,128)}, u32[]{:S(2)}) copy-start(f32[16,32,1]{0,2,1:T(1,128)} %get-tuple-element.46) | copy-start | bytes 6148
  173.7 6.0 %copy-start.43 = (f32[32]{0:T(128)S(1)}, f32[32]{0:T(128)}, u32[]{:S(2)}) copy-start(f32[32]{0:T(128)} %copy-done.42) | copy-start | bytes 388
  173.7 6.3 %copy-start.54 = (pred[2,32]{1,0:T(4,128)(4,1)S(1)}, pred[2,32]{1,0:T(4,128)(4,1)}, u32[]{:S(2)}) copy-start(pred[2,32]{1,0:T(4,128)(4,1)} %get-tuple-element.73) | copy-start | bytes 196
  175.2 18.1 %all-to-all-start.5 = ((f32[8,64,512]{2,1,0:T(8,128)}), f32[8,64,512]{2,1,0:T(8,128)S(1)}, u32[]{:S(2)}, u32[]{:S(2)}) async-start(f32[8,64,512]{2,1,0:T(8,128)} %fusion.24), calls=%async_computation.5 | async-start | bytes 2097152 | tf_op jit(solution)/shard_map/all_to_all | solution.py:177
  180.0 16.8 %copy-start.10 = (bf16[4,2,4,8,128]{4,3,2,1,0:T(8,128)(2,1)S(1)}, bf16[4,2,4,8,128]{4,3,2,1,0:T(8,128)(2,1)}, u32[]{:S(2)}) copy-start(bf16[4,2,4,8,128]{4,3,2,1,0:T(8,128)(2,1)} %copy-done.9) | copy-start | bytes 196612
  180.1 16.8 %copy-start.15 = (bf16[4,2,4,8,128]{4,3,2,1,0:T(8,128)(2,1)S(1)}, bf16[4,2,4,8,128]{4,3,2,1,0:T(8,128)(2,1)}, u32[]{:S(2)}) copy-start(bf16[4,2,4,8,128]{4,3,2,1,0:T(8,128)(2,1)} %copy-done.14) | copy-start | bytes 196612
  180.1 16.8 %copy-start.51 = (pred[4,32]{1,0:T(4,128)(4,1)S(1)}, pred[4,32]{1,0:T(4,128)(4,1)}, u32[]{:S(2)}) copy-start(pred[4,32]{1,0:T(4,128)(4,1)} %broadcast_compare_fusion.4) | copy-start | bytes 388
  193.3 17.6 %all-to-all-start.3 = ((f32[8,64,512]{2,1,0:T(8,128)}), f32[8,64,512]{2,1,0:T(8,128)S(1)}, u32[]{:S(2)}, u32[]{:S(2)}) async-start(f32[8,64,512]{2,1,0:T(8,128)} %fusion.21), calls=%async_computation.3 | async-start | bytes 2097152 | tf_op jit(solution)/shard_map/all_to_all | solution.py:177
  (2 other events, 1.1 us)

commit v6 on v3

--- a/solution.py
+++ b/solution.py
@@ -30,7 +30,13 @@
 ):
     seq_index = lax.axis_index("seq")
     requests, local_rows, width_part = tokens.shape
-    gathered = lax.all_gather(tokens, "tensor", axis=2, tiled=True).astype(jnp.float32)
+    token_copies = jnp.broadcast_to(tokens[None], (lax.axis_size("tensor"),) + tokens.shape)
+    gathered = (
+        lax.all_to_all(token_copies, "tensor", 0, 0, tiled=True)
+        .transpose(1, 2, 0, 3)
+        .reshape(requests, local_rows, -1)
+        .astype(jnp.float32)
+    )
     inverse_rms = lax.rsqrt(jnp.mean(gathered * gathered, -1, keepdims=True) + 1e-05)
     normed = (gathered * inverse_rms * norm_gain.astype(jnp.float32)).astype(jnp.bfloat16)
     flat_rows = normed.reshape(requests * local_rows, -1)
@@ -137,6 +143,7 @@
         )
     block_rows = local_rows + 1
     attended_list = []
+    tensor_count = lax.axis_size("tensor")
     for first in range(0, requests, 2):
         sent = jnp.concatenate(payload_list[first : first + 2], 1)
         arrived = lax.all_to_all(sent, "seq", 0, 0, tiled=True)
@@ -156,11 +163,17 @@
         .astype(jnp.bfloat16)
         .reshape(requests * local_rows, heads_width)
     )
-    partial_out = jnp.dot(attended, w_out, preferred_element_type=jnp.float32).reshape(
-        requests, local_rows, -1
-    )
-    mixed = lax.psum_scatter(partial_out, "tensor", scatter_dimension=2, tiled=True).astype(
-        jnp.bfloat16
+    partial_out = jnp.einsum(
+        "rk,kcn->crn",
+        attended,
+        w_out.reshape(heads_width, tensor_count, -1),
+        preferred_element_type=jnp.float32,
+    )
+    partial_sums = lax.all_to_all(partial_out, "tensor", 0, 0, tiled=True)
+    mixed = (
+        jnp.sum(partial_sums, 0)
+        .astype(jnp.bfloat16)
+        .reshape(requests, local_rows, partial_out.shape[2])
     )
     return (mixed, new_keys, new_values)
 

time: 271 us -> 222 us (0.82)
  waiting for transfers between devices: 124 us -> 56.6 us
  blocking collectives: 0 us -> 28.3 us
  between operations: 15.1 us -> 1.7 us
  starting transfers between devices: 18.7 us -> 24.7 us
  matrix products: 23.8 us -> 19.7 us
    reduce_scatter x1 -> x0, waiting for transfers between devices: 46.4 us -> none  [body(): lax.psum_scatter(partial_out, 'tensor', scatter_dimension=2, tiled=True)]
    all_gather x1 -> x0, waiting for transfers between devices: 34.4 us -> none  [body(): lax.all_gather(tokens, 'tensor', axis=2, tiled=True).astype(jnp.float32)]
    all_to_all x0 -> x1, blocking collectives: none -> 28.3 us  [body(): partial_sums = lax.all_to_all(partial_out, 'tensor', 0, 0, tiled=True)]
    all_to_all x2, waiting for transfers between devices: 29.3 us -> 38 us  [body(): arrived = lax.all_to_all(sent, 'seq', 0, 0, tiled=True)]
    all_to_all x0 -> x1, starting transfers between devices: none -> 5.4 us  [body(): lax.all_to_all(token_copies, 'tensor', 0, 0, tiled=True)]
    all_to_all x0 -> x1, waiting for transfers between devices: none -> 4.94 us  [body(): lax.all_to_all(token_copies, 'tensor', 0, 0, tiled=True)]
    slice x16, local copies, waits for them, and re-layouts: 4.52 us -> 8.29 us  [body(): received[:, local_rows, :local_rows * 2].reshape(-1, local_rows, 2)]
    dot_general x3, local copies, waits for them, and re-layouts: 12.4 us -> 8.78 us  [project(): jnp.dot(flat_rows, weight, preferred_element_type=jnp.float32)]
  transfers between devices with their start and end apart: 7 -> 6, of which waited for: 5 -> 4; matrix products, arithmetic and copies ran while one was open for 27% -> 24% of each run, Pallas kernels for 0% -> 0%
where the time goes in v6:
time: 222 us; the launch traced here: 220 us
  waiting for transfers between devices  56.6 us (25%)
  other arithmetic  46.4 us (21%)
  local copies, waits for them, and re-layouts  42.6 us (19%)
  blocking collectives  28.3 us (13%)
  starting transfers between devices  24.7 us (11%)
  matrix products  19.7 us (9%)
    all_to_all x2, waiting for transfers between devices, body(): arrived = lax.all_to_all(sent, 'seq', 0, 0, tiled=True)  38 us
    all_to_all x1, blocking collectives, body(): partial_sums = lax.all_to_all(partial_out, 'tensor', 0, 0, tiled=True)  28.3 us
    all_to_all x1, waiting for transfers between devices, body(): query_got = lax.all_to_all(query_sent, 'seq', 0, 0, tiled=True)  13.7 us
    all_to_all x1, starting transfers between devices, body(): query_got = lax.all_to_all(query_sent, 'seq', 0, 0, tiled=True)  10.9 us
    dot_general x3, local copies, waits for them, and re-layouts, project(): jnp.dot(flat_rows, weight, preferred_element_type=jnp.float32)  8.78 us
    slice x8, other arithmetic, body(): block_peak = block_stats[..., 0]  8.47 us
    slice x16, local copies, waits for them, and re-layouts, body(): received[:, local_rows, :local_rows * 2].reshape(-1, local_rows, 2)  8.29 us
    all_to_all x2, starting transfers between devices, body(): arrived = lax.all_to_all(sent, 'seq', 0, 0, tiled=True)  7.67 us
  transfers between devices with their start and end apart: 6, of which 4 were waited for; matrix products, arithmetic and copies ran while one was open for 24% of the time, Pallas kernels for 0%

profile of v6, /device:TPU:32, one launch (start us, length us, event | category | flops | bytes accessed | tf_op | source)
XLA Modules:
  0.0 220.0 jit_solution(2177850352363418412)
XLA Ops:
  0.7 2.2 broadcast_in_dim.82
  2.8 5.4 %all-to-all-start = ((bf16[8,4,32,512]{3,2,1,0:T(8,128)(2,1)}), bf16[8,4,32,512]{3,2,1,0:T(8,128)(2,1)S(1)}, u32[]{:S(2)}, u32[]{:S(2)}) async-start(bf16[8,4,32,512]{3,2,1,0:T(8,128)(2,1)} %broadcast_in_dim.82), calls=%async_computation | async-start | bytes 2097152 | tf_op jit(solution)/shard_map/all_to_all | solution.py:35
  8.2 2.9 %copy.208 = bf16[256,4096]{1,0:T(8,128)(2,1)} copy(bf16[256,4096]{0,1:T(8,128)(2,1)S(1)} %bitcast.203) | data formatting | bytes 4194304 | tf_op jit(solution)/shard_map/dot_general | solution.py:47
  11.2 2.9 %copy.209 = bf16[256,4096]{1,0:T(8,128)(2,1)S(1)} copy(bf16[256,4096]{0,1:T(8,128)(2,1)} %bitcast.204) | data formatting | bytes 4194304 | tf_op jit(solution)/shard_map/dot_general | solution.py:47
  15.3 1.8 constant_dynamic-slice_fusion.7
  17.1 1.9 constant_dynamic-slice_fusion.1
  19.0 4.9 %all-to-all-done = bf16[8,4,32,512]{3,2,1,0:T(8,128)(2,1)S(1)} async-done(((bf16[8,4,32,512]{3,2,1,0:T(8,128)(2,1)}), bf16[8,4,32,512]{3,2,1,0:T(8,128)(2,1)S(1)}, u32[]{:S(2)}, u32[]{:S(2)}) %all-to-all-start) | async-done | bytes 1048608 | tf_op jit(solution)/shard_map/all_to_all | solution.py:35
  25.2 1.3 reshape.498
  26.5 2.8 %fusion.30 = f32[4,32,2,128]{3,1,2,0:T(8,128)S(1)} fusion(bf16[2,128,4096,1]{2,1,0,3:T(8,128)(2,1)} %bitcast.209, bf16[4,32,4096,1]{2,1,0,3:T(8,128)(2,1)} %reshape.498), kind=kOutput, calls=%fused_computation.49 | convolution fusion | flops 268435456 | bytes 3276800 | tf_op jit(solution)/shard_map/dot_general | solution.py:47
  29.3 0.8 fusion.28
  30.6 1.2 tile.11
  31.8 10.9 %all-to-all-start.1 = ((bf16[32,128,128]{2,1,0:T(8,128)(2,1)}), bf16[32,128,128]{2,1,0:T(8,128)(2,1)S(1)}, u32[]{:S(2)}, u32[]{:S(2)}) async-start(bf16[32,128,128]{2,1,0:T(8,128)(2,1)} %bitcast.9), calls=%async_computation.1 | async-start | bytes 2097152 | tf_op jit(solution)/shard_map/all_to_all | solution.py:102
  42.7 1.9 pad_maximum_fusion.2
  44.7 2.9 %copy.210 = bf16[256,4096]{1,0:T(8,128)(2,1)} copy(bf16[256,4096]{0,1:T(8,128)(2,1)S(1)} %bitcast.205) | data formatting | bytes 4194304 | tf_op jit(solution)/shard_map/dot_general | solution.py:47
  49.6 2.6 %broadcast_compare_fusion.1 = (pred[512]{0:T(512)(128)(4,1)S(1)}, pred[512]{0:T(512)(128)(4,1)S(1)}, pred[512]{0:T(512)(128)(4,1)S(1)}, pred[512]{0:T(512)(128)(4,1)S(1)}) fusion(s32[]{:T(128)} %bitcast.55, s32[256]{0:T(256)S(1)} %get-tuple-element.105, s32[256]{0:T(256)S(1)} %get-tuple-element.106, s32[]{:T(128)} %bitcast.26, s32[]{:T(128)} %bitcast.66, ...), kind=kLoop, calls=%fused_computation.252 | loop fusion | flops 2560 | bytes 4112 | tf_op jit(solution)/shard_map/lt | solution.py:110
  52.3 1.8 broadcast_compare_fusion.7
  54.2 2.8 %fusion.25 = bf16[4,2,4,8,128]{4,3,2,1,0:T(8,128)(2,1)S(1)} fusion(bf16[2,128,4096,1]{2,1,0,3:T(8,128)(2,1)} %bitcast.207, bf16[4,32,4096,1]{2,1,0,3:T(8,128)(2,1)} %reshape.498), kind=kOutput, calls=%fused_computation.44 | convolution fusion | flops 268468224 | bytes 3211264 | tf_op jit(solution)/shard_map/dot_general | solution.py:47
  57.7 1.8 fusion.190
  59.5 13.7 %all-to-all-done.1 = bf16[32,128,128]{2,1,0:T(8,128)(2,1)S(1)} async-done(((bf16[32,128,128]{2,1,0:T(8,128)(2,1)}), bf16[32,128,128]{2,1,0:T(8,128)(2,1)S(1)}, u32[]{:S(2)}, u32[]{:S(2)}) %all-to-all-start.1) | async-done | bytes 1048608 | tf_op jit(solution)/shard_map/all_to_all | solution.py:102
  73.7 1.8 fusion.8
  79.3 0.9 convolution_add_fusion.2
  80.1 1.6 convolution_add_fusion.3
  83.3 2.2 %pad_maximum_fusion = f32[32,66,128]{2,1,0:T(8,128)} fusion(f32[32,1,128]{2,1,0:T(1,128)S(1)} %bitcast.252, f32[32,32,128]{2,1,0:T(8,128)S(1)} %bitcast.218, f32[32,1,128]{2,1,0:T(1,128)S(1)} %bitcast.251, f32[32,32,128]{2,1,0:T(8,128)} %bitcast.219), kind=kLoop, calls=%fused_computation.33 | loop fusion | flops 811008 | bytes 2162688 | tf_op jit(solution)/shard_map/concatenate | solution.py:148
  85.5 3.7 %all-to-all-start.2 = ((f32[32,66,128]{2,1,0:T(8,128)}), f32[32,66,128]{2,1,0:T(8,128)S(1)}, u32[]{:S(2)}, u32[]{:S(2)}) async-start(f32[32,66,128]{2,1,0:T(8,128)} %pad_maximum_fusion), calls=%async_computation.2 | async-start | bytes 2359296 | tf_op jit(solution)/shard_map/all_to_all | solution.py:149
  89.9 2.1 fusion.17
  92.0 1.0 copy.186
  93.1 1.9 reshape.492
  95.0 1.4 pad.15
  96.9 1.0 copy.187
  98.0 1.9 reshape.495
  100.6 1.3 fusion.74
  101.9 1.1 fusion.72
  103.0 2.5 %convolution_add_fusion.1 = f32[1024,128]{1,0:T(8,128)S(1)} fusion(f32[1024,128]{1,0:T(8,128)S(1)} %fusion.74, f32[1024,512]{0,1:T(8,128)} %get-tuple-element.98, f32[1024]{0:T(1024)S(1)} %max.60, pred[512]{0:T(512)(128)(4,1)S(1)} %copy-done.35, bf16[4,256,128]{2,1,0:T(8,128)(2,1)} %get-tuple-element.21, bf16[4,256,128]{2,1,0:T(8,128)(2,1)} %get-tuple-element.23), kind=kOutput, calls=%fused_computation.30 | convolution fusion | flops 137232384 | bytes 3674624 | tf_op jit(solution)/shard_map/dot_general | solution.py:130
  105.5 0.8 convolution_add_fusion
  106.4 1.1 pad_maximum_fusion.1
  107.5 14.7 %all-to-all-done.2 = f32[32,66,128]{2,1,0:T(8,128)S(1)} async-done(((f32[32,66,128]{2,1,0:T(8,128)}), f32[32,66,128]{2,1,0:T(8,128)S(1)}, u32[]{:S(2)}, u32[]{:S(2)}) %all-to-all-start.2) | async-done | bytes 1081376 | tf_op jit(solution)/shard_map/all_to_all | solution.py:149
  122.3 3.9 %all-to-all-start.3 = ((f32[32,66,128]{2,1,0:T(8,128)}), f32[32,66,128]{2,1,0:T(8,128)S(1)}, u32[]{:S(2)}, u32[]{:S(2)}) async-start(f32[32,66,128]{2,1,0:T(8,128)} %pad_maximum_fusion.1), calls=%async_computation.3 | async-start | bytes 2359296 | tf_op jit(solution)/shard_map/all_to_all | solution.py:149
  128.4 0.8 fusion.196
  129.9 0.8 fusion.195
  130.9 0.8 fusion.194
  132.4 1.7 fusion.59
  135.8 23.2 %all-to-all-done.3 = f32[32,66,128]{2,1,0:T(8,128)S(1)} async-done(((f32[32,66,128]{2,1,0:T(8,128)}), f32[32,66,128]{2,1,0:T(8,128)S(1)}, u32[]{:S(2)}, u32[]{:S(2)}) %all-to-all-start.3) | async-done | bytes 1081376 | tf_op jit(solution)/shard_map/all_to_all | solution.py:149
  161.5 1.4 copy.194
  162.9 1.4 copy.198
  164.3 1.4 copy.202
  165.7 1.4 copy.190
  167.0 1.7 fusion.197
  169.2 1.5 subtract_exponential_fusion.3
  170.7 1.4 copy.191
  172.1 1.4 fusion.55
  173.5 1.2 fusion.200
  174.7 0.9 subtract_exponential_fusion
  175.7 1.2 fusion.199
  176.9 0.9 subtract_exponential_fusion.1
  178.0 1.2 fusion.198
  179.1 0.9 subtract_exponential_fusion.2
  180.2 0.9 multiply_reduce_fusion.7
  181.9 0.9 multiply_reduce_fusion.4
  183.7 0.9 multiply_reduce_fusion.5
  185.4 0.9 multiply_reduce_fusion.6
  186.4 0.9 multiply_reduce_fusion.3
  189.0 1.4 broadcast_select_fusion
  190.8 28.3 %all_to_all.25 = f32[8,128,512]{2,1,0:T(8,128)S(1)} all-to-all(f32[8,128,512]{2,1,0:T(8,128)S(1)} %fusion.10), channel_id=1, replica_groups=mesh['seq'=32,'tensor'=8] {'tensor'}, dimensions={0} | all-to-all | bytes 4194304 | tf_op jit(solution)/shard_map/all_to_all | solution.py:172
  219.1 0.9 reduce_sum.259
  (192 shorter events, 26.5 us)
Async XLA Ops:
  0.6 7.6 %copy-start.21 = (bf16[4096]{0:T(1024)(128)(2,1)S(1)}, bf16[4096]{0:T(1024)(128)(2,1)}, u32[]{:S(2)}) copy-start(bf16[4096]{0:T(1024)(128)(2,1)} %param.11) | copy-start | bytes 24580
  0.6 7.6 %copy-start = (bf16[4096,256]{1,0:T(8,128)(2,1)S(1)}, bf16[4096,256]{1,0:T(8,128)(2,1)}, u32[]{:S(2)}) copy-start(bf16[4096,256]{1,0:T(8,128)(2,1)} %param.12) | copy-start | bytes 6291460
  2.8 21.1 %all-to-all-start = ((bf16[8,4,32,512]{3,2,1,0:T(8,128)(2,1)}), bf16[8,4,32,512]{3,2,1,0:T(8,128)(2,1)S(1)}, u32[]{:S(2)}, u32[]{:S(2)}) async-start(bf16[8,4,32,512]{3,2,1,0:T(8,128)(2,1)} %broadcast_in_dim.82), calls=%async_computation | async-start | bytes 2097152 | tf_op jit(solution)/shard_map/all_to_all | solution.py:35
  11.2 2.9 %copy-start.22 = (s32[4]{0:T(128)S(1)}, s32[4]{0:T(128)}, u32[]{:S(2)}) copy-start(s32[4]{0:T(128)} %param.18) | copy-start | bytes 52
  26.5 2.8 %copy-start.4 = (bf16[4,32,4096,1]{2,1,0,3:T(8,128)(2,1)S(1)}, bf16[4,32,4096,1]{2,1,0,3:T(8,128)(2,1)}, u32[]{:S(2)}) copy-start(bf16[4,32,4096,1]{2,1,0,3:T(8,128)(2,1)} %reshape.498) | copy-start | bytes 3145732
  29.3 1.0 copy-start.14
  30.5 23.6 %copy-start.10 = (bf16[4,2,4,8,128]{4,3,2,1,0:T(8,128)(2,1)}, bf16[4,2,4,8,128]{4,3,2,1,0:T(8,128)(2,1)S(1)}, u32[]{:S(2)}) copy-start(bf16[4,2,4,8,128]{4,3,2,1,0:T(8,128)(2,1)S(1)} %get-tuple-element.27) | copy-start | bytes 196612
  30.6 14.1 %copy-start.1 = (bf16[4096,256]{1,0:T(8,128)(2,1)S(1)}, bf16[4096,256]{1,0:T(8,128)(2,1)}, u32[]{:S(2)}) copy-start(bf16[4096,256]{1,0:T(8,128)(2,1)} %param.14) | copy-start | bytes 6291460
  31.8 41.4 %all-to-all-start.1 = ((bf16[32,128,128]{2,1,0:T(8,128)(2,1)}), bf16[32,128,128]{2,1,0:T(8,128)(2,1)S(1)}, u32[]{:S(2)}, u32[]{:S(2)}) async-start(bf16[32,128,128]{2,1,0:T(8,128)(2,1)} %bitcast.9), calls=%async_computation.1 | async-start | bytes 2097152 | tf_op jit(solution)/shard_map/all_to_all | solution.py:102
  44.6 13.1 %collective-permute-start = (bf16[4,512,128]{2,1,0:T(8,128)(2,1)}, bf16[4,512,128]{2,1,0:T(8,128)(2,1)}, u32[]{:S(2)}, u32[]{:S(2)}) collective-permute-start(bf16[4,512,128]{2,1,0:T(8,128)(2,1)} %pad_maximum_fusion.2), channel_id=1, source_target_pairs={{0,8},{8,0},{16,24},{24,16},{32,40},{40,32},{48,56},{56,48},{64,72... | collective-permute-start | bytes 1572872 | tf_op jit(solution)/shard_map/ppermute | solution.py:81
  44.7 2.9 %copy-start.24 = (s32[4]{0:T(128)S(1)}, s32[4]{0:T(128)}, u32[]{:S(2)}) copy-start(s32[4]{0:T(128)} %param.19) | copy-start | bytes 52
  44.7 4.3 %copy-start.23 = (s32[4]{0:T(128)S(1)}, s32[4]{0:T(128)}, u32[]{:S(2)}) copy-start(s32[4]{0:T(128)} %param.18) | copy-start | bytes 52
  47.6 2.0 copy-start.38
  49.0 32.8 %copy-start.20 = (s32[64]{0:T(128)}, s32[64]{0:T(128)S(1)}, u32[]{:S(2)}) copy-start(s32[64]{0:T(128)S(1)} %get-tuple-element.8) | copy-start | bytes 772
  49.0 32.8 %copy-start.36 = (pred[64]{0:T(512)(128)(4,1)}, pred[64]{0:T(512)(128)(4,1)S(1)}, u32[]{:S(2)}) copy-start(pred[64]{0:T(512)(128)(4,1)S(1)} %get-tuple-element.7) | copy-start | bytes 196
  52.3 21.5 %copy-start.33 = (pred[512]{0:T(512)(128)(4,1)}, pred[512]{0:T(512)(128)(4,1)S(1)}, u32[]{:S(2)}) copy-start(pred[512]{0:T(512)(128)(4,1)S(1)} %get-tuple-element.67) | copy-start | bytes 1540
  52.3 23.3 %copy-start.30 = (pred[512]{0:T(512)(128)(4,1)}, pred[512]{0:T(512)(128)(4,1)S(1)}, u32[]{:S(2)}) copy-start(pred[512]{0:T(512)(128)(4,1)S(1)} %get-tuple-element.69) | copy-start | bytes 1540
  54.1 27.7 %copy-start.37 = (pred[64]{0:T(512)(128)(4,1)}, pred[64]{0:T(512)(128)(4,1)S(1)}, u32[]{:S(2)}) copy-start(pred[64]{0:T(512)(128)(4,1)S(1)} %get-tuple-element.79) | copy-start | bytes 196
  56.9 2.5 %copy-start.15 = (bf16[4,2,4,8,128]{4,3,2,1,0:T(8,128)(2,1)}, bf16[4,2,4,8,128]{4,3,2,1,0:T(8,128)(2,1)S(1)}, u32[]{:S(2)}) copy-start(bf16[4,2,4,8,128]{4,3,2,1,0:T(8,128)(2,1)S(1)} %fusion.25) | copy-start | bytes 196612
  57.0 21.9 %copy-start.8 = (bf16[4,32,128]{2,1,0:T(8,128)(2,1)}, bf16[4,32,128]{2,1,0:T(8,128)(2,1)S(1)}, u32[]{:S(2)}) copy-start(bf16[4,32,128]{2,1,0:T(8,128)(2,1)S(1)} %get-tuple-element.33) | copy-start | bytes 98308
  57.0 2.4 %collective-permute-start.1 = (bf16[4,64,128]{2,1,0:T(8,128)(2,1)S(1)}, bf16[4,64,128]{2,1,0:T(8,128)(2,1)S(1)}, u32[]{:S(2)}, u32[]{:S(2)}) collective-permute-start(bf16[4,64,128]{2,1,0:T(8,128)(2,1)S(1)} %pad_maximum_fusion.7), channel_id=1, source_target_pairs={{0,8},{8,0},{16,24},{24,16},{32,40},{40,32},{48,56},{56,48},{64,72... | collective-permute-start | bytes 196616 | tf_op jit(solution)/shard_map/ppermute | solution.py:84
  59.5 19.4 %copy-start.9 = (bf16[4,32,128]{2,1,0:T(8,128)(2,1)}, bf16[4,32,128]{2,1,0:T(8,128)(2,1)S(1)}, u32[]{:S(2)}) copy-start(bf16[4,32,128]{2,1,0:T(8,128)(2,1)S(1)} %get-tuple-element.35) | copy-start | bytes 98308
  73.5 8.3 %copy-start.5 = (f32[1024,64]{0,1:T(8,128)}, f32[1024,64]{0,1:T(8,128)S(1)}, u32[]{:S(2)}) copy-start(f32[1024,64]{0,1:T(8,128)S(1)} %get-tuple-element.88) | copy-start | bytes 786436
  73.7 8.1 %copy-start.7 = (f32[1024,64]{0,1:T(8,128)}, f32[1024,64]{0,1:T(8,128)S(1)}, u32[]{:S(2)}) copy-start(f32[1024,64]{0,1:T(8,128)S(1)} %get-tuple-element.100) | copy-start | bytes 786436
  78.0 1.3 copy-start.12
  78.0 1.3 copy-start.17
  83.3 6.0 %copy-start.39 = (s32[32]{0:T(128)S(1)}, s32[32]{0:T(128)}, u32[]{:S(2)}) copy-start(s32[32]{0:T(128)} %copy-done.38) | copy-start | bytes 388
  83.3 6.6 %copy-start.34 = (pred[512]{0:T(512)(128)(4,1)S(1)}, pred[512]{0:T(512)(128)(4,1)}, u32[]{:S(2)}) copy-start(pred[512]{0:T(512)(128)(4,1)} %copy-done.33) | copy-start | bytes 1540
  85.5 36.7 %all-to-all-start.2 = ((f32[32,66,128]{2,1,0:T(8,128)}), f32[32,66,128]{2,1,0:T(8,128)S(1)}, u32[]{:S(2)}, u32[]{:S(2)}) async-start(f32[32,66,128]{2,1,0:T(8,128)} %pad_maximum_fusion), calls=%async_computation.2 | async-start | bytes 2359296 | tf_op jit(solution)/shard_map/all_to_all | solution.py:149
  89.9 6.5 %copy-start.31 = (pred[512]{0:T(512)(128)(4,1)S(1)}, pred[512]{0:T(512)(128)(4,1)}, u32[]{:S(2)}) copy-start(pred[512]{0:T(512)(128)(4,1)} %copy-done.30) | copy-start | bytes 1540
  95.0 6.9 %copy-start.6 = (f32[1024,64]{0,1:T(8,128)S(1)}, f32[1024,64]{0,1:T(8,128)}, u32[]{:S(2)}) copy-start(f32[1024,64]{0,1:T(8,128)} %copy-done.5) | copy-start | bytes 786436
  98.0 5.0 %copy-start.35 = (pred[512]{0:T(512)(128)(4,1)S(1)}, pred[512]{0:T(512)(128)(4,1)}, u32[]{:S(2)}) copy-start(pred[512]{0:T(512)(128)(4,1)} %copy-done.33) | copy-start | bytes 1540
  103.0 2.5 %copy-start.13 = (bf16[4,256,128]{2,1,0:T(8,128)(2,1)S(1)}, bf16[4,256,128]{2,1,0:T(8,128)(2,1)}, u32[]{:S(2)}) copy-start(bf16[4,256,128]{2,1,0:T(8,128)(2,1)} %get-tuple-element.21) | copy-start | bytes 786436
  103.0 2.5 %copy-start.18 = (bf16[4,256,128]{2,1,0:T(8,128)(2,1)S(1)}, bf16[4,256,128]{2,1,0:T(8,128)(2,1)}, u32[]{:S(2)}) copy-start(bf16[4,256,128]{2,1,0:T(8,128)(2,1)} %get-tuple-element.23) | copy-start | bytes 786436
  103.0 2.5 %copy-start.32 = (pred[512]{0:T(512)(128)(4,1)S(1)}, pred[512]{0:T(512)(128)(4,1)}, u32[]{:S(2)}) copy-start(pred[512]{0:T(512)(128)(4,1)} %copy-done.30) | copy-start | bytes 1540
  105.5 0.9 copy-start.19
  122.3 36.7 %all-to-all-start.3 = ((f32[32,66,128]{2,1,0:T(8,128)}), f32[32,66,128]{2,1,0:T(8,128)S(1)}, u32[]{:S(2)}, u32[]{:S(2)}) async-start(f32[32,66,128]{2,1,0:T(8,128)} %pad_maximum_fusion.1), calls=%async_computation.3 | async-start | bytes 2359296 | tf_op jit(solution)/shard_map/all_to_all | solution.py:149
  126.3 0.7 copy-start.3
  128.0 7.8 %copy-start.25 = (f32[32]{0:T(128)}, f32[32]{0:T(128)S(1)}, u32[]{:S(2)}) copy-start(f32[32]{0:T(128)S(1)} %get-tuple-element.42) | copy-start | bytes 388
  129.3 0.6 copy-start.27
  130.8 5.0 %copy-start.28 = (f32[32]{0:T(128)}, f32[32]{0:T(128)S(1)}, u32[]{:S(2)}) copy-start(f32[32]{0:T(128)S(1)} %get-tuple-element.48) | copy-start | bytes 388
  131.8 0.6 copy-start.26
  135.8 53.2 %copy-start.11 = (bf16[4,2,4,8,128]{4,3,2,1,0:T(8,128)(2,1)S(1)}, bf16[4,2,4,8,128]{4,3,2,1,0:T(8,128)(2,1)}, u32[]{:S(2)}) copy-start(bf16[4,2,4,8,128]{4,3,2,1,0:T(8,128)(2,1)} %copy-done.10) | copy-start | bytes 196612
  135.8 53.2 %copy-start.16 = (bf16[4,2,4,8,128]{4,3,2,1,0:T(8,128)(2,1)S(1)}, bf16[4,2,4,8,128]{4,3,2,1,0:T(8,128)(2,1)}, u32[]{:S(2)}) copy-start(bf16[4,2,4,8,128]{4,3,2,1,0:T(8,128)(2,1)} %copy-done.15) | copy-start | bytes 196612
  159.1 31.3 %copy-start.2 = (bf16[256,4096]{1,0:T(8,128)(2,1)S(1)}, bf16[256,4096]{1,0:T(8,128)(2,1)}, u32[]{:S(2)}) copy-start(bf16[256,4096]{1,0:T(8,128)(2,1)} %param.15) | copy-start | bytes 6291460
  168.7 0.5 copy-start.29

commit v7 on v5

--- a/solution.py
+++ b/solution.py
@@ -148,17 +148,20 @@
     for first in range(0, requests, 2):
         sent = jnp.concatenate(payload_list[first : first + 2], 1)
         arrived = lax.all_to_all(sent, "seq", 0, 0, tiled=True)
-        for member in range(sent.shape[1] // block_rows):
-            head_parts = []
-            for h in range(local_heads):
-                received = arrived[h::local_heads, member * block_rows : (member + 1) * block_rows]
-                block_stats = received[:, local_rows, : local_rows * 2].reshape(-1, local_rows, 2)
-                block_peak = block_stats[..., 0]
-                factor = jnp.exp(block_peak - jnp.max(block_peak, 0))
-                mass_sum = jnp.sum(block_stats[..., 1] * factor, 0)
-                numer_sum = jnp.sum(received[:, :local_rows] * factor[..., None], 0)
-                head_parts.append(numer_sum / mass_sum[:, None])
-            attended_list.append(jnp.concatenate(head_parts, -1))
+        members = sent.shape[1] // block_rows
+        grouped = arrived.reshape(-1, local_heads, members, block_rows, HD)
+        block_stats = grouped[:, :, :, local_rows, : local_rows * 2].reshape(
+            -1, local_heads, members, local_rows, 2
+        )
+        block_peak = block_stats[..., 0]
+        factor = jnp.exp(block_peak - jnp.max(block_peak, 0))
+        mass_sum = jnp.sum(block_stats[..., 1] * factor, 0)
+        numer_sum = jnp.sum(grouped[:, :, :, :local_rows] * factor[..., None], 0)
+        pair_attended = (numer_sum / mass_sum[..., None]).transpose(1, 2, 0, 3)
+        attended_list.extend(
+            pair_attended.reshape(members, local_rows, heads_width)[member]
+            for member in range(members)
+        )
         attended = (
             jnp.where(
                 live_rows[first : first + 2, :, None],

time: 213 us -> 207 us (0.972)
  other arithmetic: 34.7 us -> 25.3 us
  waiting for transfers between devices: 86 us -> 94.2 us
  local copies, waits for them, and re-layouts: 34.5 us -> 31 us
    all_to_all x2, waiting for transfers between devices: 38.4 us -> 43.9 us  [body(): arrived = lax.all_to_all(sent, 'seq', 0, 0, tiled=True)]
    slice x8 -> x2, other arithmetic: 5.14 us -> 0.69 us  [body(): block_peak = block_stats[..., 0]]
    slice x18 -> x10, local copies, waits for them, and re-layouts: 3.46 us -> 0.33 us  [the longest x4 0.21 us: body(): grouped[:, :, :, local_rows, :local_rows * 2]]
  transfers between devices with their start and end apart: 8 -> 8, of which waited for: 6 -> 6; matrix products, arithmetic and copies ran while one was open for 29% -> 27% of each run, Pallas kernels for 0% -> 0%
where the time goes in v7:
time: 207 us; the launch traced here: 206 us
  waiting for transfers between devices  94.2 us (46%)
  starting transfers between devices  31.5 us (15%)
  local copies, waits for them, and re-layouts  31 us (15%)
  other arithmetic  25.3 us (12%)
  matrix products  22.3 us (11%)
    all_to_all x2, waiting for transfers between devices, body(): arrived = lax.all_to_all(sent, 'seq', 0, 0, tiled=True)  43.9 us
    all_to_all x2, waiting for transfers between devices, body(): partial_sums = lax.all_to_all(partial_out, 'tensor', 0, 0, tiled=True)  25.9 us
    all_to_all x1, waiting for transfers between devices, body(): query_got = lax.all_to_all(query_sent, 'seq', 0, 0, tiled=True)  15.7 us
    all_to_all x1, starting transfers between devices, body(): query_got = lax.all_to_all(query_sent, 'seq', 0, 0, tiled=True)  10.9 us
    dot_general x3, local copies, waits for them, and re-layouts, project(): jnp.dot(flat_rows, weight, preferred_element_type=jnp.float32)  8.85 us
    all_to_all x1, waiting for transfers between devices, body(): lax.all_to_all(token_copies, 'tensor', 0, 0, tiled=True)  8.73 us
    all_to_all x2, starting transfers between devices, body(): arrived = lax.all_to_all(sent, 'seq', 0, 0, tiled=True)  7.68 us
    all_to_all x2, starting transfers between devices, body(): partial_sums = lax.all_to_all(partial_out, 'tensor', 0, 0, tiled=True)  7.11 us
  transfers between devices with their start and end apart: 8, of which 6 were waited for; matrix products, arithmetic and copies ran while one was open for 27% of the time, Pallas kernels for 0%

profile of v7, /device:TPU:32, one launch (start us, length us, event | category | flops | bytes accessed | tf_op | source)
XLA Modules:
  0.0 205.9 jit_solution(18110905425652347877)
XLA Ops:
  0.7 1.1 constant_dynamic-slice_fusion.7
  1.8 1.8 constant_dynamic-slice_fusion.1
  3.6 0.8 pad_maximum_fusion.2
  4.4 1.1 broadcast_in_dim.146
  5.5 5.4 %all-to-all-start = ((bf16[8,4,32,512]{3,2,1,0:T(8,128)(2,1)}), bf16[8,4,32,512]{3,2,1,0:T(8,128)(2,1)S(1)}, u32[]{:S(2)}, u32[]{:S(2)}) async-start(bf16[8,4,32,512]{3,2,1,0:T(8,128)(2,1)} %broadcast_in_dim.146), calls=%async_computation | async-start | bytes 2097152 | tf_op jit(solution)/shard_map/all_to_all | solution.py:35
  10.9 0.5 iota_add_fusion.3
  11.5 3.0 %copy.102 = bf16[256,4096]{1,0:T(8,128)(2,1)} copy(bf16[256,4096]{0,1:T(8,128)(2,1)S(1)} %bitcast.196) | data formatting | bytes 4194304 | tf_op jit(solution)/shard_map/dot_general | solution.py:47
  14.5 2.9 %copy.103 = bf16[256,4096]{1,0:T(8,128)(2,1)S(1)} copy(bf16[256,4096]{0,1:T(8,128)(2,1)} %bitcast.197) | data formatting | bytes 4194304 | tf_op jit(solution)/shard_map/dot_general | solution.py:47
  17.9 0.7 pad_maximum_fusion.7
  18.6 8.7 %all-to-all-done = bf16[8,4,32,512]{3,2,1,0:T(8,128)(2,1)S(1)} async-done(((bf16[8,4,32,512]{3,2,1,0:T(8,128)(2,1)}), bf16[8,4,32,512]{3,2,1,0:T(8,128)(2,1)S(1)}, u32[]{:S(2)}, u32[]{:S(2)}) %all-to-all-start) | async-done | bytes 1048608 | tf_op jit(solution)/shard_map/all_to_all | solution.py:35
  28.0 0.6 copy.72
  28.6 1.3 reshape.501
  29.9 2.8 %fusion.38 = f32[4,32,2,128]{3,1,2,0:T(8,128)S(1)} fusion(bf16[2,128,4096,1]{2,1,0,3:T(8,128)(2,1)} %bitcast.201, bf16[4,32,4096,1]{2,1,0,3:T(8,128)(2,1)} %reshape.501), kind=kOutput, calls=%fused_computation.57 | convolution fusion | flops 268435456 | bytes 3276800 | tf_op jit(solution)/shard_map/dot_general | solution.py:47
  32.9 0.8 fusion.36
  34.0 1.2 tile.11
  35.3 10.9 %all-to-all-start.1 = ((bf16[32,128,128]{2,1,0:T(8,128)(2,1)}), bf16[32,128,128]{2,1,0:T(8,128)(2,1)S(1)}, u32[]{:S(2)}, u32[]{:S(2)}) async-start(bf16[32,128,128]{2,1,0:T(8,128)(2,1)} %bitcast.9), calls=%async_computation.1 | async-start | bytes 2097152 | tf_op jit(solution)/shard_map/all_to_all | solution.py:102
  46.2 3.0 %copy.104 = bf16[256,4096]{1,0:T(8,128)(2,1)} copy(bf16[256,4096]{0,1:T(8,128)(2,1)S(1)} %bitcast.198) | data formatting | bytes 4194304 | tf_op jit(solution)/shard_map/dot_general | solution.py:47
  49.2 0.7 fusion.198
  49.9 0.7 broadcast_compare_fusion.6
  50.6 0.7 fusion.197
  51.3 2.6 %broadcast_compare_fusion.1 = (pred[512]{0:T(512)(128)(4,1)S(1)}, pred[512]{0:T(512)(128)(4,1)S(1)}, pred[512]{0:T(512)(128)(4,1)S(1)}, pred[512]{0:T(512)(128)(4,1)S(1)}) fusion(s32[]{:T(128)} %bitcast.48, s32[256]{0:T(256)S(1)} %iota_add_fusion, s32[256]{0:T(256)S(1)} %iota_add_fusion.1, s32[]{:T(128)} %bitcast.26, s32[]{:T(128)} %bitcast.59, s32[]{:T(128)} %bitcast), kind=kLoop, calls=%fused_computation.225 | loop fusion | flops 2560 | bytes 4112 | tf_op jit(solution)/shard_map/lt | solution.py:110
  53.9 1.9 broadcast_compare_fusion.7
  55.9 2.8 %fusion.31 = bf16[4,2,4,8,128]{4,3,2,1,0:T(8,128)(2,1)S(1)} fusion(bf16[2,128,4096,1]{2,1,0,3:T(8,128)(2,1)} %bitcast.199, bf16[4,32,4096,1]{2,1,0,3:T(8,128)(2,1)} %reshape.501), kind=kOutput, calls=%fused_computation.48 | convolution fusion | flops 268468224 | bytes 3211264 | tf_op jit(solution)/shard_map/dot_general | solution.py:47
  58.8 0.4 collective-permute-start.1
  59.1 1.8 fusion.189
  60.9 15.7 %all-to-all-done.1 = bf16[32,128,128]{2,1,0:T(8,128)(2,1)S(1)} async-done(((bf16[32,128,128]{2,1,0:T(8,128)(2,1)}), bf16[32,128,128]{2,1,0:T(8,128)(2,1)S(1)}, u32[]{:S(2)}, u32[]{:S(2)}) %all-to-all-start.1) | async-done | bytes 1048608 | tf_op jit(solution)/shard_map/all_to_all | solution.py:102
  77.2 1.8 fusion.9
  79.0 0.5 fusion.10
  79.7 0.5 fusion.8
  80.4 0.5 fusion.7
  81.6 1.1 fusion.13
  82.7 0.9 convolution_add_fusion.2
  83.6 1.7 convolution_add_fusion.3
  85.3 0.9 fusion.64
  87.3 2.2 %pad_maximum_fusion = f32[32,66,128]{2,1,0:T(8,128)} fusion(f32[32,1,128]{2,1,0:T(1,128)S(1)} %bitcast.240, f32[32,32,128]{2,1,0:T(8,128)S(1)} %bitcast.214, f32[32,1,128]{2,1,0:T(1,128)S(1)} %bitcast.239, f32[32,32,128]{2,1,0:T(8,128)} %bitcast.215), kind=kLoop, calls=%fused_computation.37 | loop fusion | flops 811008 | bytes 2162688 | tf_op jit(solution)/shard_map/concatenate | solution.py:149
  89.5 3.7 %all-to-all-start.2 = ((f32[32,66,128]{2,1,0:T(8,128)}), f32[32,66,128]{2,1,0:T(8,128)S(1)}, u32[]{:S(2)}, u32[]{:S(2)}) async-start(f32[32,66,128]{2,1,0:T(8,128)} %pad_maximum_fusion), calls=%async_computation.2 | async-start | bytes 2359296 | tf_op jit(solution)/shard_map/all_to_all | solution.py:150
  93.2 3.3 %fusion.17 = (f32[1024]{0:T(1024)S(1)}, f32[1024]{0:T(1024)}) fusion(f32[1024,512]{0,1:T(8,128)} %get-tuple-element.77, f32[1024]{0:T(1024)S(1)} %max.60, pred[512]{0:T(512)(128)(4,1)S(1)} %copy-done.29, f32[1024]{0:T(1024)S(1)} %max.62, f32[1024,512]{0,1:T(8,128)S(1)} %get-tuple-element.65, pred[512]{0:T(512)(128)(4,1)S(1)} %get-tuple-element.47), kind=kLoop, calls=%fused_computation.27 | loop fusion | flops 5240832 | bytes 4211712 | tf_op jit(solution)/shard_map/reduce_sum | solution.py:129
  96.5 1.0 copy.90
  97.6 1.9 reshape.495
  99.5 1.3 pad.15
  100.8 0.7 add.213
  101.5 1.0 copy.91
  102.5 1.9 reshape.498
  104.4 0.7 pad.16
  105.2 1.3 fusion.74
  106.5 1.1 fusion.72
  107.6 2.5 %convolution_add_fusion.1 = f32[1024,128]{1,0:T(8,128)S(1)} fusion(f32[1024,128]{1,0:T(8,128)S(1)} %fusion.74, f32[1024,512]{0,1:T(8,128)} %get-tuple-element.77, f32[1024]{0:T(1024)S(1)} %max.60, pred[512]{0:T(512)(128)(4,1)S(1)} %copy-done.30, bf16[4,256,128]{2,1,0:T(8,128)(2,1)} %get-tuple-element.13, bf16[4,256,128]{2,1,0:T(8,128)(2,1)} %get-tuple-element.15), kind=kOutput, calls=%fused_computation.34 | convolution fusion | flops 137232384 | bytes 3674624 | tf_op jit(solution)/shard_map/dot_general | solution.py:130
  110.1 0.8 convolution_add_fusion
  111.0 1.2 pad_maximum_fusion.1
  112.1 14.1 %all-to-all-done.2 = f32[32,66,128]{2,1,0:T(8,128)S(1)} async-done(((f32[32,66,128]{2,1,0:T(8,128)}), f32[32,66,128]{2,1,0:T(8,128)S(1)}, u32[]{:S(2)}, u32[]{:S(2)}) %all-to-all-start.2) | async-done | bytes 1081376 | tf_op jit(solution)/shard_map/all_to_all | solution.py:150
  126.2 3.9 %all-to-all-start.4 = ((f32[32,66,128]{2,1,0:T(8,128)}), f32[32,66,128]{2,1,0:T(8,128)S(1)}, u32[]{:S(2)}, u32[]{:S(2)}) async-start(f32[32,66,128]{2,1,0:T(8,128)} %pad_maximum_fusion.1), calls=%async_computation.4 | async-start | bytes 2359296 | tf_op jit(solution)/shard_map/all_to_all | solution.py:150
  131.5 0.4 copy.85
  131.9 1.3 fusion.34
  133.2 29.8 %all-to-all-done.4 = f32[32,66,128]{2,1,0:T(8,128)S(1)} async-done(((f32[32,66,128]{2,1,0:T(8,128)}), f32[32,66,128]{2,1,0:T(8,128)S(1)}, u32[]{:S(2)}, u32[]{:S(2)}) %all-to-all-start.4) | async-done | bytes 1081376 | tf_op jit(solution)/shard_map/all_to_all | solution.py:150
  164.2 1.3 copy.96
  165.4 2.2 %fusion.33 = f32[2,2,32,128]{3,0,2,1:T(2,128)S(1)} fusion(f32[16,2,2,33,128]{4,1,0,3,2:T(2,128)S(1)} %bitcast.195, f32[16,2,2,32]{1,0,3,2:T(8,128)} %copy.96), kind=kLoop, calls=%fused_computation.51 | loop fusion | flops 507904 | bytes 1122304 | tf_op jit(solution)/shard_map/reduce_sum | solution.py:159
  168.0 1.4 fusion.24
  169.4 3.6 %all-to-all-start.5 = ((f32[8,64,512]{2,1,0:T(8,128)}), f32[8,64,512]{2,1,0:T(8,128)S(1)}, u32[]{:S(2)}, u32[]{:S(2)}) async-start(f32[8,64,512]{2,1,0:T(8,128)} %fusion.24), calls=%async_computation.5 | async-start | bytes 2097152 | tf_op jit(solution)/shard_map/all_to_all | solution.py:180
  173.3 1.5 fusion.21
  174.8 12.7 %all-to-all-done.5 = f32[8,64,512]{2,1,0:T(8,128)S(1)} async-done(((f32[8,64,512]{2,1,0:T(8,128)}), f32[8,64,512]{2,1,0:T(8,128)S(1)}, u32[]{:S(2)}, u32[]{:S(2)}) %all-to-all-start.5) | async-done | bytes 1048608 | tf_op jit(solution)/shard_map/all_to_all | solution.py:180
  187.6 3.6 %all-to-all-start.3 = ((f32[8,64,512]{2,1,0:T(8,128)}), f32[8,64,512]{2,1,0:T(8,128)S(1)}, u32[]{:S(2)}, u32[]{:S(2)}) async-start(f32[8,64,512]{2,1,0:T(8,128)} %fusion.21), calls=%async_computation.3 | async-start | bytes 2097152 | tf_op jit(solution)/shard_map/all_to_all | solution.py:180
  191.1 0.7 broadcast_select_fusion
  192.0 13.2 %all-to-all-done.3 = f32[8,64,512]{2,1,0:T(8,128)S(1)} async-done(((f32[8,64,512]{2,1,0:T(8,128)}), f32[8,64,512]{2,1,0:T(8,128)S(1)}, u32[]{:S(2)}, u32[]{:S(2)}) %all-to-all-start.3) | async-done | bytes 1048608 | tf_op jit(solution)/shard_map/all_to_all | solution.py:180
  205.2 0.7 pad_maximum_fusion.5
  (149 shorter events, 7.6 us)
Async XLA Ops:
  0.6 3.8 %copy-start.18 = (bf16[4,32,512]{2,1,0:T(8,128)(2,1)S(1)}, bf16[4,32,512]{2,1,0:T(8,128)(2,1)}, u32[]{:S(2)}) copy-start(bf16[4,32,512]{2,1,0:T(8,128)(2,1)} %param.10) | copy-start | bytes 393220
  3.6 7.9 %copy-start.21 = (bf16[4096]{0:T(1024)(128)(2,1)S(1)}, bf16[4096]{0:T(1024)(128)(2,1)}, u32[]{:S(2)}) copy-start(bf16[4096]{0:T(1024)(128)(2,1)} %param.11) | copy-start | bytes 24580
  3.6 7.9 %copy-start.1 = (bf16[4096,256]{1,0:T(8,128)(2,1)S(1)}, bf16[4096,256]{1,0:T(8,128)(2,1)}, u32[]{:S(2)}) copy-start(bf16[4096,256]{1,0:T(8,128)(2,1)} %param.12) | copy-start | bytes 6291460
  4.4 54.7 %collective-permute-start = (bf16[4,512,128]{2,1,0:T(8,128)(2,1)}, bf16[4,512,128]{2,1,0:T(8,128)(2,1)}, u32[]{:S(2)}, u32[]{:S(2)}) collective-permute-start(bf16[4,512,128]{2,1,0:T(8,128)(2,1)} %pad_maximum_fusion.2), channel_id=1, source_target_pairs={{0,8},{8,0},{16,24},{24,16},{32,40},{40,32},{48,56},{56,48},{64,72... | collective-permute-start | bytes 1572872 | tf_op jit(solution)/shard_map/ppermute | solution.py:81
  5.5 21.8 %all-to-all-start = ((bf16[8,4,32,512]{3,2,1,0:T(8,128)(2,1)}), bf16[8,4,32,512]{3,2,1,0:T(8,128)(2,1)S(1)}, u32[]{:S(2)}, u32[]{:S(2)}) async-start(bf16[8,4,32,512]{3,2,1,0:T(8,128)(2,1)} %broadcast_in_dim.146), calls=%async_computation | async-start | bytes 2097152 | tf_op jit(solution)/shard_map/all_to_all | solution.py:35
  14.4 2.9 %copy-start.22 = (s32[4]{0:T(128)S(1)}, s32[4]{0:T(128)}, u32[]{:S(2)}) copy-start(s32[4]{0:T(128)} %param.18) | copy-start | bytes 52
  29.9 2.9 %copy-start.3 = (bf16[4,32,4096,1]{2,1,0,3:T(8,128)(2,1)S(1)}, bf16[4,32,4096,1]{2,1,0,3:T(8,128)(2,1)}, u32[]{:S(2)}) copy-start(bf16[4,32,4096,1]{2,1,0,3:T(8,128)(2,1)} %reshape.501) | copy-start | bytes 3145732
  32.8 1.0 copy-start.13
  33.8 12.4 %copy-start.2 = (bf16[4096,256]{1,0:T(8,128)(2,1)S(1)}, bf16[4096,256]{1,0:T(8,128)(2,1)}, u32[]{:S(2)}) copy-start(bf16[4096,256]{1,0:T(8,128)(2,1)} %param.14) | copy-start | bytes 6291460
  34.0 21.9 %copy-start.9 = (bf16[4,2,4,8,128]{4,3,2,1,0:T(8,128)(2,1)}, bf16[4,2,4,8,128]{4,3,2,1,0:T(8,128)(2,1)S(1)}, u32[]{:S(2)}) copy-start(bf16[4,2,4,8,128]{4,3,2,1,0:T(8,128)(2,1)S(1)} %get-tuple-element.25) | copy-start | bytes 196612
  35.3 41.4 %all-to-all-start.1 = ((bf16[32,128,128]{2,1,0:T(8,128)(2,1)}), bf16[32,128,128]{2,1,0:T(8,128)(2,1)S(1)}, u32[]{:S(2)}, u32[]{:S(2)}) async-start(bf16[32,128,128]{2,1,0:T(8,128)(2,1)} %bitcast.9), calls=%async_computation.1 | async-start | bytes 2097152 | tf_op jit(solution)/shard_map/all_to_all | solution.py:102
  46.2 3.0 %copy-start.24 = (s32[4]{0:T(128)S(1)}, s32[4]{0:T(128)}, u32[]{:S(2)}) copy-start(s32[4]{0:T(128)} %param.19) | copy-start | bytes 52
  46.2 3.7 %copy-start.33 = (s32[32]{0:T(128)S(1)}, s32[32]{0:T(128)}, u32[]{:S(2)}) copy-start(s32[32]{0:T(128)} %iota_add_fusion.3) | copy-start | bytes 388
  46.2 4.4 %copy-start.23 = (s32[4]{0:T(128)S(1)}, s32[4]{0:T(128)}, u32[]{:S(2)}) copy-start(s32[4]{0:T(128)} %param.18) | copy-start | bytes 52
  50.6 34.6 %copy-start.20 = (s32[64]{0:T(128)}, s32[64]{0:T(128)S(1)}, u32[]{:S(2)}) copy-start(s32[64]{0:T(128)S(1)} %get-tuple-element.8) | copy-start | bytes 772
  50.6 34.6 %copy-start.31 = (pred[64]{0:T(512)(128)(4,1)}, pred[64]{0:T(512)(128)(4,1)S(1)}, u32[]{:S(2)}) copy-start(pred[64]{0:T(512)(128)(4,1)S(1)} %get-tuple-element.7) | copy-start | bytes 196
  53.9 23.3 %copy-start.28 = (pred[512]{0:T(512)(128)(4,1)}, pred[512]{0:T(512)(128)(4,1)S(1)}, u32[]{:S(2)}) copy-start(pred[512]{0:T(512)(128)(4,1)S(1)} %get-tuple-element.45) | copy-start | bytes 1540
  53.9 39.4 %copy-start.26 = (pred[512]{0:T(512)(128)(4,1)}, pred[512]{0:T(512)(128)(4,1)S(1)}, u32[]{:S(2)}) copy-start(pred[512]{0:T(512)(128)(4,1)S(1)} %get-tuple-element.47) | copy-start | bytes 1540
  55.8 29.4 %copy-start.32 = (pred[64]{0:T(512)(128)(4,1)}, pred[64]{0:T(512)(128)(4,1)S(1)}, u32[]{:S(2)}) copy-start(pred[64]{0:T(512)(128)(4,1)S(1)} %get-tuple-element.58) | copy-start | bytes 196
  58.6 2.3 %copy-start.14 = (bf16[4,2,4,8,128]{4,3,2,1,0:T(8,128)(2,1)}, bf16[4,2,4,8,128]{4,3,2,1,0:T(8,128)(2,1)S(1)}, u32[]{:S(2)}) copy-start(bf16[4,2,4,8,128]{4,3,2,1,0:T(8,128)(2,1)S(1)} %fusion.31) | copy-start | bytes 196612
  58.7 22.5 %copy-start.7 = (bf16[4,32,128]{2,1,0:T(8,128)(2,1)}, bf16[4,32,128]{2,1,0:T(8,128)(2,1)S(1)}, u32[]{:S(2)}) copy-start(bf16[4,32,128]{2,1,0:T(8,128)(2,1)S(1)} %get-tuple-element.31) | copy-start | bytes 98308
  58.8 2.2 %collective-permute-start.1 = (bf16[4,64,128]{2,1,0:T(8,128)(2,1)S(1)}, bf16[4,64,128]{2,1,0:T(8,128)(2,1)S(1)}, u32[]{:S(2)}, u32[]{:S(2)}) collective-permute-start(bf16[4,64,128]{2,1,0:T(8,128)(2,1)S(1)} %pad_maximum_fusion.8), channel_id=1, source_target_pairs={{0,8},{8,0},{16,24},{24,16},{32,40},{40,32},{48,56},{56,48},{64,72... | collective-permute-start | bytes 196616 | tf_op jit(solution)/shard_map/ppermute | solution.py:84
  60.9 20.3 %copy-start.8 = (bf16[4,32,128]{2,1,0:T(8,128)(2,1)}, bf16[4,32,128]{2,1,0:T(8,128)(2,1)S(1)}, u32[]{:S(2)}) copy-start(bf16[4,32,128]{2,1,0:T(8,128)(2,1)S(1)} %get-tuple-element.33) | copy-start | bytes 98308
  76.9 8.3 %copy-start.4 = (f32[1024,64]{0,1:T(8,128)}, f32[1024,64]{0,1:T(8,128)S(1)}, u32[]{:S(2)}) copy-start(f32[1024,64]{0,1:T(8,128)S(1)} %get-tuple-element.67) | copy-start | bytes 786436
  77.2 8.1 %copy-start.6 = (f32[1024,64]{0,1:T(8,128)}, f32[1024,64]{0,1:T(8,128)S(1)}, u32[]{:S(2)}) copy-start(f32[1024,64]{0,1:T(8,128)S(1)} %get-tuple-element.79) | copy-start | bytes 786436
  81.6 1.1 copy-start.11
  81.6 1.1 copy-start.16
  87.3 6.0 %copy-start.29 = (pred[512]{0:T(512)(128)(4,1)S(1)}, pred[512]{0:T(512)(128)(4,1)}, u32[]{:S(2)}) copy-start(pred[512]{0:T(512)(128)(4,1)} %copy-done.28) | copy-start | bytes 1540
  89.5 36.7 %all-to-all-start.2 = ((f32[32,66,128]{2,1,0:T(8,128)}), f32[32,66,128]{2,1,0:T(8,128)S(1)}, u32[]{:S(2)}, u32[]{:S(2)}) async-start(f32[32,66,128]{2,1,0:T(8,128)} %pad_maximum_fusion), calls=%async_computation.2 | async-start | bytes 2359296 | tf_op jit(solution)/shard_map/all_to_all | solution.py:150
  96.5 9.9 %copy-start.5 = (f32[1024,64]{0,1:T(8,128)S(1)}, f32[1024,64]{0,1:T(8,128)}, u32[]{:S(2)}) copy-start(f32[1024,64]{0,1:T(8,128)} %copy-done.4) | copy-start | bytes 786436
  102.5 5.0 %copy-start.30 = (pred[512]{0:T(512)(128)(4,1)S(1)}, pred[512]{0:T(512)(128)(4,1)}, u32[]{:S(2)}) copy-start(pred[512]{0:T(512)(128)(4,1)} %copy-done.28) | copy-start | bytes 1540
  107.5 2.5 %copy-start.12 = (bf16[4,256,128]{2,1,0:T(8,128)(2,1)S(1)}, bf16[4,256,128]{2,1,0:T(8,128)(2,1)}, u32[]{:S(2)}) copy-start(bf16[4,256,128]{2,1,0:T(8,128)(2,1)} %get-tuple-element.13) | copy-start | bytes 786436
  107.5 2.5 %copy-start.17 = (bf16[4,256,128]{2,1,0:T(8,128)(2,1)S(1)}, bf16[4,256,128]{2,1,0:T(8,128)(2,1)}, u32[]{:S(2)}) copy-start(bf16[4,256,128]{2,1,0:T(8,128)(2,1)} %get-tuple-element.15) | copy-start | bytes 786436
  107.6 2.5 %copy-start.27 = (pred[512]{0:T(512)(128)(4,1)S(1)}, pred[512]{0:T(512)(128)(4,1)}, u32[]{:S(2)}) copy-start(pred[512]{0:T(512)(128)(4,1)} %copy-done.26) | copy-start | bytes 1540
  110.1 0.9 copy-start.19
  110.9 19.3 %copy-start.25 = (s32[4]{0:T(128)S(1)}, s32[4]{0:T(128)}, u32[]{:S(2)}) copy-start(s32[4]{0:T(128)} %param.19) | copy-start | bytes 52
  111.0 19.3 %copy-start.34 = (s32[32]{0:T(128)S(1)}, s32[32]{0:T(128)}, u32[]{:S(2)}) copy-start(s32[32]{0:T(128)} %iota_add_fusion.3) | copy-start | bytes 388
  126.2 36.7 %all-to-all-start.4 = ((f32[32,66,128]{2,1,0:T(8,128)}), f32[32,66,128]{2,1,0:T(8,128)S(1)}, u32[]{:S(2)}, u32[]{:S(2)}) async-start(f32[32,66,128]{2,1,0:T(8,128)} %pad_maximum_fusion.1), calls=%async_computation.4 | async-start | bytes 2359296 | tf_op jit(solution)/shard_map/all_to_all | solution.py:150
  163.2 4.8 %copy-start = (bf16[256,4096]{1,0:T(8,128)(2,1)S(1)}, bf16[256,4096]{1,0:T(8,128)(2,1)}, u32[]{:S(2)}) copy-start(bf16[256,4096]{1,0:T(8,128)(2,1)} %param.15) | copy-start | bytes 6291460
  169.4 18.1 %all-to-all-start.5 = ((f32[8,64,512]{2,1,0:T(8,128)}), f32[8,64,512]{2,1,0:T(8,128)S(1)}, u32[]{:S(2)}, u32[]{:S(2)}) async-start(f32[8,64,512]{2,1,0:T(8,128)} %fusion.24), calls=%async_computation.5 | async-start | bytes 2097152 | tf_op jit(solution)/shard_map/all_to_all | solution.py:180
  173.3 17.8 %copy-start.10 = (bf16[4,2,4,8,128]{4,3,2,1,0:T(8,128)(2,1)S(1)}, bf16[4,2,4,8,128]{4,3,2,1,0:T(8,128)(2,1)}, u32[]{:S(2)}) copy-start(bf16[4,2,4,8,128]{4,3,2,1,0:T(8,128)(2,1)} %copy-done.9) | copy-start | bytes 196612
  173.3 17.8 %copy-start.15 = (bf16[4,2,4,8,128]{4,3,2,1,0:T(8,128)(2,1)S(1)}, bf16[4,2,4,8,128]{4,3,2,1,0:T(8,128)(2,1)}, u32[]{:S(2)}) copy-start(bf16[4,2,4,8,128]{4,3,2,1,0:T(8,128)(2,1)} %copy-done.14) | copy-start | bytes 196612
  187.6 17.6 %all-to-all-start.3 = ((f32[8,64,512]{2,1,0:T(8,128)}), f32[8,64,512]{2,1,0:T(8,128)S(1)}, u32[]{:S(2)}, u32[]{:S(2)}) async-start(f32[8,64,512]{2,1,0:T(8,128)} %fusion.21), calls=%async_computation.3 | async-start | bytes 2097152 | tf_op jit(solution)/shard_map/all_to_all | solution.py:180

commit v8 on v7

--- a/solution.py
+++ b/solution.py
@@ -177,7 +177,9 @@
             w_out.reshape(heads_width, tensor_count, -1),
             preferred_element_type=jnp.float32,
         )
-        partial_sums = lax.all_to_all(partial_out, "tensor", 0, 0, tiled=True)
+        partial_sums = lax.all_to_all(
+            partial_out.astype(jnp.bfloat16), "tensor", 0, 0, tiled=True
+        ).astype(jnp.float32)
         mixed_list.append(
             jnp.sum(partial_sums, 0).astype(jnp.bfloat16).reshape(-1, local_rows, partial_out.shape[2])
         )

time: 207 us -> 191 us (0.923)
  waiting for transfers between devices: 94.2 us -> 69.7 us
  local copies, waits for them, and re-layouts: 31 us -> 35.9 us
    all_to_all x2, waiting for transfers between devices: 25.9 us -> 8.29 us  [body(): lax.all_to_all(partial_out.astype(jnp.bfloat16), 'tensor', 0, 0, tiled=True)]
    all_to_all x2, waiting for transfers between devices: 43.9 us -> 38.7 us  [body(): arrived = lax.all_to_all(sent, 'seq', 0, 0, tiled=True)]
    dot_general x3, local copies, waits for them, and re-layouts: 8.85 us -> 12.4 us  [project(): jnp.dot(flat_rows, weight, preferred_element_type=jnp.float32)]
  transfers between devices with their start and end apart: 8 -> 8, of which waited for: 6 -> 6; matrix products, arithmetic and copies ran while one was open for 27% -> 35% of each run, Pallas kernels for 0% -> 0%
where the time goes in v8:
time: 191 us; the launch traced here: 189 us
  waiting for transfers between devices  69.7 us (36%)
  local copies, waits for them, and re-layouts  35.9 us (19%)
  starting transfers between devices  33.4 us (17%)
  other arithmetic  27.1 us (14%)
  matrix products  21.3 us (11%)
    all_to_all x2, waiting for transfers between devices, body(): arrived = lax.all_to_all(sent, 'seq', 0, 0, tiled=True)  38.7 us
    all_to_all x1, waiting for transfers between devices, body(): query_got = lax.all_to_all(query_sent, 'seq', 0, 0, tiled=True)  15.2 us
    dot_general x3, local copies, waits for them, and re-layouts, project(): jnp.dot(flat_rows, weight, preferred_element_type=jnp.float32)  12.4 us
    all_to_all x1, starting transfers between devices, body(): query_got = lax.all_to_all(query_sent, 'seq', 0, 0, tiled=True)  10.9 us
    all_to_all x2, starting transfers between devices, body(): arrived = lax.all_to_all(sent, 'seq', 0, 0, tiled=True)  8.4 us
    all_to_all x2, starting transfers between devices, body(): lax.all_to_all(partial_out.astype(jnp.bfloat16), 'tensor', 0, 0, tiled=True)  8.3 us
    all_to_all x2, waiting for transfers between devices, body(): lax.all_to_all(partial_out.astype(jnp.bfloat16), 'tensor', 0, 0, tiled=True)  8.29 us
    all_to_all x1, waiting for transfers between devices, body(): lax.all_to_all(token_copies, 'tensor', 0, 0, tiled=True)  7.49 us
  transfers between devices with their start and end apart: 8, of which 6 were waited for; matrix products, arithmetic and copies ran while one was open for 35% of the time, Pallas kernels for 0%

profile of v8, /device:TPU:32, one launch (start us, length us, event | category | flops | bytes accessed | tf_op | source)
XLA Modules:
  0.0 189.2 jit_solution(1824309961745879376)
XLA Ops:
  0.7 1.1 constant_dynamic-slice_fusion.7
  1.8 1.8 constant_dynamic-slice_fusion.1
  3.5 0.8 pad_maximum_fusion.2
  4.4 1.1 broadcast_in_dim.146
  5.5 5.4 %all-to-all-start = ((bf16[8,4,32,512]{3,2,1,0:T(8,128)(2,1)}), bf16[8,4,32,512]{3,2,1,0:T(8,128)(2,1)S(1)}, u32[]{:S(2)}, u32[]{:S(2)}) async-start(bf16[8,4,32,512]{3,2,1,0:T(8,128)(2,1)} %broadcast_in_dim.146), calls=%async_computation | async-start | bytes 2097152 | tf_op jit(solution)/shard_map/all_to_all | solution.py:35
  10.9 4.1 %copy.102 = bf16[256,4096]{1,0:T(8,128)(2,1)} copy(bf16[256,4096]{0,1:T(8,128)(2,1)} %bitcast.200) | data formatting | bytes 4194304 | tf_op jit(solution)/shard_map/dot_general | solution.py:47
  15.1 4.1 %copy.103 = bf16[256,4096]{1,0:T(8,128)(2,1)} copy(bf16[256,4096]{0,1:T(8,128)(2,1)} %bitcast.201) | data formatting | bytes 4194304 | tf_op jit(solution)/shard_map/dot_general | solution.py:47
  19.8 7.5 %all-to-all-done = bf16[8,4,32,512]{3,2,1,0:T(8,128)(2,1)S(1)} async-done(((bf16[8,4,32,512]{3,2,1,0:T(8,128)(2,1)}), bf16[8,4,32,512]{3,2,1,0:T(8,128)(2,1)S(1)}, u32[]{:S(2)}, u32[]{:S(2)}) %all-to-all-start) | async-done | bytes 1048608 | tf_op jit(solution)/shard_map/all_to_all | solution.py:35
  28.0 0.6 copy.72
  28.5 0.5 reshape.503
  29.1 2.6 %fusion.44 = f32[4,32,2,128]{3,1,2,0:T(8,128)S(1)} fusion(bf16[2,128,4096,1]{2,1,0,3:T(8,128)(2,1)} %bitcast.205, bf16[4,32,4096,1]{2,1,0,3:T(8,128)(2,1)S(1)} %reshape.503), kind=kOutput, calls=%fused_computation.59 | convolution fusion | flops 268435456 | bytes 3276800 | tf_op jit(solution)/shard_map/dot_general | solution.py:47
  31.8 0.8 fusion.42
  33.0 1.2 tile.11
  34.2 10.9 %all-to-all-start.1 = ((bf16[32,128,128]{2,1,0:T(8,128)(2,1)}), bf16[32,128,128]{2,1,0:T(8,128)(2,1)S(1)}, u32[]{:S(2)}, u32[]{:S(2)}) async-start(bf16[32,128,128]{2,1,0:T(8,128)(2,1)} %bitcast.9), calls=%async_computation.1 | async-start | bytes 2097152 | tf_op jit(solution)/shard_map/all_to_all | solution.py:102
  45.1 4.1 %copy.104 = bf16[256,4096]{1,0:T(8,128)(2,1)} copy(bf16[256,4096]{0,1:T(8,128)(2,1)} %bitcast.202) | data formatting | bytes 4194304 | tf_op jit(solution)/shard_map/dot_general | solution.py:47
  49.3 0.6 fusion.204
  49.9 0.7 broadcast_compare_fusion.6
  50.6 0.6 fusion.203
  51.3 2.5 %broadcast_compare_fusion.1 = (pred[512]{0:T(512)(128)(4,1)S(1)}, pred[512]{0:T(512)(128)(4,1)S(1)}, pred[512]{0:T(512)(128)(4,1)S(1)}, pred[512]{0:T(512)(128)(4,1)S(1)}) fusion(s32[]{:T(128)} %bitcast.48, s32[256]{0:T(256)S(1)} %iota_add_fusion, s32[256]{0:T(256)S(1)} %iota_add_fusion.1, s32[]{:T(128)} %bitcast.26, s32[]{:T(128)} %bitcast.59, s32[]{:T(128)} %bitcast), kind=kLoop, calls=%fused_computation.227 | loop fusion | flops 2560 | bytes 4112 | tf_op jit(solution)/shard_map/lt | solution.py:110
  53.8 1.8 broadcast_compare_fusion.7
  55.6 2.4 %fusion.37 = bf16[4,2,4,8,128]{4,3,2,1,0:T(8,128)(2,1)S(1)} fusion(bf16[2,128,4096,1]{2,1,0,3:T(8,128)(2,1)} %bitcast.203, bf16[4,32,4096,1]{2,1,0,3:T(8,128)(2,1)S(1)} %reshape.503), kind=kOutput, calls=%fused_computation.50 | convolution fusion | flops 268468224 | bytes 3211264 | tf_op jit(solution)/shard_map/dot_general | solution.py:47
  58.6 1.8 fusion.195
  60.4 15.2 %all-to-all-done.1 = bf16[32,128,128]{2,1,0:T(8,128)(2,1)S(1)} async-done(((bf16[32,128,128]{2,1,0:T(8,128)(2,1)}), bf16[32,128,128]{2,1,0:T(8,128)(2,1)S(1)}, u32[]{:S(2)}, u32[]{:S(2)}) %all-to-all-start.1) | async-done | bytes 1048608 | tf_op jit(solution)/shard_map/all_to_all | solution.py:102
  76.1 1.8 fusion.9
  77.9 0.5 fusion.10
  78.6 0.5 fusion.8
  79.3 0.5 fusion.7
  80.5 1.1 fusion.13
  81.6 0.9 convolution_add_fusion.2
  82.5 1.7 convolution_add_fusion.3
  84.2 0.9 fusion.70
  86.3 2.2 %pad_maximum_fusion = f32[32,66,128]{2,1,0:T(8,128)} fusion(f32[32,1,128]{2,1,0:T(1,128)S(1)} %bitcast.244, f32[32,32,128]{2,1,0:T(8,128)S(1)} %bitcast.218, f32[32,1,128]{2,1,0:T(1,128)S(1)} %bitcast.243, f32[32,32,128]{2,1,0:T(8,128)} %bitcast.219), kind=kLoop, calls=%fused_computation.39 | loop fusion | flops 811008 | bytes 2162688 | tf_op jit(solution)/shard_map/concatenate | solution.py:149
  88.5 3.7 %all-to-all-start.2 = ((f32[32,66,128]{2,1,0:T(8,128)}), f32[32,66,128]{2,1,0:T(8,128)S(1)}, u32[]{:S(2)}, u32[]{:S(2)}) async-start(f32[32,66,128]{2,1,0:T(8,128)} %pad_maximum_fusion), calls=%async_computation.2 | async-start | bytes 2359296 | tf_op jit(solution)/shard_map/all_to_all | solution.py:150
  92.2 0.7 broadcast_compare_fusion.4
  92.9 3.3 %fusion.17 = (f32[1024]{0:T(1024)S(1)}, f32[1024]{0:T(1024)}) fusion(f32[1024,512]{0,1:T(8,128)} %get-tuple-element.77, f32[1024]{0:T(1024)S(1)} %max.60, pred[512]{0:T(512)(128)(4,1)S(1)} %copy-done.26, f32[1024]{0:T(1024)S(1)} %max.62, f32[1024,512]{0,1:T(8,128)S(1)} %get-tuple-element.65, pred[512]{0:T(512)(128)(4,1)S(1)} %copy-done.23), kind=kLoop, calls=%fused_computation.27 | loop fusion | flops 5240832 | bytes 4211712 | tf_op jit(solution)/shard_map/reduce_sum | solution.py:129
  96.2 1.0 copy.90
  97.2 1.9 %reshape.496 = f32[32,1,64]{2,0,1:T(8,128)} reshape(f32[1024,2]{1,0:T(8,128)} %copy.90) | data formatting | bytes 16384 | tf_op jit(solution)/shard_map/reshape | solution.py:139
  99.1 1.3 pad.15
  100.5 0.7 add.213
  101.2 1.0 copy.91
  102.2 1.9 %reshape.499 = f32[32,1,64]{2,0,1:T(8,128)} reshape(f32[1024,2]{1,0:T(8,128)} %copy.91) | data formatting | bytes 16384 | tf_op jit(solution)/shard_map/reshape | solution.py:139
  104.1 0.7 pad.16
  104.9 1.3 fusion.80
  106.2 1.1 fusion.78
  107.3 2.5 %convolution_add_fusion.1 = f32[1024,128]{1,0:T(8,128)S(1)} fusion(f32[1024,128]{1,0:T(8,128)S(1)} %fusion.80, f32[1024,512]{0,1:T(8,128)} %get-tuple-element.77, f32[1024]{0:T(1024)S(1)} %max.60, pred[512]{0:T(512)(128)(4,1)S(1)} %copy-done.27, bf16[4,256,128]{2,1,0:T(8,128)(2,1)} %get-tuple-element.13, bf16[4,256,128]{2,1,0:T(8,128)(2,1)} %get-tuple-element.15), kind=kOutput, calls=%fused_computation.34 | convolution fusion | flops 137232384 | bytes 3674624 | tf_op jit(solution)/shard_map/dot_general | solution.py:130
  109.8 0.8 convolution_add_fusion
  110.7 1.1 pad_maximum_fusion.1
  111.8 13.4 %all-to-all-done.2 = f32[32,66,128]{2,1,0:T(8,128)S(1)} async-done(((f32[32,66,128]{2,1,0:T(8,128)}), f32[32,66,128]{2,1,0:T(8,128)S(1)}, u32[]{:S(2)}, u32[]{:S(2)}) %all-to-all-start.2) | async-done | bytes 1081376 | tf_op jit(solution)/shard_map/all_to_all | solution.py:150
  125.2 4.7 %all-to-all-start.4 = ((f32[32,66,128]{2,1,0:T(8,128)}), f32[32,66,128]{2,1,0:T(8,128)}, u32[]{:S(2)}, u32[]{:S(2)}) async-start(f32[32,66,128]{2,1,0:T(8,128)} %pad_maximum_fusion.1), calls=%async_computation.4 | async-start | bytes 2359296 | tf_op jit(solution)/shard_map/all_to_all | solution.py:150
  130.2 1.0 copy-done.1
  132.6 2.9 %fusion.40 = f32[2,2,32,128]{3,0,2,1:T(2,128)S(1)} fusion(f32[16,2,2,33,128]{4,1,0,3,2:T(2,128)} %bitcast.197, f32[16,2,2,32]{1,0,3,2:T(8,128)S(1)} %copy.85), kind=kLoop, calls=%fused_computation.55 | loop fusion | flops 507904 | bytes 1122304 | tf_op jit(solution)/shard_map/reduce_sum | solution.py:159
  135.8 1.3 fusion.30
  137.1 25.3 %all-to-all-done.4 = f32[32,66,128]{2,1,0:T(8,128)} async-done(((f32[32,66,128]{2,1,0:T(8,128)}), f32[32,66,128]{2,1,0:T(8,128)}, u32[]{:S(2)}, u32[]{:S(2)}) %all-to-all-start.4) | async-done | bytes 1081376 | tf_op jit(solution)/shard_map/all_to_all | solution.py:150
  162.4 4.2 %all-to-all-start.3 = ((bf16[8,64,512]{2,1,0:T(8,128)(2,1)}), bf16[8,64,512]{2,1,0:T(8,128)(2,1)}, u32[]{:S(2)}, u32[]{:S(2)}) async-start(bf16[8,64,512]{2,1,0:T(8,128)(2,1)} %fusion.30), calls=%async_computation.3 | async-start | bytes 1048576 | tf_op jit(solution)/shard_map/all_to_all | solution.py:180
  166.6 1.5 copy.94
  169.0 1.3 copy.96
  170.3 2.2 %fusion.39 = f32[2,2,32,128]{3,0,2,1:T(2,128)S(1)} fusion(f32[16,2,2,33,128]{4,1,0,3,2:T(2,128)S(1)} %bitcast.199, f32[16,2,2,32]{1,0,3,2:T(8,128)} %copy.96), kind=kLoop, calls=%fused_computation.53 | loop fusion | flops 507904 | bytes 1122304 | tf_op jit(solution)/shard_map/reduce_sum | solution.py:159
  172.9 1.3 fusion.27
  174.1 1.5 all-to-all-done.3
  175.6 4.1 %all-to-all-start.5 = ((bf16[8,64,512]{2,1,0:T(8,128)(2,1)}), bf16[8,64,512]{2,1,0:T(8,128)(2,1)S(1)}, u32[]{:S(2)}, u32[]{:S(2)}) async-start(bf16[8,64,512]{2,1,0:T(8,128)(2,1)} %fusion.27), calls=%async_computation.5 | async-start | bytes 1048576 | tf_op jit(solution)/shard_map/all_to_all | solution.py:180
  179.8 0.7 broadcast_select_fusion
  180.5 1.1 reduce_sum.153
  181.6 6.8 %all-to-all-done.5 = bf16[8,64,512]{2,1,0:T(8,128)(2,1)S(1)} async-done(((bf16[8,64,512]{2,1,0:T(8,128)(2,1)}), bf16[8,64,512]{2,1,0:T(8,128)(2,1)S(1)}, u32[]{:S(2)}, u32[]{:S(2)}) %all-to-all-start.5) | async-done | bytes 524320 | tf_op jit(solution)/shard_map/all_to_all | solution.py:180
  188.5 0.7 pad_maximum_fusion.5
  (145 shorter events, 8.1 us)
Async XLA Ops:
  0.6 3.7 %copy-start.16 = (bf16[4,32,512]{2,1,0:T(8,128)(2,1)S(1)}, bf16[4,32,512]{2,1,0:T(8,128)(2,1)}, u32[]{:S(2)}) copy-start(bf16[4,32,512]{2,1,0:T(8,128)(2,1)} %param.10) | copy-start | bytes 393220
  3.5 7.4 %copy-start.19 = (bf16[4096]{0:T(1024)(128)(2,1)S(1)}, bf16[4096]{0:T(1024)(128)(2,1)}, u32[]{:S(2)}) copy-start(bf16[4096]{0:T(1024)(128)(2,1)} %param.11) | copy-start | bytes 24580
  4.4 54.2 %collective-permute-start = (bf16[4,512,128]{2,1,0:T(8,128)(2,1)}, bf16[4,512,128]{2,1,0:T(8,128)(2,1)}, u32[]{:S(2)}, u32[]{:S(2)}) collective-permute-start(bf16[4,512,128]{2,1,0:T(8,128)(2,1)} %pad_maximum_fusion.2), channel_id=1, source_target_pairs={{0,8},{8,0},{16,24},{24,16},{32,40},{40,32},{48,56},{56,48},{64,72... | collective-permute-start | bytes 1572872 | tf_op jit(solution)/shard_map/ppermute | solution.py:81
  5.5 21.8 %all-to-all-start = ((bf16[8,4,32,512]{3,2,1,0:T(8,128)(2,1)}), bf16[8,4,32,512]{3,2,1,0:T(8,128)(2,1)S(1)}, u32[]{:S(2)}, u32[]{:S(2)}) async-start(bf16[8,4,32,512]{3,2,1,0:T(8,128)(2,1)} %broadcast_in_dim.146), calls=%async_computation | async-start | bytes 2097152 | tf_op jit(solution)/shard_map/all_to_all | solution.py:35
  10.9 39.0 %copy-start.31 = (s32[32]{0:T(128)}, s32[32]{0:T(128)S(1)}, u32[]{:S(2)}) copy-start(s32[32]{0:T(128)S(1)} %iota_add_fusion.3) | copy-start | bytes 388
  15.1 4.1 %copy-start.20 = (s32[4]{0:T(128)S(1)}, s32[4]{0:T(128)}, u32[]{:S(2)}) copy-start(s32[4]{0:T(128)} %param.18) | copy-start | bytes 52
  29.1 2.7 %copy-start.2 = (bf16[256,4096]{1,0:T(8,128)(2,1)S(1)}, bf16[256,4096]{1,0:T(8,128)(2,1)}, u32[]{:S(2)}) copy-start(bf16[256,4096]{1,0:T(8,128)(2,1)} %copy.103) | copy-start | bytes 6291460
  32.9 22.7 %copy-start.8 = (bf16[4,2,4,8,128]{4,3,2,1,0:T(8,128)(2,1)}, bf16[4,2,4,8,128]{4,3,2,1,0:T(8,128)(2,1)S(1)}, u32[]{:S(2)}) copy-start(bf16[4,2,4,8,128]{4,3,2,1,0:T(8,128)(2,1)S(1)} %get-tuple-element.25) | copy-start | bytes 196612
  34.2 41.4 %all-to-all-start.1 = ((bf16[32,128,128]{2,1,0:T(8,128)(2,1)}), bf16[32,128,128]{2,1,0:T(8,128)(2,1)S(1)}, u32[]{:S(2)}, u32[]{:S(2)}) async-start(bf16[32,128,128]{2,1,0:T(8,128)(2,1)} %bitcast.9), calls=%async_computation.1 | async-start | bytes 2097152 | tf_op jit(solution)/shard_map/all_to_all | solution.py:102
  45.1 4.1 %copy-start.21 = (s32[4]{0:T(128)S(1)}, s32[4]{0:T(128)}, u32[]{:S(2)}) copy-start(s32[4]{0:T(128)} %param.19) | copy-start | bytes 52
  50.6 33.6 %copy-start.18 = (s32[64]{0:T(128)}, s32[64]{0:T(128)S(1)}, u32[]{:S(2)}) copy-start(s32[64]{0:T(128)S(1)} %get-tuple-element.8) | copy-start | bytes 772
  50.6 33.6 %copy-start.29 = (pred[64]{0:T(512)(128)(4,1)}, pred[64]{0:T(512)(128)(4,1)S(1)}, u32[]{:S(2)}) copy-start(pred[64]{0:T(512)(128)(4,1)S(1)} %get-tuple-element.7) | copy-start | bytes 196
  53.8 22.3 %copy-start.25 = (pred[512]{0:T(512)(128)(4,1)}, pred[512]{0:T(512)(128)(4,1)S(1)}, u32[]{:S(2)}) copy-start(pred[512]{0:T(512)(128)(4,1)S(1)} %get-tuple-element.45) | copy-start | bytes 1540
  53.8 24.1 %copy-start.22 = (pred[512]{0:T(512)(128)(4,1)}, pred[512]{0:T(512)(128)(4,1)S(1)}, u32[]{:S(2)}) copy-start(pred[512]{0:T(512)(128)(4,1)S(1)} %get-tuple-element.47) | copy-start | bytes 1540
  55.6 28.6 %copy-start.30 = (pred[64]{0:T(512)(128)(4,1)}, pred[64]{0:T(512)(128)(4,1)S(1)}, u32[]{:S(2)}) copy-start(pred[64]{0:T(512)(128)(4,1)S(1)} %get-tuple-element.58) | copy-start | bytes 196
  58.1 2.3 %copy-start.12 = (bf16[4,2,4,8,128]{4,3,2,1,0:T(8,128)(2,1)}, bf16[4,2,4,8,128]{4,3,2,1,0:T(8,128)(2,1)S(1)}, u32[]{:S(2)}) copy-start(bf16[4,2,4,8,128]{4,3,2,1,0:T(8,128)(2,1)S(1)} %fusion.37) | copy-start | bytes 196612
  58.1 22.0 %copy-start.6 = (bf16[4,32,128]{2,1,0:T(8,128)(2,1)}, bf16[4,32,128]{2,1,0:T(8,128)(2,1)S(1)}, u32[]{:S(2)}) copy-start(bf16[4,32,128]{2,1,0:T(8,128)(2,1)S(1)} %get-tuple-element.31) | copy-start | bytes 98308
  58.2 2.2 %collective-permute-start.1 = (bf16[4,64,128]{2,1,0:T(8,128)(2,1)S(1)}, bf16[4,64,128]{2,1,0:T(8,128)(2,1)S(1)}, u32[]{:S(2)}, u32[]{:S(2)}) collective-permute-start(bf16[4,64,128]{2,1,0:T(8,128)(2,1)S(1)} %pad_maximum_fusion.8), channel_id=1, source_target_pairs={{0,8},{8,0},{16,24},{24,16},{32,40},{40,32},{48,56},{56,48},{64,72... | collective-permute-start | bytes 196616 | tf_op jit(solution)/shard_map/ppermute | solution.py:84
  60.3 19.8 %copy-start.7 = (bf16[4,32,128]{2,1,0:T(8,128)(2,1)}, bf16[4,32,128]{2,1,0:T(8,128)(2,1)S(1)}, u32[]{:S(2)}) copy-start(bf16[4,32,128]{2,1,0:T(8,128)(2,1)S(1)} %get-tuple-element.33) | copy-start | bytes 98308
  75.9 8.3 %copy-start.3 = (f32[1024,64]{0,1:T(8,128)}, f32[1024,64]{0,1:T(8,128)S(1)}, u32[]{:S(2)}) copy-start(f32[1024,64]{0,1:T(8,128)S(1)} %get-tuple-element.67) | copy-start | bytes 786436
  76.1 8.1 %copy-start.5 = (f32[1024,64]{0,1:T(8,128)}, f32[1024,64]{0,1:T(8,128)S(1)}, u32[]{:S(2)}) copy-start(f32[1024,64]{0,1:T(8,128)S(1)} %get-tuple-element.79) | copy-start | bytes 786436
  80.5 1.1 copy-start.10
  80.5 1.1 copy-start.14
  86.3 6.0 %copy-start.32 = (s32[32]{0:T(128)S(1)}, s32[32]{0:T(128)}, u32[]{:S(2)}) copy-start(s32[32]{0:T(128)} %copy-done.31) | copy-start | bytes 388
  86.3 6.6 %copy-start.23 = (pred[512]{0:T(512)(128)(4,1)S(1)}, pred[512]{0:T(512)(128)(4,1)}, u32[]{:S(2)}) copy-start(pred[512]{0:T(512)(128)(4,1)} %copy-done.22) | copy-start | bytes 1540
  86.3 6.6 %copy-start.26 = (pred[512]{0:T(512)(128)(4,1)S(1)}, pred[512]{0:T(512)(128)(4,1)}, u32[]{:S(2)}) copy-start(pred[512]{0:T(512)(128)(4,1)} %copy-done.25) | copy-start | bytes 1540
  88.5 36.7 %all-to-all-start.2 = ((f32[32,66,128]{2,1,0:T(8,128)}), f32[32,66,128]{2,1,0:T(8,128)S(1)}, u32[]{:S(2)}, u32[]{:S(2)}) async-start(f32[32,66,128]{2,1,0:T(8,128)} %pad_maximum_fusion), calls=%async_computation.2 | async-start | bytes 2359296 | tf_op jit(solution)/shard_map/all_to_all | solution.py:150
  96.2 10.0 %copy-start.4 = (f32[1024,64]{0,1:T(8,128)S(1)}, f32[1024,64]{0,1:T(8,128)}, u32[]{:S(2)}) copy-start(f32[1024,64]{0,1:T(8,128)} %copy-done.3) | copy-start | bytes 786436
  102.2 5.0 %copy-start.27 = (pred[512]{0:T(512)(128)(4,1)S(1)}, pred[512]{0:T(512)(128)(4,1)}, u32[]{:S(2)}) copy-start(pred[512]{0:T(512)(128)(4,1)} %copy-done.25) | copy-start | bytes 1540
  107.2 2.5 %copy-start.11 = (bf16[4,256,128]{2,1,0:T(8,128)(2,1)S(1)}, bf16[4,256,128]{2,1,0:T(8,128)(2,1)}, u32[]{:S(2)}) copy-start(bf16[4,256,128]{2,1,0:T(8,128)(2,1)} %get-tuple-element.13) | copy-start | bytes 786436
  107.2 2.5 %copy-start.15 = (bf16[4,256,128]{2,1,0:T(8,128)(2,1)S(1)}, bf16[4,256,128]{2,1,0:T(8,128)(2,1)}, u32[]{:S(2)}) copy-start(bf16[4,256,128]{2,1,0:T(8,128)(2,1)} %get-tuple-element.15) | copy-start | bytes 786436
  107.3 2.5 %copy-start.24 = (pred[512]{0:T(512)(128)(4,1)S(1)}, pred[512]{0:T(512)(128)(4,1)}, u32[]{:S(2)}) copy-start(pred[512]{0:T(512)(128)(4,1)} %copy-done.22) | copy-start | bytes 1540
  109.8 0.9 copy-start.17
  110.6 19.3 %copy-start.28 = (pred[4,32]{1,0:T(4,128)(4,1)S(1)}, pred[4,32]{1,0:T(4,128)(4,1)}, u32[]{:S(2)}) copy-start(pred[4,32]{1,0:T(4,128)(4,1)} %broadcast_compare_fusion.4) | copy-start | bytes 388
  125.2 37.2 %all-to-all-start.4 = ((f32[32,66,128]{2,1,0:T(8,128)}), f32[32,66,128]{2,1,0:T(8,128)}, u32[]{:S(2)}, u32[]{:S(2)}) async-start(f32[32,66,128]{2,1,0:T(8,128)} %pad_maximum_fusion.1), calls=%async_computation.4 | async-start | bytes 2359296 | tf_op jit(solution)/shard_map/all_to_all | solution.py:150
  130.2 1.0 copy-start.1
  130.2 5.6 %copy-start = (bf16[256,4096]{1,0:T(8,128)(2,1)S(1)}, bf16[256,4096]{1,0:T(8,128)(2,1)}, u32[]{:S(2)}) copy-start(bf16[256,4096]{1,0:T(8,128)(2,1)} %param.15) | copy-start | bytes 6291460
  162.4 13.2 %all-to-all-start.3 = ((bf16[8,64,512]{2,1,0:T(8,128)(2,1)}), bf16[8,64,512]{2,1,0:T(8,128)(2,1)}, u32[]{:S(2)}, u32[]{:S(2)}) async-start(bf16[8,64,512]{2,1,0:T(8,128)(2,1)} %fusion.30), calls=%async_computation.3 | async-start | bytes 1048576 | tf_op jit(solution)/shard_map/all_to_all | solution.py:180
  172.5 7.2 %copy-start.9 = (bf16[4,2,4,8,128]{4,3,2,1,0:T(8,128)(2,1)S(1)}, bf16[4,2,4,8,128]{4,3,2,1,0:T(8,128)(2,1)}, u32[]{:S(2)}) copy-start(bf16[4,2,4,8,128]{4,3,2,1,0:T(8,128)(2,1)} %copy-done.8) | copy-start | bytes 196612
  172.5 7.2 %copy-start.13 = (bf16[4,2,4,8,128]{4,3,2,1,0:T(8,128)(2,1)S(1)}, bf16[4,2,4,8,128]{4,3,2,1,0:T(8,128)(2,1)}, u32[]{:S(2)}) copy-start(bf16[4,2,4,8,128]{4,3,2,1,0:T(8,128)(2,1)} %copy-done.12) | copy-start | bytes 196612
  175.6 12.9 %all-to-all-start.5 = ((bf16[8,64,512]{2,1,0:T(8,128)(2,1)}), bf16[8,64,512]{2,1,0:T(8,128)(2,1)S(1)}, u32[]{:S(2)}, u32[]{:S(2)}) async-start(bf16[8,64,512]{2,1,0:T(8,128)(2,1)} %fusion.27), calls=%async_computation.5 | async-start | bytes 1048576 | tf_op jit(solution)/shard_map/all_to_all | solution.py:180
